TPU v7x, 256 devices: a whole 4x4x8 slice. The times are simulated.
256 devices in a mesh: row: 32 (over z, y), col: 8 (over x, core).
Axes of the slice: x: 4, y: 4, z: 8, core: 2. Of those that a mesh axis runs over, the one named last changes fastest.
Arguments:
- amps: bfloat16 [30720, 30720], P(('col', 'row')), may hold values from -6 to 6
- cycle_int: bfloat16 [30720, 1024], P('col'), may hold values from -0.03125 to 0.03125
- tile_mask: int32 [480, 16], P('col'), may hold values 0 or 1
- coulomb: bfloat16 [30720, 1024], P('row', 'col'), may hold values from -6 to 6
- occ_irrep: int32 [240], replicated, may hold values from 0 to 7
- vir_irrep: int32 [192], replicated, may hold values from 0 to 7
- occ_energy: float32 [240], replicated, may hold values from -1.5 to -0.3
- vir_energy: float32 [192], replicated, may hold values from 0.3 to 2
Outputs:
- new_amps: bfloat16 [30720, 1024], P('row', 'col')
All inputs are finite; a program needn't handle non-finite values. No bound on the sum of `tile_mask` on one device may be relied on, other than what follows from the above.
Results may differ from a plain program's by a relative error of at most 0.001.
Values may be sent and summed in bfloat16 or wider, within the bound.
No kernel may reach another device: no remote copies, remote signals or barrier semaphores. Data moves between devices by JAX's collectives and lax.ppermute only.
A program may use at most 128 MiB of HBM per device.

v0:
```python
import jax
import jax.numpy as jnp
from jax import lax
from jax.sharding import PartitionSpec as P

BLK = 64


def lookup(positions, values_table):
    entries = jnp.arange(values_table.shape[0], dtype=jnp.int32)
    picked = jnp.where(
        positions[:, None] == entries[None, :],
        values_table[None, :],
        jnp.zeros((), values_table.dtype),
    )
    return jnp.sum(picked, axis=1)


def local(amps, cycle_int, tile_mask, coulomb, occ_irrep, vir_irrep, occ_energy, vir_energy):
    block_size = BLK
    occupied = occ_energy.shape[0]
    row_blocks = vir_energy.shape[0] // block_size - 1
    kc_rows, jb_all = cycle_int.shape
    rows_here, cols_here = coulomb.shape
    tiled_int = cycle_int.reshape(
        kc_rows // block_size, block_size, jb_all // block_size, block_size
    )
    tile_keep = tile_mask.astype(jnp.bfloat16)[:, None, :, None]
    masked = (tiled_int * tile_keep).reshape(kc_rows, jb_all)
    sorted_amps = lax.all_to_all(amps, "row", split_axis=1, concat_axis=0, tiled=True)
    partial_value = lax.dot_general(
        sorted_amps, masked, (((0,), (0,)), ((), ())), preferred_element_type=jnp.float32
    )
    cycle_sum = lax.psum_scatter(partial_value, "col", scatter_dimension=1, tiled=True)
    row_pos = lax.axis_index("row") * rows_here + jnp.arange(rows_here, dtype=jnp.int32)
    col_pos = lax.axis_index("col") * cols_here + jnp.arange(cols_here, dtype=jnp.int32)
    occ_row = row_pos // block_size % occupied
    vir_row = block_size * (row_pos // (occupied * block_size)) + row_pos % block_size
    occ_col = col_pos // block_size % occupied
    vir_col = col_pos % block_size + row_blocks * block_size
    sym_row = jnp.bitwise_xor(lookup(occ_row, occ_irrep), lookup(vir_row, vir_irrep))
    sym_col = jnp.bitwise_xor(lookup(occ_col, occ_irrep), lookup(vir_col, vir_irrep))
    allowed = sym_row[:, None] == sym_col[None, :]
    gap_row = lookup(vir_row, vir_energy) - lookup(occ_row, occ_energy)
    gap_col = lookup(vir_col, vir_energy) - lookup(occ_col, occ_energy)
    denominator = gap_row[:, None] + gap_col[None, :]
    updated = (coulomb.astype(jnp.float32) + cycle_sum) / denominator
    return jnp.where(allowed, updated, jnp.float32(0.0)).astype(jnp.bfloat16)


def solution(mesh):
    return jax.shard_map(
        local,
        mesh=mesh,
        in_specs=(
            P(("col", "row"), None),
            P("col", None),
            P("col", None),
            P("row", "col"),
            P(),
            P(),
            P(),
            P(),
        ),
        out_specs=P("row", "col"),
        check_vma=False,
    )
```

profile of v0, /device:TPU:7, one launch (start us, length us, event | category | flops | bytes accessed | tf_op | source)
XLA Modules:
  0.0 296.2 jit_solution(12997518924684539961)
XLA Ops:
  6.5 10.3 %copy.16 = bf16[120,30720]{0,1:T(8,128)(2,1)} copy(bf16[120,30720]{1,0:T(8,128)(2,1)} %param.8) | data formatting | bytes 14745600 | tf_op args[0]
  16.8 0.0 copy-start.1
  16.8 11.4 %all-to-all-start = ((bf16[120,32,960]{0,2,1:T(8,128)(2,1)}), bf16[120,32,960]{0,2,1:T(8,128)(2,1)}, u32[]{:S(2)}, u32[]{:S(2)}) async-start(bf16[120,32,960]{0,2,1:T(8,128)(2,1)} %bitcast.9), calls=%async_computation | async-start | bytes 15728640 | tf_op jit(solution)/shard_map/all_to_all | solution.py:30
  28.3 0.0 reduce-scatter.2.cloned.1.call-start
  28.3 0.0 copy-done.1
  28.3 0.1 copy.15
  28.5 5.9 %mul.28 = bf16[60,64,16,64]{3,2,1,0:T(8,128)(2,1)} broadcast(bf16[60,16]{1,0:T(8,128)(2,1)S(1)} %copy.15), dimensions={0,2} | broadcast | bytes 7866240 | tf_op jit(solution)/shard_map/mul | solution.py:29
  34.4 21.2 %mul.29 = bf16[3840,1024]{1,0:T(8,128)(2,1)} reshape(bf16[60,64,16,64]{3,2,1,0:T(8,128)(2,1)} %mul.28) | data formatting | bytes 15728640 | tf_op jit(solution)/shard_map/mul | solution.py:29
  55.6 148.6 %all-to-all-done = bf16[120,32,960]{0,2,1:T(8,128)(2,1)} async-done(((bf16[120,32,960]{0,2,1:T(8,128)(2,1)}), bf16[120,32,960]{0,2,1:T(8,128)(2,1)}, u32[]{:S(2)}, u32[]{:S(2)}) %all-to-all-start) | async-done | bytes 7372832 | tf_op jit(solution)/shard_map/all_to_all | solution.py:30
  204.2 11.4 %copy.17 = bf16[32,120,960]{1,0,2:T(8,128)(2,1)} copy(bf16[32,120,960]{1,2,0:T(8,128)(2,1)} %bitcast.1) | data formatting | bytes 14745600 | tf_op jit(solution)/shard_map/all_to_all | solution.py:30
  215.6 15.7 %all_to_all.17 = bf16[3840,960]{0,1:T(8,128)(2,1)} reshape(bf16[32,120,960]{1,0,2:T(8,128)(2,1)} %copy.17) | data formatting | bytes 14745600 | tf_op jit(solution)/shard_map/all_to_all | solution.py:30
  231.2 0.0 copy-start.2
  231.2 0.0 copy-start.3
  231.2 0.0 copy-start.4
  231.2 0.0 copy-start.5
  231.2 0.0 copy-start
  231.2 14.8 %fusion.2 = f32[960,1024]{1,0:T(8,128)} fusion(bf16[3840,960]{0,1:T(8,128)(2,1)} %all_to_all.17, bf16[3840,1024]{1,0:T(8,128)(2,1)} %param.9, bf16[3840,1024]{1,0:T(8,128)(2,1)} %mul.29), kind=kOutput, calls=%fused_computation.2 | convolution fusion | flops 7553679360 | bytes 27033600 | tf_op jit(solution)/shard_map/dot_general | solution.py:31
  246.0 0.0 reduce-scatter.2.cloned.1.call-update
  246.1 0.0 copy-done.2
  246.1 0.2 select_reduce_fusion.2
  246.3 0.0 copy-done.3
  246.3 0.4 select_reduce_fusion
  246.7 0.0 copy-done.4
  246.7 0.2 select_reduce_fusion.3
  246.9 0.0 copy-done.5
  246.9 0.4 select_reduce_fusion.1
  247.3 0.1 select_reduce_fusion.6
  247.4 0.1 select_reduce_fusion.4
  247.5 0.1 select_reduce_fusion.7
  247.6 0.1 select_reduce_fusion.5
  247.7 39.6 %reduce-scatter.2.cloned.1.call-done = f32[960,128]{1,0:T(8,128)} async-done(((f32[960,1024]{1,0:T(8,128)}), f32[960,128]{1,0:T(8,128)}) %reduce-scatter.2.cloned.1.call-update) | async-done | bytes 491536 | tf_op jit(solution)/shard_map/reduce_scatter | solution.py:34
  287.3 0.0 copy-done
  287.3 2.0 select_convert_fusion
  (7 shorter events, 0.1 us)
Async XLA Ops:
  16.8 11.5 %copy-start.1 = (s32[60,16]{0,1:T(8,128)S(1)}, s32[60,16]{0,1:T(8,128)}, u32[]{:S(2)}) copy-start(s32[60,16]{0,1:T(8,128)} %param.10) | copy-start | bytes 11524
  16.8 187.4 %all-to-all-start = ((bf16[120,32,960]{0,2,1:T(8,128)(2,1)}), bf16[120,32,960]{0,2,1:T(8,128)(2,1)}, u32[]{:S(2)}, u32[]{:S(2)}) async-start(bf16[120,32,960]{0,2,1:T(8,128)(2,1)} %bitcast.9), calls=%async_computation | async-start | bytes 15728640 | tf_op jit(solution)/shard_map/all_to_all | solution.py:30
  28.3 259.0 %reduce-scatter.2.cloned.1.call-start = ((), (), s32[]{:S(2)}) async-start(), calls=%async_computation.2 | async-start | bytes 4423680 | tf_op jit(solution)/shard_map/reduce_scatter | solution.py:34
  231.2 14.9 %copy-start.2 = (f32[192]{0:T(256)S(1)}, f32[192]{0:T(256)}, u32[]{:S(2)}) copy-start(f32[192]{0:T(256)} %param.15) | copy-start | bytes 2308
  231.2 15.1 %copy-start.3 = (f32[240]{0:T(256)S(1)}, f32[240]{0:T(256)}, u32[]{:S(2)}) copy-start(f32[240]{0:T(256)} %param.14) | copy-start | bytes 2884
  231.2 15.5 %copy-start.4 = (s32[192]{0:T(256)S(1)}, s32[192]{0:T(256)}, u32[]{:S(2)}) copy-start(s32[192]{0:T(256)} %param.13) | copy-start | bytes 2308
  231.2 15.6 %copy-start.5 = (s32[240]{0:T(256)S(1)}, s32[240]{0:T(256)}, u32[]{:S(2)}) copy-start(s32[240]{0:T(256)} %param.12) | copy-start | bytes 2884
  231.2 56.1 %copy-start = (bf16[960,128]{1,0:T(8,128)(2,1)S(1)}, bf16[960,128]{1,0:T(8,128)(2,1)}, u32[]{:S(2)}) copy-start(bf16[960,128]{1,0:T(8,128)(2,1)} %param.11) | copy-start | bytes 737284
Sparse Core Ops, SparseCore 0:
  246.2 41.0 reduce-scatter.1
where the time goes:
time: 299 us; the launch traced here: 296 us
  waiting for transfers between devices  188 us (63%)
  local copies, waits for them, and re-layouts  64.6 us (22%)
  matrix products  14.8 us (5%)
  between operations  13.5 us (5%)
  starting transfers between devices  11.5 us (4%)
  other arithmetic  3.61 us (1%)
    all_to_all x1, waiting for transfers between devices, local(): lax.all_to_all(amps, 'row', split_axis=1, concat_axis=0, tiled=True)  149 us
    reduce_scatter x1, waiting for transfers between devices, local(): lax.psum_scatter(partial_value, 'col', scatter_dimension=1, tiled=True)  39.6 us
    mul x2, local copies, waits for them, and re-layouts, local(): masked = (tiled_int * tile_keep).reshape(kc_rows, jb_all)  27.1 us
    all_to_all x2, local copies, waits for them, and re-layouts, local(): lax.all_to_all(amps, 'row', split_axis=1, concat_axis=0, tiled=True)  27 us
    dot_general x1, matrix products, local(): lax.dot_general(sorted_amps, masked, (((0,), (0,)), ((), ())), preferred_...  14.8 us
    all_to_all x1, starting transfers between devices, local(): lax.all_to_all(amps, 'row', split_axis=1, concat_axis=0, tiled=True)  11.4 us
    unnamed x13, local copies, waits for them, and re-layouts  10.3 us
  transfers between devices with their start and end apart: 2, of which 2 were waited for; matrix products, arithmetic and copies ran while one was open for 10% of the time, Pallas kernels for 0%

commit v1 on v0

v1 whole, which is shorter than its diff:
```python
import jax
import jax.numpy as jnp
from jax import lax
from jax.sharding import Mesh, PartitionSpec as P

BLK = 64

Z, Y, X, C = "z", "y", "x", "core"
COL = (X, C)
ROW = (Z, Y)


def lookup(positions, values_table):
    entries = jnp.arange(values_table.shape[0], dtype=jnp.int32)
    picked = jnp.where(
        positions[:, None] == entries[None, :],
        values_table[None, :],
        jnp.zeros((), values_table.dtype),
    )
    return jnp.sum(picked, axis=1)


def swap_perm(nz, nc):
    return [(z * nc + c, c * nz + z) for z in range(nz) for c in range(nc)]


def local(amps, cycle_int, tile_mask, coulomb, occ_irrep, vir_irrep, occ_energy, vir_energy):
    block_size = BLK
    occupied = occ_energy.shape[0]
    row_blocks = vir_energy.shape[0] // block_size - 1
    kc_rows, jb_all = cycle_int.shape
    rows_here, cols_here = coulomb.shape
    nz = lax.axis_size(Z)
    ny = lax.axis_size(Y)
    ncol = lax.axis_size(COL)
    z = lax.axis_index(Z)
    y = lax.axis_index(Y)
    c = lax.axis_index(COL)
    sub = amps.shape[0]
    span = sub * ny

    ci_rows = lax.dynamic_slice_in_dim(cycle_int, z * span, span, axis=0)
    mask_rows = jnp.repeat(tile_mask.astype(jnp.bfloat16), block_size, axis=0)
    mask_rows = lax.dynamic_slice_in_dim(mask_rows, z * span, span, axis=0)
    masked = (
        ci_rows.reshape(span, jb_all // block_size, block_size) * mask_rows[:, :, None]
    ).reshape(span, jb_all)
    masked_all = lax.all_gather(masked, COL, axis=0, tiled=True)

    plane_amps = lax.all_to_all(amps, (X, C, Y), split_axis=1, concat_axis=0, tiled=True)
    partial_value = lax.dot_general(
        plane_amps, masked_all, (((0,), (0,)), ((), ())), preferred_element_type=jnp.float32
    )
    cycle_sum = lax.psum_scatter(partial_value, Z, scatter_dimension=1, tiled=True)

    perm = swap_perm(nz, ncol)
    coulomb_here = lax.ppermute(coulomb, (Z, X, C), perm)
    row_block = c * ny + y
    row_pos = row_block * rows_here + jnp.arange(rows_here, dtype=jnp.int32)
    col_pos = z * cols_here + jnp.arange(cols_here, dtype=jnp.int32)
    occ_row = row_pos // block_size % occupied
    vir_row = block_size * (row_pos // (occupied * block_size)) + row_pos % block_size
    occ_col = col_pos // block_size % occupied
    vir_col = col_pos % block_size + row_blocks * block_size
    sym_row = jnp.bitwise_xor(lookup(occ_row, occ_irrep), lookup(vir_row, vir_irrep))
    sym_col = jnp.bitwise_xor(lookup(occ_col, occ_irrep), lookup(vir_col, vir_irrep))
    allowed = sym_row[:, None] == sym_col[None, :]
    gap_row = lookup(vir_row, vir_energy) - lookup(occ_row, occ_energy)
    gap_col = lookup(vir_col, vir_energy) - lookup(occ_col, occ_energy)
    denominator = gap_row[:, None] + gap_col[None, :]
    updated = (coulomb_here.astype(jnp.float32) + cycle_sum) / denominator
    out = jnp.where(allowed, updated, jnp.float32(0.0)).astype(jnp.bfloat16)
    return lax.ppermute(out, (Z, X, C), perm)


def solution(mesh):
    nrow, ncol = mesh.devices.shape
    ncore = 2
    nx = ncol // ncore
    nz = ncol
    ny = nrow // nz
    torus = Mesh(mesh.devices.reshape(nz, ny, nx, ncore), (Z, Y, X, C))
    return jax.shard_map(
        local,
        mesh=torus,
        in_specs=(
            P(COL + ROW, None),
            P(COL, None),
            P(COL, None),
            P(ROW, COL),
            P(),
            P(),
            P(),
            P(),
        ),
        out_specs=P(ROW, COL),
        check_vma=False,
    )
```

time: 299 us -> 278 us (0.930)
  blocking collectives: 0 us -> 126 us
  waiting for transfers between devices: 188 us -> 71.2 us
  local copies, waits for them, and re-layouts: 64.6 us -> 38.4 us
    all_to_all x1 -> x0, waiting for transfers between devices: 149 us -> none  [local(): lax.all_to_all(amps, 'row', split_axis=1, concat_axis=0, tiled=True)]
    all_to_all x0 -> x1, blocking collectives: none -> 126 us  [local(): lax.all_to_all(amps, (X, C, Y), split_axis=1, concat_axis=0, tiled=True)]
    ppermute x0 -> x2, waiting for transfers between devices: none -> 37.6 us  [the longest x1 19.5 us: local(): coulomb_here = lax.ppermute(coulomb, (Z, X, C), perm)]
    mul x2 -> x1, local copies, waits for them, and re-layouts: 27.1 us -> 1.36 us  [local(): ci_rows.reshape(span, jb_all // block_size, block_size)]
    all_to_all x1 -> x0, starting transfers between devices: 11.4 us -> none  [local(): lax.all_to_all(amps, 'row', split_axis=1, concat_axis=0, tiled=True)]
    ppermute x0 -> x2, starting transfers between devices: none -> 9.9 us  [the longest x1 6.88 us: local(): coulomb_here = lax.ppermute(coulomb, (Z, X, C), perm)]
    reduce_scatter x1, waiting for transfers between devices: 39.6 us -> 33.6 us  [local(): lax.psum_scatter(partial_value, Z, scatter_dimension=1, tiled=True)]
    all_to_all x2, local copies, waits for them, and re-layouts: 27 us -> 23.9 us  [local(): lax.all_to_all(amps, (X, C, Y), split_axis=1, concat_axis=0, tiled=True)]
  transfers between devices with their start and end apart: 2 -> 4, of which waited for: 2 -> 3; matrix products, arithmetic and copies ran while one was open for 10% -> 7% of each run, Pallas kernels for 0% -> 0%
where the time goes in v1:
time: 278 us; the launch traced here: 277 us
  blocking collectives  126 us (45%)
  waiting for transfers between devices  71.2 us (26%)
  local copies, waits for them, and re-layouts  38.4 us (14%)
  matrix products  13.7 us (5%)
  between operations  13.6 us (5%)
  starting transfers between devices  9.94 us (4%)
  other arithmetic  3.68 us (1%)
    all_to_all x1, blocking collectives, local(): lax.all_to_all(amps, (X, C, Y), split_axis=1, concat_axis=0, tiled=True)  126 us
    reduce_scatter x1, waiting for transfers between devices, local(): lax.psum_scatter(partial_value, Z, scatter_dimension=1, tiled=True)  33.6 us
    all_to_all x2, local copies, waits for them, and re-layouts, local(): lax.all_to_all(amps, (X, C, Y), split_axis=1, concat_axis=0, tiled=True)  23.9 us
    ppermute x1, waiting for transfers between devices, local(): coulomb_here = lax.ppermute(coulomb, (Z, X, C), perm)  19.5 us
    ppermute x1, waiting for transfers between devices, local(): return lax.ppermute(out, (Z, X, C), perm)  18 us
    dot_general x1, matrix products, local(): lax.dot_general(plane_amps, masked_all, (((0,), (0,)), ((), ())), preferr...  13.7 us
    unnamed x13, local copies, waits for them, and re-layouts  11.4 us
    ppermute x1, starting transfers between devices, local(): coulomb_here = lax.ppermute(coulomb, (Z, X, C), perm)  6.88 us
  transfers between devices with their start and end apart: 4, of which 3 were waited for; matrix products, arithmetic and copies ran while one was open for 7% of the time, Pallas kernels for 0%

profile of v1, /device:TPU:7, one launch (start us, length us, event | category | flops | bytes accessed | tf_op | source)
XLA Modules:
  0.0 276.8 jit_solution(13097134514686713037)
XLA Ops:
  6.5 0.0 all-gather.2.cloned.1.call-start
  6.5 1.3 constant_dynamic-slice_fusion
  7.8 0.5 copy.22
  8.4 0.7 convert_element_type.10
  9.1 0.2 broadcast_in_dim.140
  9.3 0.3 reshape.119
  9.5 0.1 constant_dynamic-slice_fusion.1
  9.6 0.1 bitcast_multiply_fusion
  9.7 1.4 copy.19
  11.1 0.0 all-gather.2.cloned.1.call-update
  11.1 0.0 reduce-scatter.2.cloned.1.call-start
  11.1 10.1 %copy.20 = bf16[120,30720]{0,1:T(8,128)(2,1)} copy(bf16[120,30720]{1,0:T(8,128)(2,1)} %param.8) | data formatting | bytes 14745600 | tf_op args[0]
  21.3 126.3 %all_to_all.19 = bf16[120,32,960]{0,2,1:T(8,128)(2,1)S(1)} all-to-all(bf16[120,32,960]{0,2,1:T(8,128)(2,1)} %bitcast.13), channel_id=1, replica_groups=mesh['z'=8,'y'=4,'x'=4,'core'=2] {'x','core','y'}, dimensions={1} | all-to-all | bytes 14745600 | tf_op jit(solution)/shard_map/all_to_all | solution.py:50
  147.6 8.2 %copy.21 = bf16[32,120,960]{1,0,2:T(8,128)(2,1)} copy(bf16[32,120,960]{1,2,0:T(8,128)(2,1)S(1)} %bitcast.12) | data formatting | bytes 14745600 | tf_op jit(solution)/shard_map/all_to_all | solution.py:50
  155.8 15.6 %all_to_all.17 = bf16[3840,960]{0,1:T(8,128)(2,1)} reshape(bf16[32,120,960]{1,0,2:T(8,128)(2,1)} %copy.21) | data formatting | bytes 14745600 | tf_op jit(solution)/shard_map/all_to_all | solution.py:50
  171.4 0.0 copy-start.4
  171.4 0.0 copy-start
  171.4 0.0 copy-start.1
  171.4 0.0 copy-start.2
  171.4 0.0 copy-start.3
  171.5 0.0 all-gather.2.cloned.1.call-done
  171.5 13.7 %convolution_bitcast_fusion = f32[960,1024]{1,0:T(8,128)} fusion(bf16[3840,960]{0,1:T(8,128)(2,1)} %all_to_all.17, bf16[3840,1024]{1,0:T(8,128)(2,1)} %all-gather.2.cloned.1.call-done), kind=kOutput, calls=%fused_computation | convolution fusion | flops 7549747200 | bytes 19169280 | tf_op jit(solution)/shard_map/dot_general | solution.py:51
  185.2 0.0 reduce-scatter.2.cloned.1.call-update
  185.2 0.0 copy-done.4
  185.2 6.9 %collective-permute-start = (bf16[960,128]{1,0:T(8,128)(2,1)S(1)}, bf16[960,128]{1,0:T(8,128)(2,1)S(1)}, u32[]{:S(2)}, u32[]{:S(2)}) collective-permute-start(bf16[960,128]{1,0:T(8,128)(2,1)S(1)} %copy-done.4), channel_id=1, source_target_pairs={{0,0},{1,32},{2,64},{3,96},{4,128},{5,160},{6,192},{7,224},{32,1},... | collective-permute-start | bytes 737288 | tf_op jit(solution)/shard_map/ppermute | solution.py:57
  192.1 0.0 copy-done
  192.1 0.1 select_reduce_fusion.6
  192.2 0.0 copy-done.1
  192.2 0.1 select_reduce_fusion.4
  192.4 0.2 select_reduce_fusion.2
  192.6 0.4 select_reduce_fusion
  193.0 0.0 copy-done.2
  193.0 0.1 select_reduce_fusion.7
  193.1 0.0 copy-done.3
  193.1 0.1 select_reduce_fusion.5
  193.2 0.2 select_reduce_fusion.3
  193.4 0.4 select_reduce_fusion.1
  193.8 19.5 %collective-permute-done = bf16[960,128]{1,0:T(8,128)(2,1)S(1)} collective-permute-done((bf16[960,128]{1,0:T(8,128)(2,1)S(1)}, bf16[960,128]{1,0:T(8,128)(2,1)S(1)}, u32[]{:S(2)}, u32[]{:S(2)}) %collective-permute-start) | collective-permute-done | bytes 245792 | tf_op jit(solution)/shard_map/ppermute | solution.py:57
  213.3 33.6 %reduce-scatter.2.cloned.1.call-done = f32[960,128]{1,0:T(8,128)} async-done(((f32[960,1024]{1,0:T(8,128)}), f32[960,128]{1,0:T(8,128)}) %reduce-scatter.2.cloned.1.call-update) | async-done | bytes 491536 | tf_op jit(solution)/shard_map/reduce_scatter | solution.py:54
  246.8 1.3 select_convert_fusion
  248.2 3.0 %collective-permute-start.1 = (bf16[960,128]{1,0:T(8,128)(2,1)S(1)}, bf16[960,128]{1,0:T(8,128)(2,1)S(1)}, u32[]{:S(2)}, u32[]{:S(2)}) collective-permute-start(bf16[960,128]{1,0:T(8,128)(2,1)S(1)} %select_convert_fusion), channel_id=1, source_target_pairs={{0,0},{1,32},{2,64},{3,96},{4,128},{5,160},{6,192},{7,224},{32,1},... | collective-permute-start | bytes 737288 | tf_op jit(solution)/shard_map/ppermute | solution.py:73
  251.2 18.0 %collective-permute-done.1 = bf16[960,128]{1,0:T(8,128)(2,1)S(1)} collective-permute-done((bf16[960,128]{1,0:T(8,128)(2,1)S(1)}, bf16[960,128]{1,0:T(8,128)(2,1)S(1)}, u32[]{:S(2)}, u32[]{:S(2)}) %collective-permute-start.1) | collective-permute-done | bytes 245792 | tf_op jit(solution)/shard_map/ppermute | solution.py:73
  269.3 0.7 copy.24
  (6 shorter events, 0.1 us)
Async XLA Ops:
  6.5 164.9 %all-gather.2.cloned.1.call-start = ((), (), s32[]{:S(2)}) async-start(), calls=%async_computation.2 | async-start | bytes 8847360 | tf_op jit(solution)/shard_map/all_gather | solution.py:48
  11.1 235.7 %reduce-scatter.2.cloned.1.call-start = ((), (), s32[]{:S(2)}) async-start(), calls=%async_computation.3 | async-start | bytes 4423680 | tf_op jit(solution)/shard_map/reduce_scatter | solution.py:54
  171.4 13.8 %copy-start.4 = (bf16[960,128]{1,0:T(8,128)(2,1)S(1)}, bf16[960,128]{1,0:T(8,128)(2,1)}, u32[]{:S(2)}) copy-start(bf16[960,128]{1,0:T(8,128)(2,1)} %param.11) | copy-start | bytes 737284
  171.4 20.7 %copy-start = (f32[192]{0:T(256)S(1)}, f32[192]{0:T(256)}, u32[]{:S(2)}) copy-start(f32[192]{0:T(256)} %param.15) | copy-start | bytes 2308
  171.4 20.8 %copy-start.1 = (f32[240]{0:T(256)S(1)}, f32[240]{0:T(256)}, u32[]{:S(2)}) copy-start(f32[240]{0:T(256)} %param.14) | copy-start | bytes 2884
  171.4 21.5 %copy-start.2 = (s32[192]{0:T(256)S(1)}, s32[192]{0:T(256)}, u32[]{:S(2)}) copy-start(s32[192]{0:T(256)} %param.13) | copy-start | bytes 2308
  171.4 21.6 %copy-start.3 = (s32[240]{0:T(256)S(1)}, s32[240]{0:T(256)}, u32[]{:S(2)}) copy-start(s32[240]{0:T(256)} %param.12) | copy-start | bytes 2884
  185.2 28.1 %collective-permute-start = (bf16[960,128]{1,0:T(8,128)(2,1)S(1)}, bf16[960,128]{1,0:T(8,128)(2,1)S(1)}, u32[]{:S(2)}, u32[]{:S(2)}) collective-permute-start(bf16[960,128]{1,0:T(8,128)(2,1)S(1)} %copy-done.4), channel_id=1, source_target_pairs={{0,0},{1,32},{2,64},{3,96},{4,128},{5,160},{6,192},{7,224},{32,1},... | collective-permute-start | bytes 737288 | tf_op jit(solution)/shard_map/ppermute | solution.py:57
  248.2 21.1 %collective-permute-start.1 = (bf16[960,128]{1,0:T(8,128)(2,1)S(1)}, bf16[960,128]{1,0:T(8,128)(2,1)S(1)}, u32[]{:S(2)}, u32[]{:S(2)}) collective-permute-start(bf16[960,128]{1,0:T(8,128)(2,1)S(1)} %select_convert_fusion), channel_id=1, source_target_pairs={{0,0},{1,32},{2,64},{3,96},{4,128},{5,160},{6,192},{7,224},{32,1},... | collective-permute-start | bytes 737288 | tf_op jit(solution)/shard_map/ppermute | solution.py:73
Sparse Core Ops, SparseCore 0:
  11.2 113.2 all-gather.1
  185.3 61.4 reduce-scatter.1

commit v2 on v1

--- a/solution.py
+++ b/solution.py
@@ -4,6 +4,7 @@
 from jax.sharding import Mesh, PartitionSpec as P
 
 BLK = 64
+CHUNKS = 2
 
 Z, Y, X, C = "z", "y", "x", "core"
 COL = (X, C)
@@ -47,11 +48,22 @@
     ).reshape(span, jb_all)
     masked_all = lax.all_gather(masked, COL, axis=0, tiled=True)
 
-    plane_amps = lax.all_to_all(amps, (X, C, Y), split_axis=1, concat_axis=0, tiled=True)
-    partial_value = lax.dot_general(
-        plane_amps, masked_all, (((0,), (0,)), ((), ())), preferred_element_type=jnp.float32
-    )
-    cycle_sum = lax.psum_scatter(partial_value, Z, scatter_dimension=1, tiled=True)
+    groups = lax.axis_size((X, C, Y))
+    width = amps.shape[1] // groups // CHUNKS
+    pieces = amps.reshape(sub, groups, CHUNKS, width)
+    sums = []
+    previous = None
+    for k in range(CHUNKS):
+        piece = pieces[:, :, k, :].reshape(sub, groups * width)
+        if previous is not None:
+            previous, piece = lax.optimization_barrier((previous, piece))
+            sums.append(lax.psum_scatter(previous, Z, scatter_dimension=1, tiled=True))
+        plane_amps = lax.all_to_all(piece, (X, C, Y), split_axis=1, concat_axis=0, tiled=True)
+        previous = lax.dot_general(
+            plane_amps, masked_all, (((0,), (0,)), ((), ())), preferred_element_type=jnp.float32
+        )
+    sums.append(lax.psum_scatter(previous, Z, scatter_dimension=1, tiled=True))
+    cycle_sum = jnp.concatenate(sums, axis=0)
 
     perm = swap_perm(nz, ncol)
     coulomb_here = lax.ppermute(coulomb, (Z, X, C), perm)

time: 278 us -> 280 us (level)
  blocking collectives: 126 us -> 0 us
  waiting for transfers between devices: 71.2 us -> 159 us
  starting transfers between devices: 9.94 us -> 29.5 us
  local copies, waits for them, and re-layouts: 38.4 us -> 53.2 us
  matrix products: 13.7 us -> 19.4 us
    all_to_all x1 -> x0, blocking collectives: 126 us -> none  [local(): lax.all_to_all(amps, (X, C, Y), split_axis=1, concat_axis=0, tiled=True)]
    all_to_all x0 -> x2, waiting for transfers between devices: none -> 105 us  [local(): lax.all_to_all(piece, (X, C, Y), split_axis=1, concat_axis=0, tiled=True)]
    all_to_all x0 -> x2, starting transfers between devices: none -> 15.3 us  [local(): lax.all_to_all(piece, (X, C, Y), split_axis=1, concat_axis=0, tiled=True)]
    reduce_scatter x1 -> x2, waiting for transfers between devices: 33.6 us -> 18.7 us  [local(): sums.append(lax.psum_scatter(previous, Z, scatter_dimension=1, tiled=True))]
    another operation x0 -> x1, local copies, waits for them, and re-layouts: none -> 6.19 us  [local(): piece = pieces[:, :, k, :].reshape(sub, groups * width)]
    dot_general x1 -> x2, matrix products: 13.7 us -> 19.4 us  [local(): lax.dot_general(plane_amps, masked_all, (((0,), (0,)), ((), ())), preferr...]
    slice x0 -> x1, local copies, waits for them, and re-layouts: none -> 5.67 us  [local(): piece = pieces[:, :, k, :].reshape(sub, groups * width)]
    ppermute x1, starting transfers between devices: 3.02 us -> 7.74 us  [local(): return lax.ppermute(out, (Z, X, C), perm)]
  transfers between devices with their start and end apart: 4 -> 7, of which waited for: 3 -> 5; matrix products, arithmetic and copies ran while one was open for 7% -> 16% of each run, Pallas kernels for 0% -> 0%
where the time goes in v2:
time: 280 us; the launch traced here: 278 us
  waiting for transfers between devices  159 us (57%)
  local copies, waits for them, and re-layouts  53.2 us (19%)
  starting transfers between devices  29.5 us (11%)
  matrix products  19.4 us (7%)
  between operations  13.3 us (5%)
  other arithmetic  3.02 us (1%)
    all_to_all x2, waiting for transfers between devices, local(): lax.all_to_all(piece, (X, C, Y), split_axis=1, concat_axis=0, tiled=True)  105 us
    all_to_all x4, local copies, waits for them, and re-layouts, local(): lax.all_to_all(piece, (X, C, Y), split_axis=1, concat_axis=0, tiled=True)  26.8 us
    dot_general x2, matrix products, local(): lax.dot_general(plane_amps, masked_all, (((0,), (0,)), ((), ())), preferr...  19.4 us
    ppermute x1, waiting for transfers between devices, local(): coulomb_here = lax.ppermute(coulomb, (Z, X, C), perm)  19 us
    reduce_scatter x2, waiting for transfers between devices, local(): sums.append(lax.psum_scatter(previous, Z, scatter_dimension=1, tiled=True))  18.7 us
    ppermute x1, waiting for transfers between devices, local(): return lax.ppermute(out, (Z, X, C), perm)  16.1 us
    all_to_all x2, starting transfers between devices, local(): lax.all_to_all(piece, (X, C, Y), split_axis=1, concat_axis=0, tiled=True)  15.3 us
    unnamed x15, local copies, waits for them, and re-layouts  11.4 us
  transfers between devices with their start and end apart: 7, of which 5 were waited for; matrix products, arithmetic and copies ran while one was open for 16% of the time, Pallas kernels for 0%

profile of v2, /device:TPU:7, one launch (start us, length us, event | category | flops | bytes accessed | tf_op | source)
XLA Modules:
  0.0 277.7 jit_solution(2675612284590024433)
XLA Ops:
  6.5 0.0 copy-start
  6.5 0.0 all-gather.2.cloned.1.call-start
  6.5 1.3 constant_dynamic-slice_fusion
  7.8 0.5 copy.42
  8.4 0.0 copy-done
  8.4 0.2 broadcast_in_dim.140
  8.6 0.3 reshape.126
  8.9 0.1 constant_dynamic-slice_fusion.1
  9.0 0.1 bitcast_multiply_fusion
  9.0 1.3 copy.29
  10.3 0.0 all-gather.2.cloned.1.call-update
  10.4 10.1 %copy.30 = bf16[120,30720]{0,1:T(8,128)(2,1)} copy(bf16[120,30720]{1,0:T(8,128)(2,1)} %param.8) | data formatting | bytes 14745600 | tf_op args[0]
  20.5 5.7 %fusion.12 = (bf16[120,32,1,480]{0,3,2,1:T(8,128)(2,1)}, bf16[120,32,480]{0,2,1:T(8,128)(2,1)}) fusion(bf16[120,32,2,480]{0,3,2,1:T(8,128)(2,1)} %bitcast.21), kind=kLoop, calls=%fused_computation.47 | loop fusion | bytes 14745600 | tf_op jit(solution)/shard_map/slice | solution.py:57
  26.1 6.5 %copy.32 = bf16[120,32,480]{2,0,1:T(8,128)(2,1)} copy(bf16[120,32,480]{0,2,1:T(8,128)(2,1)} %get-tuple-element.10) | data formatting | bytes 7372800 | tf_op jit(solution)/shard_map/all_to_all | solution.py:61
  32.6 8.0 %all-to-all-start = ((bf16[120,32,480]{2,0,1:T(8,128)(2,1)}), bf16[120,32,480]{2,0,1:T(8,128)(2,1)}, u32[]{:S(2)}, u32[]{:S(2)}) async-start(bf16[120,32,480]{2,0,1:T(8,128)(2,1)} %copy.32), calls=%async_computation | async-start | bytes 7864320 | tf_op jit(solution)/shard_map/all_to_all | solution.py:61
  40.6 6.2 %copy.40 = bf16[120,15360]{1,0:T(8,128)(2,1)} copy(bf16[120,15360]{0,1:T(8,128)(2,1)} %bitcast.23) | data formatting | bytes 7372800 | tf_op jit(solution)/shard_map/reshape;squeeze | solution.py:57
  46.8 58.4 %all-to-all-done = bf16[120,32,480]{2,0,1:T(8,128)(2,1)} async-done(((bf16[120,32,480]{2,0,1:T(8,128)(2,1)}), bf16[120,32,480]{2,0,1:T(8,128)(2,1)}, u32[]{:S(2)}, u32[]{:S(2)}) %all-to-all-start) | async-done | bytes 3686432 | tf_op jit(solution)/shard_map/all_to_all | solution.py:61
  105.2 0.0 all-gather.2.cloned.1.call-done
  105.2 9.7 %convolution_bitcast_fusion = f32[480,1024]{1,0:T(8,128)} fusion(bf16[3840,480]{1,0:T(8,128)(2,1)} %bitcast.4, bf16[3840,1024]{1,0:T(8,128)(2,1)} %all-gather.2.cloned.1.call-done), kind=kOutput, calls=%fused_computation.1 | convolution fusion | flops 3774873600 | bytes 13516800 | tf_op jit(solution)/shard_map/dot_general | solution.py:62
  114.9 6.1 %copy.41 = bf16[120,15360]{0,1:T(8,128)(2,1)} copy(bf16[120,15360]{1,0:T(8,128)(2,1)} %copy.40) | data formatting | bytes 7372800 | tf_op jit(solution)/shard_map/all_to_all | solution.py:61
  121.0 7.3 %all-to-all-start.1 = ((bf16[120,32,480]{0,2,1:T(8,128)(2,1)}), bf16[120,32,480]{0,2,1:T(8,128)(2,1)}, u32[]{:S(2)}, u32[]{:S(2)}) async-start(bf16[120,32,480]{0,2,1:T(8,128)(2,1)} %bitcast.22), calls=%async_computation.2 | async-start | bytes 7864320 | tf_op jit(solution)/shard_map/all_to_all | solution.py:61
  128.3 0.0 reduce-scatter.3.cloned.1.call-start
  128.4 0.7 reduce-scatter.3.cloned.1.call-update
  129.1 0.0 reduce-scatter.5.cloned.1.call-start
  129.1 46.2 %all-to-all-done.1 = bf16[120,32,480]{0,2,1:T(8,128)(2,1)} async-done(((bf16[120,32,480]{0,2,1:T(8,128)(2,1)}), bf16[120,32,480]{0,2,1:T(8,128)(2,1)}, u32[]{:S(2)}, u32[]{:S(2)}) %all-to-all-start.1) | async-done | bytes 3686432 | tf_op jit(solution)/shard_map/all_to_all | solution.py:61
  175.3 5.6 %copy.36 = bf16[32,120,480]{1,0,2:T(8,128)(2,1)} copy(bf16[32,120,480]{1,2,0:T(8,128)(2,1)} %bitcast.8) | data formatting | bytes 7372800 | tf_op jit(solution)/shard_map/all_to_all | solution.py:61
  180.9 8.6 %all_to_all.35 = bf16[3840,480]{0,1:T(8,128)(2,1)} reshape(bf16[32,120,480]{1,0,2:T(8,128)(2,1)} %copy.36) | data formatting | bytes 7372800 | tf_op jit(solution)/shard_map/all_to_all | solution.py:61
  189.6 0.0 copy-start.5
  189.6 0.0 copy-start.1
  189.6 0.0 copy-start.2
  189.6 0.0 copy-start.3
  189.6 0.0 copy-start.4
  189.6 9.7 %fusion.13 = f32[480,1024]{1,0:T(8,128)} fusion(bf16[3840,480]{0,1:T(8,128)(2,1)} %all_to_all.35, bf16[3840,1024]{1,0:T(8,128)(2,1)} %all-gather.2.cloned.1.call-done), kind=kOutput, calls=%fused_computation.48 | convolution fusion | flops 3774873600 | bytes 13516800 | tf_op jit(solution)/shard_map/dot_general | solution.py:62
  199.3 0.0 reduce-scatter.5.cloned.1.call-update
  199.3 0.0 copy-done.5
  199.4 6.4 %collective-permute-start = (bf16[960,128]{1,0:T(8,128)(2,1)S(1)}, bf16[960,128]{1,0:T(8,128)(2,1)S(1)}, u32[]{:S(2)}, u32[]{:S(2)}) collective-permute-start(bf16[960,128]{1,0:T(8,128)(2,1)S(1)} %copy-done.5), channel_id=1, source_target_pairs={{0,0},{1,32},{2,64},{3,96},{4,128},{5,160},{6,192},{7,224},{32,1},... | collective-permute-start | bytes 737288 | tf_op jit(solution)/shard_map/ppermute | solution.py:69
  205.8 0.0 copy-done.1
  205.8 0.1 select_reduce_fusion.6
  205.9 0.0 copy-done.2
  205.9 0.1 select_reduce_fusion.4
  206.1 0.2 select_reduce_fusion.2
  206.3 0.4 select_reduce_fusion
  206.7 0.0 copy-done.3
  206.7 0.1 select_reduce_fusion.7
  206.8 0.0 copy-done.4
  206.8 0.1 select_reduce_fusion.5
  206.9 0.2 select_reduce_fusion.3
  207.1 0.4 select_reduce_fusion.1
  207.5 19.0 %collective-permute-done = bf16[960,128]{1,0:T(8,128)(2,1)S(1)} collective-permute-done((bf16[960,128]{1,0:T(8,128)(2,1)S(1)}, bf16[960,128]{1,0:T(8,128)(2,1)S(1)}, u32[]{:S(2)}, u32[]{:S(2)}) %collective-permute-start) | collective-permute-done | bytes 245792 | tf_op jit(solution)/shard_map/ppermute | solution.py:69
  226.5 0.0 reduce-scatter.3.cloned.1.call-done
  226.5 18.7 %reduce-scatter.5.cloned.1.call-done = f32[480,128]{1,0:T(8,128)} async-done(((f32[480,1024]{1,0:T(8,128)}), f32[480,128]{1,0:T(8,128)}) %reduce-scatter.5.cloned.1.call-update) | async-done | bytes 245776 | tf_op jit(solution)/shard_map/reduce_scatter | solution.py:65
  245.2 1.4 fusion.2
  246.6 7.7 %collective-permute-start.1 = (bf16[960,128]{1,0:T(8,128)(2,1)S(1)}, bf16[960,128]{1,0:T(8,128)(2,1)S(1)}, u32[]{:S(2)}, u32[]{:S(2)}) collective-permute-start(bf16[960,128]{1,0:T(8,128)(2,1)S(1)} %fusion.2), channel_id=1, source_target_pairs={{0,0},{1,32},{2,64},{3,96},{4,128},{5,160},{6,192},{7,224},{32,1},... | collective-permute-start | bytes 737288 | tf_op jit(solution)/shard_map/ppermute | solution.py:85
  254.3 16.1 %collective-permute-done.1 = bf16[960,128]{1,0:T(8,128)(2,1)S(1)} collective-permute-done((bf16[960,128]{1,0:T(8,128)(2,1)S(1)}, bf16[960,128]{1,0:T(8,128)(2,1)S(1)}, u32[]{:S(2)}, u32[]{:S(2)}) %collective-permute-start.1) | collective-permute-done | bytes 245792 | tf_op jit(solution)/shard_map/ppermute | solution.py:85
  270.5 0.7 copy.44
  (7 shorter events, 0.1 us)
Async XLA Ops:
  6.5 1.8 copy-start
  6.5 98.7 %all-gather.2.cloned.1.call-start = ((), (), s32[]{:S(2)}) async-start(), calls=%async_computation.4 | async-start | bytes 8847360 | tf_op jit(solution)/shard_map/all_gather | solution.py:49
  32.6 72.6 %all-to-all-start = ((bf16[120,32,480]{2,0,1:T(8,128)(2,1)}), bf16[120,32,480]{2,0,1:T(8,128)(2,1)}, u32[]{:S(2)}, u32[]{:S(2)}) async-start(bf16[120,32,480]{2,0,1:T(8,128)(2,1)} %copy.32), calls=%async_computation | async-start | bytes 7864320 | tf_op jit(solution)/shard_map/all_to_all | solution.py:61
  121.0 54.3 %all-to-all-start.1 = ((bf16[120,32,480]{0,2,1:T(8,128)(2,1)}), bf16[120,32,480]{0,2,1:T(8,128)(2,1)}, u32[]{:S(2)}, u32[]{:S(2)}) async-start(bf16[120,32,480]{0,2,1:T(8,128)(2,1)} %bitcast.22), calls=%async_computation.2 | async-start | bytes 7864320 | tf_op jit(solution)/shard_map/all_to_all | solution.py:61
  128.3 98.2 %reduce-scatter.3.cloned.1.call-start = ((), (), s32[]{:S(2)}) async-start(), calls=%async_computation.5 | async-start | bytes 2211840 | tf_op jit(solution)/shard_map/reduce_scatter | solution.py:60
  129.1 116.2 %reduce-scatter.5.cloned.1.call-start = ((), (), s32[]{:S(2)}) async-start(), calls=%async_computation.6 | async-start | bytes 2211840 | tf_op jit(solution)/shard_map/reduce_scatter | solution.py:65
  189.6 9.8 %copy-start.5 = (bf16[960,128]{1,0:T(8,128)(2,1)S(1)}, bf16[960,128]{1,0:T(8,128)(2,1)}, u32[]{:S(2)}) copy-start(bf16[960,128]{1,0:T(8,128)(2,1)} %param.11) | copy-start | bytes 737284
  189.6 16.3 %copy-start.1 = (f32[192]{0:T(256)S(1)}, f32[192]{0:T(256)}, u32[]{:S(2)}) copy-start(f32[192]{0:T(256)} %param.15) | copy-start | bytes 2308
  189.6 16.4 %copy-start.2 = (f32[240]{0:T(256)S(1)}, f32[240]{0:T(256)}, u32[]{:S(2)}) copy-start(f32[240]{0:T(256)} %param.14) | copy-start | bytes 2884
  189.6 17.1 %copy-start.3 = (s32[192]{0:T(256)S(1)}, s32[192]{0:T(256)}, u32[]{:S(2)}) copy-start(s32[192]{0:T(256)} %param.13) | copy-start | bytes 2308
  189.6 17.2 %copy-start.4 = (s32[240]{0:T(256)S(1)}, s32[240]{0:T(256)}, u32[]{:S(2)}) copy-start(s32[240]{0:T(256)} %param.12) | copy-start | bytes 2884
  199.4 27.1 %collective-permute-start = (bf16[960,128]{1,0:T(8,128)(2,1)S(1)}, bf16[960,128]{1,0:T(8,128)(2,1)S(1)}, u32[]{:S(2)}, u32[]{:S(2)}) collective-permute-start(bf16[960,128]{1,0:T(8,128)(2,1)S(1)} %copy-done.5), channel_id=1, source_target_pairs={{0,0},{1,32},{2,64},{3,96},{4,128},{5,160},{6,192},{7,224},{32,1},... | collective-permute-start | bytes 737288 | tf_op jit(solution)/shard_map/ppermute | solution.py:69
  246.6 23.9 %collective-permute-start.1 = (bf16[960,128]{1,0:T(8,128)(2,1)S(1)}, bf16[960,128]{1,0:T(8,128)(2,1)S(1)}, u32[]{:S(2)}, u32[]{:S(2)}) collective-permute-start(bf16[960,128]{1,0:T(8,128)(2,1)S(1)} %fusion.2), channel_id=1, source_target_pairs={{0,0},{1,32},{2,64},{3,96},{4,128},{5,160},{6,192},{7,224},{32,1},... | collective-permute-start | bytes 737288 | tf_op jit(solution)/shard_map/ppermute | solution.py:85
Sparse Core Ops, SparseCore 0:
  10.5 87.6 all-gather.1
  131.7 38.7 reduce-scatter.2
  199.5 45.6 reduce-scatter.4

commit v3 on v1

--- a/solution.py
+++ b/solution.py
@@ -1,6 +1,8 @@
 import jax
 import jax.numpy as jnp
 from jax import lax
+from jax.experimental import pallas as pl
+from jax.experimental.pallas import tpu as pltpu
 from jax.sharding import Mesh, PartitionSpec as P
 
 BLK = 64
@@ -18,6 +20,36 @@
         jnp.zeros((), values_table.dtype),
     )
     return jnp.sum(picked, axis=1)
+
+
+def product_kernel(left_ref, right_ref, out_ref):
+    out_ref[...] = jnp.dot(left_ref[...], right_ref[...], preferred_element_type=jnp.float32)
+
+
+def product(left, right):
+    rows, depth = left.shape
+    width = right.shape[1]
+    tile = 256
+    return pl.pallas_call(
+        product_kernel,
+        out_shape=jax.ShapeDtypeStruct((rows, width), jnp.float32),
+        grid=(rows // tile,),
+        in_specs=[
+            pl.BlockSpec((tile, depth), lambda i: (i, 0)),
+            pl.BlockSpec((depth, width), lambda i: (0, 0)),
+        ],
+        out_specs=pl.BlockSpec((tile, width), lambda i: (i, 0)),
+        cost_estimate=pl.CostEstimate(
+            flops=2 * rows * depth * width,
+            bytes_accessed=2 * rows * depth + 2 * depth * width + 4 * rows * width,
+            transcendentals=0,
+        ),
+    )(left, right)
+
+
+def chunk_widths(total):
+    half = total // 2
+    return [half, total - half]
 
 
 def swap_perm(nz, nc):
@@ -45,13 +77,19 @@
     masked = (
         ci_rows.reshape(span, jb_all // block_size, block_size) * mask_rows[:, :, None]
     ).reshape(span, jb_all)
-    masked_all = lax.all_gather(masked, COL, axis=0, tiled=True)
+    masked_all_t = lax.all_gather(masked.T, COL, axis=1, tiled=True)
 
-    plane_amps = lax.all_to_all(amps, (X, C, Y), split_axis=1, concat_axis=0, tiled=True)
-    partial_value = lax.dot_general(
-        plane_amps, masked_all, (((0,), (0,)), ((), ())), preferred_element_type=jnp.float32
-    )
-    cycle_sum = lax.psum_scatter(partial_value, Z, scatter_dimension=1, tiled=True)
+    groups = lax.axis_size((X, C, Y))
+    pieces = amps.reshape(sub, groups, amps.shape[1] // groups)
+    sums = []
+    start = 0
+    for width in chunk_widths(pieces.shape[2]):
+        piece = jnp.transpose(pieces[:, :, start:start + width], (1, 0, 2))
+        start += width
+        plane_amps = lax.all_to_all(piece, (X, C, Y), split_axis=0, concat_axis=0, tiled=True)
+        partial_value = product(masked_all_t, plane_amps.reshape(groups * sub, width))
+        sums.append(lax.psum_scatter(partial_value, Z, scatter_dimension=0, tiled=True))
+    cycle_sum = jnp.concatenate(sums, axis=1).T
 
     perm = swap_perm(nz, ncol)
     coulomb_here = lax.ppermute(coulomb, (Z, X, C), perm)

time: 278 us -> 264 us (0.950)
  blocking collectives: 126 us -> 52.3 us
  waiting for transfers between devices: 71.2 us -> 111 us
  Pallas kernels: 0 us -> 17.9 us
  matrix products: 13.7 us -> 0 us
  starting transfers between devices: 9.94 us -> 22.1 us
  local copies, waits for them, and re-layouts: 38.4 us -> 42.8 us
    all_to_all x1, blocking collectives: 126 us -> 52.3 us  [local(): lax.all_to_all(piece, (X, C, Y), split_axis=0, concat_axis=0, tiled=True)]
    all_gather x1, waiting for transfers between devices: 0.02 us -> 54.3 us  [local(): masked_all_t = lax.all_gather(masked.T, COL, axis=1, tiled=True)]
    all_to_all x2 -> x0, local copies, waits for them, and re-layouts: 23.9 us -> none  [local(): lax.all_to_all(amps, (X, C, Y), split_axis=1, concat_axis=0, tiled=True)]
    pallas_call x0 -> x2, Pallas kernels: none -> 17.9 us  [product(): pl.pallas_call(product_kernel, out_shape=jax.ShapeDtypeStruct((rows, widt...]
    reduce_scatter x1 -> x2, waiting for transfers between devices: 33.6 us -> 18.7 us  [local(): lax.psum_scatter(partial_value, Z, scatter_dimension=0, tiled=True)]
    dot_general x1 -> x0, matrix products: 13.7 us -> none  [local(): lax.dot_general(plane_amps, masked_all, (((0,), (0,)), ((), ())), preferr...]
    reshape x0 -> x1, local copies, waits for them, and re-layouts: none -> 12.5 us  [local(): pieces = amps.reshape(sub, groups, amps.shape[1] // groups)]
    all_gather x0 -> x1, local copies, waits for them, and re-layouts: none -> 10.5 us  [local(): masked_all_t = lax.all_gather(masked.T, COL, axis=1, tiled=True)]
  transfers between devices with their start and end apart: 4 -> 6, of which waited for: 3 -> 4; matrix products, arithmetic and copies ran while one was open for 7% -> 15% of each run, Pallas kernels for 0% -> 3%
where the time goes in v3:
time: 264 us; the launch traced here: 263 us
  waiting for transfers between devices  111 us (42%)
  blocking collectives  52.3 us (20%)
  local copies, waits for them, and re-layouts  42.8 us (16%)
  starting transfers between devices  22.1 us (8%)
  Pallas kernels  17.9 us (7%)
  between operations  13.3 us (5%)
  other arithmetic  2.87 us (1%)
    all_gather x1, waiting for transfers between devices, local(): masked_all_t = lax.all_gather(masked.T, COL, axis=1, tiled=True)  54.3 us
    all_to_all x1, blocking collectives, local(): lax.all_to_all(piece, (X, C, Y), split_axis=0, concat_axis=0, tiled=True)  52.3 us
    ppermute x1, waiting for transfers between devices, local(): coulomb_here = lax.ppermute(coulomb, (Z, X, C), perm)  20.8 us
    reduce_scatter x2, waiting for transfers between devices, local(): lax.psum_scatter(partial_value, Z, scatter_dimension=0, tiled=True)  18.7 us
    pallas_call x2, Pallas kernels, product(): pl.pallas_call(product_kernel, out_shape=jax.ShapeDtypeStruct((rows, widt...  17.9 us
    ppermute x1, waiting for transfers between devices, local(): return lax.ppermute(out, (Z, X, C), perm)  17.6 us
    reshape x1, local copies, waits for them, and re-layouts, local(): pieces = amps.reshape(sub, groups, amps.shape[1] // groups)  12.5 us
    all_gather x1, local copies, waits for them, and re-layouts, local(): masked_all_t = lax.all_gather(masked.T, COL, axis=1, tiled=True)  10.5 us
  transfers between devices with their start and end apart: 6, of which 4 were waited for; matrix products, arithmetic and copies ran while one was open for 15% of the time, Pallas kernels for 3%

profile of v3, /device:TPU:7, one launch (start us, length us, event | category | flops | bytes accessed | tf_op | source)
XLA Modules:
  0.0 262.7 jit_solution(9945642867955565530)
XLA Ops:
  6.5 0.0 copy-start.1
  6.5 0.0 all-gather.2.cloned.1.call-start
  6.5 1.3 constant_dynamic-slice_fusion
  7.8 0.5 copy.42
  8.4 0.0 copy-done.1
  8.4 0.2 broadcast_in_dim.140
  8.6 0.3 reshape.125
  8.9 0.1 constant_dynamic-slice_fusion.1
  9.0 0.1 bitcast_multiply_fusion
  9.0 1.3 copy.36
  10.4 0.0 all-gather.2.cloned.1.call-update
  10.4 12.5 %reshape.126 = bf16[120,32,960]{2,1,0:T(8,128)(2,1)} reshape(bf16[120,30720]{1,0:T(8,128)(2,1)} %param.8) | data formatting | bytes 14745600 | tf_op jit(solution)/shard_map/reshape | solution.py:83
  22.9 6.6 %fusion.13 = (bf16[120,32,480]{2,1,0:T(8,128)(2,1)S(1)}, bf16[120,32,480]{2,1,0:T(8,128)(2,1)}) fusion(bf16[120,32,960]{2,1,0:T(8,128)(2,1)} %reshape.126), kind=kLoop, calls=%fused_computation.48 | loop fusion | bytes 14745600 | tf_op jit(solution)/shard_map/slice | solution.py:87
  29.5 4.2 %copy.48 = bf16[120,32,480]{2,0,1:T(8,128)(2,1)} copy(bf16[120,32,480]{2,1,0:T(8,128)(2,1)S(1)} %get-tuple-element.5) | data formatting | bytes 7372800
  33.7 8.2 %all-to-all-start = ((bf16[32,120,480]{2,1,0:T(8,128)(2,1)}), bf16[32,120,480]{2,1,0:T(8,128)(2,1)}, u32[]{:S(2)}, u32[]{:S(2)}) async-start(bf16[32,120,480]{2,1,0:T(8,128)(2,1)} %bitcast.23), calls=%async_computation | async-start | bytes 7864320 | tf_op jit(solution)/shard_map/all_to_all | solution.py:89
  41.8 0.0 reduce-scatter.3.cloned.1.call-start
  41.9 54.3 %all-gather.2.cloned.1.call-done = bf16[1024,3840]{0,1:T(8,128)(2,1)} async-done(((bf16[1024,480]{0,1:T(8,128)(2,1)}), bf16[1024,3840]{0,1:T(8,128)(2,1)}) %all-gather.2.cloned.1.call-update) | async-done | bytes 7864336 | tf_op jit(solution)/shard_map/all_gather | solution.py:80
  96.2 10.5 %copy.38.left_ref = bf16[1024,3840]{1,0:T(8,128)(2,1)} copy(bf16[1024,3840]{0,1:T(8,128)(2,1)} %all-gather.2.cloned.1.call-done) | data formatting | bytes 15728640 | tf_op jit(solution)/shard_map/all_gather | solution.py:80
  106.7 0.0 all-to-all-done
  106.7 8.9 %shard_map.82 = f32[1024,480]{1,0:T(8,128)} custom-call(bf16[1024,3840]{1,0:T(8,128)(2,1)} %copy.38.left_ref, bf16[3840,480]{1,0:T(8,128)(2,1)} %bitcast.3.right_ref), custom_call_target="tpu_custom_call" | custom-call | flops 3774873600 | bytes 13516800 | tf_op jit(solution)/shard_map/pallas_call | solution.py:33
  115.6 0.0 reduce-scatter.3.cloned.1.call-update
  115.7 0.0 reduce-scatter.5.cloned.1.call-start
  115.7 4.3 %copy.47 = bf16[120,32,480]{2,0,1:T(8,128)(2,1)S(1)} copy(bf16[120,32,480]{2,1,0:T(8,128)(2,1)} %get-tuple-element.6) | data formatting | bytes 7372800
  120.0 52.3 %all_to_all.10 = bf16[32,120,480]{2,1,0:T(8,128)(2,1)} all-to-all(bf16[32,120,480]{2,1,0:T(8,128)(2,1)S(1)} %bitcast.24), channel_id=1, replica_groups=mesh['z'=8,'y'=4,'x'=4,'core'=2] {'x','core','y'}, dimensions={0} | all-to-all | bytes 7372800 | tf_op jit(solution)/shard_map/all_to_all | solution.py:89
  172.3 0.0 copy-start
  172.3 0.0 copy-start.2
  172.3 0.0 copy-start.3
  172.3 0.0 copy-start.4
  172.3 0.0 copy-start.5
  172.3 9.0 %shard_map.83 = f32[1024,480]{1,0:T(8,128)} custom-call(bf16[1024,3840]{1,0:T(8,128)(2,1)} %copy.38.left_ref, bf16[3840,480]{1,0:T(8,128)(2,1)} %bitcast.26), custom_call_target="tpu_custom_call" | custom-call | flops 3774873600 | bytes 13516800 | tf_op jit(solution)/shard_map/pallas_call | solution.py:33
  181.3 0.0 reduce-scatter.5.cloned.1.call-update
  181.3 0.0 copy-done
  181.4 0.1 copy.34
  181.5 6.7 %collective-permute-start = (bf16[960,128]{0,1:T(8,128)(2,1)S(1)}, bf16[960,128]{0,1:T(8,128)(2,1)S(1)}, u32[]{:S(2)}, u32[]{:S(2)}) collective-permute-start(bf16[960,128]{0,1:T(8,128)(2,1)S(1)} %copy.34), channel_id=1, source_target_pairs={{0,0},{1,32},{2,64},{3,96},{4,128},{5,160},{6,192},{7,224},{32,1},... | collective-permute-start | bytes 737288 | tf_op jit(solution)/shard_map/ppermute | solution.py:95
  188.3 0.0 copy-done.2
  188.3 0.1 select_reduce_fusion.4
  188.4 0.0 copy-done.3
  188.4 0.2 select_reduce_fusion.2
  188.6 0.0 copy-done.4
  188.6 0.2 select_reduce_fusion.3
  188.8 0.4 select_reduce_fusion
  189.2 0.0 copy-done.5
  189.2 0.4 select_reduce_fusion.1
  189.5 0.1 select_reduce_fusion.6
  189.7 0.1 select_reduce_fusion.7
  189.8 0.1 select_reduce_fusion.5
  189.9 20.8 %collective-permute-done = bf16[960,128]{0,1:T(8,128)(2,1)S(1)} collective-permute-done((bf16[960,128]{0,1:T(8,128)(2,1)S(1)}, bf16[960,128]{0,1:T(8,128)(2,1)S(1)}, u32[]{:S(2)}, u32[]{:S(2)}) %collective-permute-start) | collective-permute-done | bytes 245792 | tf_op jit(solution)/shard_map/ppermute | solution.py:95
  210.7 0.0 reduce-scatter.3.cloned.1.call-done
  210.7 18.7 %reduce-scatter.5.cloned.1.call-done = f32[128,480]{1,0:T(8,128)} async-done(((f32[1024,480]{1,0:T(8,128)}), f32[128,480]{1,0:T(8,128)}) %reduce-scatter.5.cloned.1.call-update) | async-done | bytes 245776 | tf_op jit(solution)/shard_map/reduce_scatter | solution.py:91
  229.4 1.2 fusion.3
  230.6 7.1 %collective-permute-start.1 = (bf16[960,128]{0,1:T(8,128)(2,1)S(1)}, bf16[960,128]{0,1:T(8,128)(2,1)S(1)}, u32[]{:S(2)}, u32[]{:S(2)}) collective-permute-start(bf16[960,128]{0,1:T(8,128)(2,1)S(1)} %fusion.3), channel_id=1, source_target_pairs={{0,0},{1,32},{2,64},{3,96},{4,128},{5,160},{6,192},{7,224},{32,1},... | collective-permute-start | bytes 737288 | tf_op jit(solution)/shard_map/ppermute | solution.py:111
  237.8 17.6 %collective-permute-done.1 = bf16[960,128]{0,1:T(8,128)(2,1)S(1)} collective-permute-done((bf16[960,128]{0,1:T(8,128)(2,1)S(1)}, bf16[960,128]{0,1:T(8,128)(2,1)S(1)}, u32[]{:S(2)}, u32[]{:S(2)}) %collective-permute-start.1) | collective-permute-done | bytes 245792 | tf_op jit(solution)/shard_map/ppermute | solution.py:111
  255.3 0.8 copy.41
  (7 shorter events, 0.1 us)
Async XLA Ops:
  6.5 1.8 copy-start.1
  6.5 89.6 %all-gather.2.cloned.1.call-start = ((), (), s32[]{:S(2)}) async-start(), calls=%async_computation.4 | async-start | bytes 8847360 | tf_op jit(solution)/shard_map/all_gather | solution.py:80
  33.7 73.0 %all-to-all-start = ((bf16[32,120,480]{2,1,0:T(8,128)(2,1)}), bf16[32,120,480]{2,1,0:T(8,128)(2,1)}, u32[]{:S(2)}, u32[]{:S(2)}) async-start(bf16[32,120,480]{2,1,0:T(8,128)(2,1)} %bitcast.23), calls=%async_computation | async-start | bytes 7864320 | tf_op jit(solution)/shard_map/all_to_all | solution.py:89
  41.8 168.8 %reduce-scatter.3.cloned.1.call-start = ((), (), s32[]{:S(2)}) async-start(), calls=%async_computation.5 | async-start | bytes 2359296 | tf_op jit(solution)/shard_map/reduce_scatter | solution.py:91
  115.7 113.7 %reduce-scatter.5.cloned.1.call-start = ((), (), s32[]{:S(2)}) async-start(), calls=%async_computation.6 | async-start | bytes 2359296 | tf_op jit(solution)/shard_map/reduce_scatter | solution.py:91
  172.3 9.1 %copy-start = (bf16[960,128]{1,0:T(8,128)(2,1)S(1)}, bf16[960,128]{1,0:T(8,128)(2,1)}, u32[]{:S(2)}) copy-start(bf16[960,128]{1,0:T(8,128)(2,1)} %param.11) | copy-start | bytes 737284
  172.3 16.0 %copy-start.2 = (f32[240]{0:T(256)S(1)}, f32[240]{0:T(256)}, u32[]{:S(2)}) copy-start(f32[240]{0:T(256)} %param.14) | copy-start | bytes 2884
  172.3 16.1 %copy-start.3 = (f32[192]{0:T(256)S(1)}, f32[192]{0:T(256)}, u32[]{:S(2)}) copy-start(f32[192]{0:T(256)} %param.15) | copy-start | bytes 2308
  172.3 16.3 %copy-start.4 = (s32[192]{0:T(256)S(1)}, s32[192]{0:T(256)}, u32[]{:S(2)}) copy-start(s32[192]{0:T(256)} %param.13) | copy-start | bytes 2308
  172.3 16.9 %copy-start.5 = (s32[240]{0:T(256)S(1)}, s32[240]{0:T(256)}, u32[]{:S(2)}) copy-start(s32[240]{0:T(256)} %param.12) | copy-start | bytes 2884
  181.5 29.2 %collective-permute-start = (bf16[960,128]{0,1:T(8,128)(2,1)S(1)}, bf16[960,128]{0,1:T(8,128)(2,1)S(1)}, u32[]{:S(2)}, u32[]{:S(2)}) collective-permute-start(bf16[960,128]{0,1:T(8,128)(2,1)S(1)} %copy.34), channel_id=1, source_target_pairs={{0,0},{1,32},{2,64},{3,96},{4,128},{5,160},{6,192},{7,224},{32,1},... | collective-permute-start | bytes 737288 | tf_op jit(solution)/shard_map/ppermute | solution.py:95
  230.6 24.7 %collective-permute-start.1 = (bf16[960,128]{0,1:T(8,128)(2,1)S(1)}, bf16[960,128]{0,1:T(8,128)(2,1)S(1)}, u32[]{:S(2)}, u32[]{:S(2)}) collective-permute-start(bf16[960,128]{0,1:T(8,128)(2,1)S(1)} %fusion.3), channel_id=1, source_target_pairs={{0,0},{1,32},{2,64},{3,96},{4,128},{5,160},{6,192},{7,224},{32,1},... | collective-permute-start | bytes 737288 | tf_op jit(solution)/shard_map/ppermute | solution.py:111
Sparse Core Ops, SparseCore 0:
  10.5 85.5 all-gather.1
  115.8 37.9 reduce-scatter.2
  181.5 47.8 reduce-scatter.4

commit v4 on v3

--- a/solution.py
+++ b/solution.py
@@ -23,22 +23,24 @@
 
 
 def product_kernel(left_ref, right_ref, out_ref):
-    out_ref[...] = jnp.dot(left_ref[...], right_ref[...], preferred_element_type=jnp.float32)
+    out_ref[...] = lax.dot_general(
+        left_ref[...], right_ref[...], (((0,), (0,)), ((), ())), preferred_element_type=jnp.float32
+    )
 
 
 def product(left, right):
-    rows, depth = left.shape
+    depth, rows = left.shape
     width = right.shape[1]
     tile = 256
     return pl.pallas_call(
         product_kernel,
         out_shape=jax.ShapeDtypeStruct((rows, width), jnp.float32),
-        grid=(rows // tile,),
+        grid=(width // tile,),
         in_specs=[
-            pl.BlockSpec((tile, depth), lambda i: (i, 0)),
-            pl.BlockSpec((depth, width), lambda i: (0, 0)),
+            pl.BlockSpec((depth, rows), lambda j: (0, 0)),
+            pl.BlockSpec((depth, tile), lambda j: (0, j)),
         ],
-        out_specs=pl.BlockSpec((tile, width), lambda i: (i, 0)),
+        out_specs=pl.BlockSpec((rows, tile), lambda j: (0, j)),
         cost_estimate=pl.CostEstimate(
             flops=2 * rows * depth * width,
             bytes_accessed=2 * rows * depth + 2 * depth * width + 4 * rows * width,
@@ -77,19 +79,21 @@
     masked = (
         ci_rows.reshape(span, jb_all // block_size, block_size) * mask_rows[:, :, None]
     ).reshape(span, jb_all)
-    masked_all_t = lax.all_gather(masked.T, COL, axis=1, tiled=True)
+    masked_all = lax.all_gather(masked, COL, axis=0, tiled=True)
 
     groups = lax.axis_size((X, C, Y))
-    pieces = amps.reshape(sub, groups, amps.shape[1] // groups)
+    block = amps.shape[1] // groups
     sums = []
     start = 0
-    for width in chunk_widths(pieces.shape[2]):
-        piece = jnp.transpose(pieces[:, :, start:start + width], (1, 0, 2))
+    for width in chunk_widths(block):
+        piece = jnp.stack(
+            [amps[:, g * block + start:g * block + start + width] for g in range(groups)]
+        )
         start += width
         plane_amps = lax.all_to_all(piece, (X, C, Y), split_axis=0, concat_axis=0, tiled=True)
-        partial_value = product(masked_all_t, plane_amps.reshape(groups * sub, width))
-        sums.append(lax.psum_scatter(partial_value, Z, scatter_dimension=0, tiled=True))
-    cycle_sum = jnp.concatenate(sums, axis=1).T
+        partial_value = product(plane_amps.reshape(groups * sub, width), masked_all)
+        sums.append(lax.psum_scatter(partial_value, Z, scatter_dimension=1, tiled=True))
+    cycle_sum = jnp.concatenate(sums, axis=0)
 
     perm = swap_perm(nz, ncol)
     coulomb_here = lax.ppermute(coulomb, (Z, X, C), perm)

time: 264 us -> 260 us (0.985)
  blocking collectives: 52.3 us -> 124 us
  waiting for transfers between devices: 111 us -> 54.7 us
  local copies, waits for them, and re-layouts: 42.8 us -> 27.5 us
  starting transfers between devices: 22.1 us -> 14.1 us
  other arithmetic: 2.87 us -> 6.46 us
    all_to_all x1 -> x2, blocking collectives: 52.3 us -> 124 us  [local(): lax.all_to_all(piece, (X, C, Y), split_axis=0, concat_axis=0, tiled=True)]
    all_gather x1, waiting for transfers between devices: 54.3 us -> 0.01 us  [local(): masked_all = lax.all_gather(masked, COL, axis=0, tiled=True)]
    unnamed x16 -> x49, local copies, waits for them, and re-layouts: 9.21 us -> 23.1 us
    reshape x1 -> x0, local copies, waits for them, and re-layouts: 12.5 us -> none  [local(): pieces = amps.reshape(sub, groups, amps.shape[1] // groups)]
    all_gather x1 -> x0, local copies, waits for them, and re-layouts: 10.5 us -> none  [local(): masked_all_t = lax.all_gather(masked.T, COL, axis=1, tiled=True)]
    all_to_all x1 -> x0, starting transfers between devices: 8.16 us -> none  [local(): lax.all_to_all(piece, (X, C, Y), split_axis=0, concat_axis=0, tiled=True)]
    slice x1 -> x0, local copies, waits for them, and re-layouts: 6.56 us -> none  [local(): piece = jnp.transpose(pieces[:, :, start:start + width], (1, 0, 2))]
    mul x0 -> x2, local copies, waits for them, and re-layouts: none -> 3.6 us  [local(): ci_rows.reshape(span, jb_all // block_size, block_size)]
  transfers between devices with their start and end apart: 6 -> 5, of which waited for: 4 -> 3; matrix products, arithmetic and copies ran while one was open for 15% -> 9% of each run, Pallas kernels for 3% -> 4%
where the time goes in v4:
time: 260 us; the launch traced here: 259 us
  blocking collectives  124 us (48%)
  waiting for transfers between devices  54.7 us (21%)
  local copies, waits for them, and re-layouts  27.5 us (11%)
  Pallas kernels  18.3 us (7%)
  starting transfers between devices  14.1 us (5%)
  between operations  13.5 us (5%)
  other arithmetic  6.46 us (2%)
    all_to_all x2, blocking collectives, local(): lax.all_to_all(piece, (X, C, Y), split_axis=0, concat_axis=0, tiled=True)  124 us
    unnamed x49, local copies, waits for them, and re-layouts  23.1 us
    ppermute x1, waiting for transfers between devices, local(): coulomb_here = lax.ppermute(coulomb, (Z, X, C), perm)  19.3 us
    reduce_scatter x2, waiting for transfers between devices, local(): lax.psum_scatter(partial_value, Z, scatter_dimension=1, tiled=True)  18.5 us
    pallas_call x2, Pallas kernels, product(): pl.pallas_call(product_kernel, out_shape=jax.ShapeDtypeStruct((rows, widt...  18.3 us
    ppermute x1, waiting for transfers between devices, local(): return lax.ppermute(out, (Z, X, C), perm)  16.9 us
    ppermute x1, starting transfers between devices, local(): coulomb_here = lax.ppermute(coulomb, (Z, X, C), perm)  7.13 us
    ppermute x1, starting transfers between devices, local(): return lax.ppermute(out, (Z, X, C), perm)  6.93 us
  transfers between devices with their start and end apart: 5, of which 3 were waited for; matrix products, arithmetic and copies ran while one was open for 9% of the time, Pallas kernels for 4%

profile of v4, /device:TPU:7, one launch (start us, length us, event | category | flops | bytes accessed | tf_op | source)
XLA Modules:
  0.0 258.8 jit_solution(8351240258755139610)
XLA Ops:
  6.5 0.7 convert_element_type.10
  7.2 0.2 broadcast_in_dim.140
  7.4 0.3 reshape.123
  7.7 0.1 constant_dynamic-slice_fusion
  7.8 1.1 mul.41
  8.9 2.5 copy.12
  11.4 2.8 %dynamic-slice_multiply_fusion = bf16[480,1024]{1,0:T(8,128)(2,1)} fusion(bf16[480,1024]{1,0:T(8,128)(2,1)} %copy.12, bf16[3840,1024]{1,0:T(8,128)(2,1)} %param.9, s32[]{:T(128)S(6)} %select_n.113), kind=kLoop, calls=%fused_computation.1 | loop fusion | flops 1966080 | bytes 2949124 | tf_op jit(solution)/shard_map/mul | solution.py:80
  14.2 0.0 all-gather.2.cloned.1.call-update
  14.3 0.0 reduce-scatter.5.cloned.1.call-start
  14.3 0.9 constant_dynamic-update-slice_fusion.31
  15.2 1.2 constant_dynamic-update-slice_fusion.30
  16.4 1.2 constant_dynamic-update-slice_fusion.29
  17.6 1.1 constant_dynamic-update-slice_fusion.28
  18.8 1.1 constant_dynamic-update-slice_fusion.27
  19.9 1.1 constant_dynamic-update-slice_fusion.26
  21.0 1.1 constant_dynamic-update-slice_fusion.25
  22.1 1.1 constant_dynamic-update-slice_fusion.24
  23.2 1.1 constant_dynamic-update-slice_fusion.23
  24.3 1.1 constant_dynamic-update-slice_fusion.22
  25.4 1.1 constant_dynamic-update-slice_fusion.21
  26.5 1.1 constant_dynamic-update-slice_fusion.20
  27.6 1.1 constant_dynamic-update-slice_fusion.19
  28.7 1.2 constant_dynamic-update-slice_fusion.18
  29.9 1.1 constant_dynamic-update-slice_fusion.17
  31.0 1.2 constant_dynamic-update-slice_fusion.16
  32.2 1.1 constant_dynamic-update-slice_fusion.15
  33.3 0.1 constant_dynamic-update-slice_fusion.14
  33.5 0.1 constant_dynamic-update-slice_fusion.13
  33.6 0.1 constant_dynamic-update-slice_fusion.12
  33.7 0.1 constant_dynamic-update-slice_fusion.11
  33.8 0.1 constant_dynamic-update-slice_fusion.10
  34.0 0.1 constant_dynamic-update-slice_fusion.9
  34.1 0.1 constant_dynamic-update-slice_fusion.8
  34.2 0.1 constant_dynamic-update-slice_fusion.7
  34.3 0.1 constant_dynamic-update-slice_fusion.6
  34.5 0.1 constant_dynamic-update-slice_fusion.5
  34.6 0.1 constant_dynamic-update-slice_fusion.4
  34.7 0.1 constant_dynamic-update-slice_fusion.3
  34.8 0.1 constant_dynamic-update-slice_fusion.2
  35.0 0.1 constant_dynamic-update-slice_fusion.1
  35.1 0.1 constant_dynamic-update-slice_fusion
  35.2 0.1 constant_dynamic-update-slice_fusion.33
  35.3 0.1 constant_dynamic-update-slice_fusion.32
  35.5 1.7 copy-done
  37.2 71.1 %all_to_all.10 = bf16[32,120,480]{2,1,0:T(8,128)(2,1)} all-to-all(bf16[32,120,480]{2,1,0:T(8,128)(2,1)S(1)} %constant_dynamic-update-slice_fusion.32), channel_id=1, replica_groups=mesh['z'=8,'y'=4,'x'=4,'core'=2] {'x','core','y'}, dimensions={0} | all-to-all | bytes 7372800 | tf_op jit(solution)/shard_map/all_to_all | solution.py:93
  108.2 9.1 %shard_map.83 = f32[480,1024]{1,0:T(8,128)} custom-call(bf16[3840,480]{1,0:T(8,128)(2,1)} %bitcast.136, bf16[3840,1024]{1,0:T(8,128)(2,1)} %all-gather.2.cloned.1.call-done.right_ref), custom_call_target="tpu_custom_call" | custom-call | flops 3774873600 | bytes 13516800 | tf_op jit(solution)/shard_map/pallas_call | solution.py:35
  117.4 0.0 reduce-scatter.3.cloned.1.call-start
  117.5 53.1 %all_to_all.11 = bf16[32,120,480]{2,1,0:T(8,128)(2,1)} all-to-all(bf16[32,120,480]{2,1,0:T(8,128)(2,1)} %copy-done), channel_id=1, replica_groups=mesh['z'=8,'y'=4,'x'=4,'core'=2] {'x','core','y'}, dimensions={0} | all-to-all | bytes 7372800 | tf_op jit(solution)/shard_map/all_to_all | solution.py:93
  170.5 9.1 %shard_map.82 = f32[480,1024]{1,0:T(8,128)} custom-call(bf16[3840,480]{1,0:T(8,128)(2,1)} %bitcast.137, bf16[3840,1024]{1,0:T(8,128)(2,1)} %all-gather.2.cloned.1.call-done.right_ref), custom_call_target="tpu_custom_call" | custom-call | flops 3774873600 | bytes 13516800 | tf_op jit(solution)/shard_map/pallas_call | solution.py:35
  179.7 7.1 %collective-permute-start = (bf16[960,128]{1,0:T(8,128)(2,1)S(1)}, bf16[960,128]{1,0:T(8,128)(2,1)S(1)}, u32[]{:S(2)}, u32[]{:S(2)}) collective-permute-start(bf16[960,128]{1,0:T(8,128)(2,1)S(1)} %copy-done.5), channel_id=1, source_target_pairs={{0,0},{1,32},{2,64},{3,96},{4,128},{5,160},{6,192},{7,224},{32,1},... | collective-permute-start | bytes 737288 | tf_op jit(solution)/shard_map/ppermute | solution.py:99
  186.9 0.1 select_reduce_fusion.4
  187.0 0.2 select_reduce_fusion.2
  187.2 0.2 select_reduce_fusion.3
  187.4 0.4 select_reduce_fusion
  187.8 0.4 select_reduce_fusion.1
  188.2 0.1 select_reduce_fusion.6
  188.3 0.1 select_reduce_fusion.7
  188.4 0.1 select_reduce_fusion.5
  188.5 19.3 %collective-permute-done = bf16[960,128]{1,0:T(8,128)(2,1)S(1)} collective-permute-done((bf16[960,128]{1,0:T(8,128)(2,1)S(1)}, bf16[960,128]{1,0:T(8,128)(2,1)S(1)}, u32[]{:S(2)}, u32[]{:S(2)}) %collective-permute-start) | collective-permute-done | bytes 245792 | tf_op jit(solution)/shard_map/ppermute | solution.py:99
  207.8 18.5 %reduce-scatter.3.cloned.1.call-done = f32[480,128]{1,0:T(8,128)} async-done(((f32[480,1024]{1,0:T(8,128)}), f32[480,128]{1,0:T(8,128)}) %reduce-scatter.3.cloned.1.call-update) | async-done | bytes 245776 | tf_op jit(solution)/shard_map/reduce_scatter | solution.py:95
  226.3 1.4 fusion.2
  227.7 6.9 %collective-permute-start.1 = (bf16[960,128]{1,0:T(8,128)(2,1)S(1)}, bf16[960,128]{1,0:T(8,128)(2,1)S(1)}, u32[]{:S(2)}, u32[]{:S(2)}) collective-permute-start(bf16[960,128]{1,0:T(8,128)(2,1)S(1)} %fusion.2), channel_id=1, source_target_pairs={{0,0},{1,32},{2,64},{3,96},{4,128},{5,160},{6,192},{7,224},{32,1},... | collective-permute-start | bytes 737288 | tf_op jit(solution)/shard_map/ppermute | solution.py:115
  234.7 16.9 %collective-permute-done.1 = bf16[960,128]{1,0:T(8,128)(2,1)S(1)} collective-permute-done((bf16[960,128]{1,0:T(8,128)(2,1)S(1)}, bf16[960,128]{1,0:T(8,128)(2,1)S(1)}, u32[]{:S(2)}, u32[]{:S(2)}) %collective-permute-start.1) | collective-permute-done | bytes 245792 | tf_op jit(solution)/shard_map/ppermute | solution.py:115
  251.5 0.7 copy.76
  (27 shorter events, 0.1 us)
Async XLA Ops:
  6.5 101.7 %all-gather.2.cloned.1.call-start = ((), (), s32[]{:S(2)}) async-start(), calls=%async_computation.4 | async-start | bytes 8847360 | tf_op jit(solution)/shard_map/all_gather | solution.py:82
  7.8 25.5 %slice-start = ((s8[7372800]{0:T(1024)(128)(4,1)}), s8[3178496]{0:T(1024)(128)(4,1)S(1)}, s32[]{:S(2)}) async-start(s8[7372800]{0:T(1024)(128)(4,1)} %bitcast.133), calls=%async_computation.7 | async-start | bytes 6356992
  14.3 193.6 %reduce-scatter.5.cloned.1.call-start = ((), (), s32[]{:S(2)}) async-start(), calls=%async_computation.6 | async-start | bytes 2211840 | tf_op jit(solution)/shard_map/reduce_scatter | solution.py:95
  15.2 18.1 %slice-start.1 = ((s8[7372800]{0:T(1024)(128)(4,1)}), s8[4194304]{0:T(1024)(128)(4,1)S(1)}, s32[]{:S(2)}) async-start(s8[7372800]{0:T(1024)(128)(4,1)} %bitcast.133), calls=%async_computation.8 | async-start | bytes 8388608
  35.2 1.9 copy-start
  117.4 108.9 %reduce-scatter.3.cloned.1.call-start = ((), (), s32[]{:S(2)}) async-start(), calls=%async_computation.5 | async-start | bytes 2211840 | tf_op jit(solution)/shard_map/reduce_scatter | solution.py:95
  170.5 9.2 %copy-start.5 = (bf16[960,128]{1,0:T(8,128)(2,1)S(1)}, bf16[960,128]{1,0:T(8,128)(2,1)}, u32[]{:S(2)}) copy-start(bf16[960,128]{1,0:T(8,128)(2,1)} %param.11) | copy-start | bytes 737284
  170.5 16.4 %copy-start.1 = (f32[240]{0:T(256)S(1)}, f32[240]{0:T(256)}, u32[]{:S(2)}) copy-start(f32[240]{0:T(256)} %param.14) | copy-start | bytes 2884
  170.5 16.5 %copy-start.2 = (f32[192]{0:T(256)S(1)}, f32[192]{0:T(256)}, u32[]{:S(2)}) copy-start(f32[192]{0:T(256)} %param.15) | copy-start | bytes 2308
  170.5 16.7 %copy-start.3 = (s32[192]{0:T(256)S(1)}, s32[192]{0:T(256)}, u32[]{:S(2)}) copy-start(s32[192]{0:T(256)} %param.13) | copy-start | bytes 2308
  170.5 17.3 %copy-start.4 = (s32[240]{0:T(256)S(1)}, s32[240]{0:T(256)}, u32[]{:S(2)}) copy-start(s32[240]{0:T(256)} %param.12) | copy-start | bytes 2884
  179.7 28.1 %collective-permute-start = (bf16[960,128]{1,0:T(8,128)(2,1)S(1)}, bf16[960,128]{1,0:T(8,128)(2,1)S(1)}, u32[]{:S(2)}, u32[]{:S(2)}) collective-permute-start(bf16[960,128]{1,0:T(8,128)(2,1)S(1)} %copy-done.5), channel_id=1, source_target_pairs={{0,0},{1,32},{2,64},{3,96},{4,128},{5,160},{6,192},{7,224},{32,1},... | collective-permute-start | bytes 737288 | tf_op jit(solution)/shard_map/ppermute | solution.py:99
  227.7 23.8 %collective-permute-start.1 = (bf16[960,128]{1,0:T(8,128)(2,1)S(1)}, bf16[960,128]{1,0:T(8,128)(2,1)S(1)}, u32[]{:S(2)}, u32[]{:S(2)}) collective-permute-start(bf16[960,128]{1,0:T(8,128)(2,1)S(1)} %fusion.2), channel_id=1, source_target_pairs={{0,0},{1,32},{2,64},{3,96},{4,128},{5,160},{6,192},{7,224},{32,1},... | collective-permute-start | bytes 737288 | tf_op jit(solution)/shard_map/ppermute | solution.py:115
Sparse Core Ops, SparseCore 0:
  14.4 86.8 all-gather.1
  117.5 37.4 reduce-scatter.4
  179.8 46.4 reduce-scatter.2

commit v5 on v4

--- a/solution.py
+++ b/solution.py
@@ -1,3 +1,5 @@
+import functools
+
 import jax
 import jax.numpy as jnp
 from jax import lax
@@ -49,6 +51,26 @@
     )(left, right)
 
 
+def stack_kernel(widths, block, in_ref, *out_refs):
+    for half in range(2):
+        start = half * block
+        for width, out_ref in zip(widths, out_refs):
+            out_ref[half] = in_ref[:, start:start + width]
+            start += width
+
+
+def stack_chunks(amps, groups, widths):
+    sub, total = amps.shape
+    block = total // groups
+    return pl.pallas_call(
+        functools.partial(stack_kernel, widths, block),
+        out_shape=[jax.ShapeDtypeStruct((groups, sub, width), amps.dtype) for width in widths],
+        grid=(groups // 2,),
+        in_specs=[pl.BlockSpec((sub, 2 * block), lambda h: (0, h))],
+        out_specs=[pl.BlockSpec((2, sub, width), lambda h: (h, 0, 0)) for width in widths],
+    )(amps)
+
+
 def chunk_widths(total):
     half = total // 2
     return [half, total - half]
@@ -83,13 +105,9 @@
 
     groups = lax.axis_size((X, C, Y))
     block = amps.shape[1] // groups
+    widths = chunk_widths(block)
     sums = []
-    start = 0
-    for width in chunk_widths(block):
-        piece = jnp.stack(
-            [amps[:, g * block + start:g * block + start + width] for g in range(groups)]
-        )
-        start += width
+    for piece, width in zip(stack_chunks(amps, groups, widths), widths):
         plane_amps = lax.all_to_all(piece, (X, C, Y), split_axis=0, concat_axis=0, tiled=True)
         partial_value = product(plane_amps.reshape(groups * sub, width), masked_all)
         sums.append(lax.psum_scatter(partial_value, Z, scatter_dimension=1, tiled=True))

time: 260 us -> 256 us (0.985)
  local copies, waits for them, and re-layouts: 27.5 us -> 1.88 us
  Pallas kernels: 18.3 us -> 30.9 us
  blocking collectives: 124 us -> 134 us
    unnamed x49 -> x11, local copies, waits for them, and re-layouts: 23.1 us -> 0.71 us
    pallas_call x0 -> x1, Pallas kernels: none -> 12.6 us  [stack_chunks(): pl.pallas_call(functools.partial(stack_kernel, widths, block), out_shape=...]
    all_to_all x2, blocking collectives: 124 us -> 134 us  [local(): lax.all_to_all(piece, (X, C, Y), split_axis=0, concat_axis=0, tiled=True)]
    mul x2, local copies, waits for them, and re-layouts: 3.6 us -> 0.61 us  [local(): ci_rows.reshape(span, jb_all // block_size, block_size)]
  transfers between devices with their start and end apart: 5 -> 5, of which waited for: 3 -> 3; matrix products, arithmetic and copies ran while one was open for 9% -> 1% of each run, Pallas kernels for 4% -> 9%
where the time goes in v5:
time: 256 us; the launch traced here: 255 us
  blocking collectives  134 us (52%)
  waiting for transfers between devices  54.7 us (21%)
  Pallas kernels  30.9 us (12%)
  starting transfers between devices  14.1 us (6%)
  between operations  13.3 us (5%)
  other arithmetic  6.17 us (2%)
    all_to_all x2, blocking collectives, local(): lax.all_to_all(piece, (X, C, Y), split_axis=0, concat_axis=0, tiled=True)  134 us
    ppermute x1, waiting for transfers between devices, local(): coulomb_here = lax.ppermute(coulomb, (Z, X, C), perm)  19.3 us
    reduce_scatter x2, waiting for transfers between devices, local(): lax.psum_scatter(partial_value, Z, scatter_dimension=1, tiled=True)  18.5 us
    pallas_call x2, Pallas kernels, product(): pl.pallas_call(product_kernel, out_shape=jax.ShapeDtypeStruct((rows, widt...  18.2 us
    ppermute x1, waiting for transfers between devices, local(): return lax.ppermute(out, (Z, X, C), perm)  16.9 us
    pallas_call x1, Pallas kernels, stack_chunks(): pl.pallas_call(functools.partial(stack_kernel, widths, block), out_shape=...  12.6 us
    ppermute x1, starting transfers between devices, local(): coulomb_here = lax.ppermute(coulomb, (Z, X, C), perm)  7.13 us
    ppermute x1, starting transfers between devices, local(): return lax.ppermute(out, (Z, X, C), perm)  6.93 us
  transfers between devices with their start and end apart: 5, of which 3 were waited for; matrix products, arithmetic and copies ran while one was open for 1% of the time, Pallas kernels for 9%

profile of v5, /device:TPU:7, one launch (start us, length us, event | category | flops | bytes accessed | tf_op | source)
XLA Modules:
  0.0 255.3 jit_solution(9342766178306248274)
XLA Ops:
  6.5 0.0 all-gather.2.cloned.1.call-start
  6.5 0.7 convert_element_type.10
  7.2 0.2 broadcast_in_dim.140
  7.4 0.3 reshape.123
  7.7 0.1 constant_dynamic-slice_fusion
  7.8 0.1 mul.41
  7.9 0.5 copy.12
  8.4 2.5 dynamic-slice_multiply_fusion
  11.0 0.0 all-gather.2.cloned.1.call-update
  11.0 0.0 reduce-scatter.5.cloned.1.call-start
  11.0 12.6 %shard_map.82 = (bf16[32,120,480]{2,1,0:T(8,128)(2,1)}, bf16[32,120,480]{2,1,0:T(8,128)(2,1)}) custom-call(bf16[120,30720]{1,0:T(8,128)(2,1)} %in_ref.1), custom_call_target="tpu_custom_call" | custom-call | tf_op jit(solution)/shard_map/pallas_call | solution.py:65
  23.7 81.3 %all_to_all.10 = bf16[32,120,480]{2,1,0:T(8,128)(2,1)} all-to-all(bf16[32,120,480]{2,1,0:T(8,128)(2,1)} %get-tuple-element.8), channel_id=1, replica_groups=mesh['z'=8,'y'=4,'x'=4,'core'=2] {'x','core','y'}, dimensions={0} | all-to-all | bytes 7372800 | tf_op jit(solution)/shard_map/all_to_all | solution.py:111
  105.0 0.0 all-gather.2.cloned.1.call-done.right_ref
  105.0 9.1 %shard_map.84 = f32[480,1024]{1,0:T(8,128)} custom-call(bf16[3840,480]{1,0:T(8,128)(2,1)} %bitcast.6, bf16[3840,1024]{1,0:T(8,128)(2,1)} %all-gather.2.cloned.1.call-done.right_ref), custom_call_target="tpu_custom_call" | custom-call | flops 3774873600 | bytes 13516800 | tf_op jit(solution)/shard_map/pallas_call | solution.py:37
  114.1 0.0 reduce-scatter.5.cloned.1.call-update
  114.1 0.0 reduce-scatter.3.cloned.1.call-start
  114.2 52.9 %all_to_all.11 = bf16[32,120,480]{2,1,0:T(8,128)(2,1)} all-to-all(bf16[32,120,480]{2,1,0:T(8,128)(2,1)} %get-tuple-element.7), channel_id=1, replica_groups=mesh['z'=8,'y'=4,'x'=4,'core'=2] {'x','core','y'}, dimensions={0} | all-to-all | bytes 7372800 | tf_op jit(solution)/shard_map/all_to_all | solution.py:111
  167.1 0.0 copy-start.4
  167.1 0.0 copy-start
  167.1 0.0 copy-start.1
  167.1 0.0 copy-start.2
  167.1 0.0 copy-start.3
  167.1 9.1 %shard_map.83 = f32[480,1024]{1,0:T(8,128)} custom-call(bf16[3840,480]{1,0:T(8,128)(2,1)} %bitcast.7, bf16[3840,1024]{1,0:T(8,128)(2,1)} %all-gather.2.cloned.1.call-done.right_ref), custom_call_target="tpu_custom_call" | custom-call | flops 3774873600 | bytes 13516800 | tf_op jit(solution)/shard_map/pallas_call | solution.py:37
  176.2 0.0 reduce-scatter.3.cloned.1.call-update
  176.2 0.0 copy-done.4
  176.3 7.1 %collective-permute-start = (bf16[960,128]{1,0:T(8,128)(2,1)S(1)}, bf16[960,128]{1,0:T(8,128)(2,1)S(1)}, u32[]{:S(2)}, u32[]{:S(2)}) collective-permute-start(bf16[960,128]{1,0:T(8,128)(2,1)S(1)} %copy-done.4), channel_id=1, source_target_pairs={{0,0},{1,32},{2,64},{3,96},{4,128},{5,160},{6,192},{7,224},{32,1},... | collective-permute-start | bytes 737288 | tf_op jit(solution)/shard_map/ppermute | solution.py:117
  183.4 0.0 copy-done
  183.4 0.1 select_reduce_fusion.6
  183.5 0.0 copy-done.1
  183.6 0.1 select_reduce_fusion.4
  183.7 0.2 select_reduce_fusion.2
  183.9 0.4 select_reduce_fusion
  184.3 0.0 copy-done.2
  184.3 0.1 select_reduce_fusion.7
  184.4 0.0 copy-done.3
  184.4 0.1 select_reduce_fusion.5
  184.5 0.2 select_reduce_fusion.3
  184.7 0.4 select_reduce_fusion.1
  185.1 19.3 %collective-permute-done = bf16[960,128]{1,0:T(8,128)(2,1)S(1)} collective-permute-done((bf16[960,128]{1,0:T(8,128)(2,1)S(1)}, bf16[960,128]{1,0:T(8,128)(2,1)S(1)}, u32[]{:S(2)}, u32[]{:S(2)}) %collective-permute-start) | collective-permute-done | bytes 245792 | tf_op jit(solution)/shard_map/ppermute | solution.py:117
  204.4 0.0 reduce-scatter.5.cloned.1.call-done
  204.4 18.5 %reduce-scatter.3.cloned.1.call-done = f32[480,128]{1,0:T(8,128)} async-done(((f32[480,1024]{1,0:T(8,128)}), f32[480,128]{1,0:T(8,128)}) %reduce-scatter.3.cloned.1.call-update) | async-done | bytes 245776 | tf_op jit(solution)/shard_map/reduce_scatter | solution.py:113
  222.9 1.4 fusion.2
  224.3 6.9 %collective-permute-start.1 = (bf16[960,128]{1,0:T(8,128)(2,1)S(1)}, bf16[960,128]{1,0:T(8,128)(2,1)S(1)}, u32[]{:S(2)}, u32[]{:S(2)}) collective-permute-start(bf16[960,128]{1,0:T(8,128)(2,1)S(1)} %fusion.2), channel_id=1, source_target_pairs={{0,0},{1,32},{2,64},{3,96},{4,128},{5,160},{6,192},{7,224},{32,1},... | collective-permute-start | bytes 737288 | tf_op jit(solution)/shard_map/ppermute | solution.py:133
  231.2 16.9 %collective-permute-done.1 = bf16[960,128]{1,0:T(8,128)(2,1)S(1)} collective-permute-done((bf16[960,128]{1,0:T(8,128)(2,1)S(1)}, bf16[960,128]{1,0:T(8,128)(2,1)S(1)}, u32[]{:S(2)}, u32[]{:S(2)}) %collective-permute-start.1) | collective-permute-done | bytes 245792 | tf_op jit(solution)/shard_map/ppermute | solution.py:133
  248.1 0.7 copy.14
  (6 shorter events, 0.1 us)
Async XLA Ops:
  6.5 98.4 %all-gather.2.cloned.1.call-start = ((), (), s32[]{:S(2)}) async-start(), calls=%async_computation.4 | async-start | bytes 8847360 | tf_op jit(solution)/shard_map/all_gather | solution.py:104
  11.0 193.4 %reduce-scatter.5.cloned.1.call-start = ((), (), s32[]{:S(2)}) async-start(), calls=%async_computation.6 | async-start | bytes 2211840 | tf_op jit(solution)/shard_map/reduce_scatter | solution.py:113
  114.1 108.8 %reduce-scatter.3.cloned.1.call-start = ((), (), s32[]{:S(2)}) async-start(), calls=%async_computation.5 | async-start | bytes 2211840 | tf_op jit(solution)/shard_map/reduce_scatter | solution.py:113
  167.1 9.2 %copy-start.4 = (bf16[960,128]{1,0:T(8,128)(2,1)S(1)}, bf16[960,128]{1,0:T(8,128)(2,1)}, u32[]{:S(2)}) copy-start(bf16[960,128]{1,0:T(8,128)(2,1)} %param.11) | copy-start | bytes 737284
  167.1 16.4 %copy-start = (f32[192]{0:T(256)S(1)}, f32[192]{0:T(256)}, u32[]{:S(2)}) copy-start(f32[192]{0:T(256)} %param.15) | copy-start | bytes 2308
  167.1 16.5 %copy-start.1 = (f32[240]{0:T(256)S(1)}, f32[240]{0:T(256)}, u32[]{:S(2)}) copy-start(f32[240]{0:T(256)} %param.14) | copy-start | bytes 2884
  167.1 17.2 %copy-start.2 = (s32[192]{0:T(256)S(1)}, s32[192]{0:T(256)}, u32[]{:S(2)}) copy-start(s32[192]{0:T(256)} %param.13) | copy-start | bytes 2308
  167.1 17.3 %copy-start.3 = (s32[240]{0:T(256)S(1)}, s32[240]{0:T(256)}, u32[]{:S(2)}) copy-start(s32[240]{0:T(256)} %param.12) | copy-start | bytes 2884
  176.3 28.1 %collective-permute-start = (bf16[960,128]{1,0:T(8,128)(2,1)S(1)}, bf16[960,128]{1,0:T(8,128)(2,1)S(1)}, u32[]{:S(2)}, u32[]{:S(2)}) collective-permute-start(bf16[960,128]{1,0:T(8,128)(2,1)S(1)} %copy-done.4), channel_id=1, source_target_pairs={{0,0},{1,32},{2,64},{3,96},{4,128},{5,160},{6,192},{7,224},{32,1},... | collective-permute-start | bytes 737288 | tf_op jit(solution)/shard_map/ppermute | solution.py:117
  224.3 23.8 %collective-permute-start.1 = (bf16[960,128]{1,0:T(8,128)(2,1)S(1)}, bf16[960,128]{1,0:T(8,128)(2,1)S(1)}, u32[]{:S(2)}, u32[]{:S(2)}) collective-permute-start(bf16[960,128]{1,0:T(8,128)(2,1)S(1)} %fusion.2), channel_id=1, source_target_pairs={{0,0},{1,32},{2,64},{3,96},{4,128},{5,160},{6,192},{7,224},{32,1},... | collective-permute-start | bytes 737288 | tf_op jit(solution)/shard_map/ppermute | solution.py:133
Sparse Core Ops, SparseCore 0:
  11.1 91.6 all-gather.1
  114.2 37.4 reduce-scatter.4
  176.4 46.4 reduce-scatter.2

commit v6 on v5

--- a/solution.py
+++ b/solution.py
@@ -76,8 +76,16 @@
     return [half, total - half]
 
 
-def swap_perm(nz, nc):
-    return [(z * nc + c, c * nz + z) for z in range(nz) for c in range(nc)]
+def owner_perm(nz, nx, ncore, to_owner):
+    pairs = []
+    for z in range(nz):
+        for x in range(nx):
+            for core in range(ncore):
+                row_major = core * nx + x
+                src = z * nx * ncore + x * ncore + core
+                dst = row_major * nx * ncore + (z // ncore) * ncore + z % ncore
+                pairs.append((src, dst) if to_owner else (dst, src))
+    return pairs
 
 
 def local(amps, cycle_int, tile_mask, coulomb, occ_irrep, vir_irrep, occ_energy, vir_energy):
@@ -101,21 +109,23 @@
     masked = (
         ci_rows.reshape(span, jb_all // block_size, block_size) * mask_rows[:, :, None]
     ).reshape(span, jb_all)
-    masked_all = lax.all_gather(masked, COL, axis=0, tiled=True)
+    masked_all = lax.all_gather(masked, X, axis=0, tiled=True)
+    masked_all = lax.all_gather(masked_all, C, axis=0, tiled=True)
 
-    groups = lax.axis_size((X, C, Y))
+    groups = lax.axis_size((C, X, Y))
     block = amps.shape[1] // groups
     widths = chunk_widths(block)
     sums = []
     for piece, width in zip(stack_chunks(amps, groups, widths), widths):
-        plane_amps = lax.all_to_all(piece, (X, C, Y), split_axis=0, concat_axis=0, tiled=True)
+        plane_amps = lax.all_to_all(piece, (C, X, Y), split_axis=0, concat_axis=0, tiled=True)
         partial_value = product(plane_amps.reshape(groups * sub, width), masked_all)
         sums.append(lax.psum_scatter(partial_value, Z, scatter_dimension=1, tiled=True))
     cycle_sum = jnp.concatenate(sums, axis=0)
 
-    perm = swap_perm(nz, ncol)
-    coulomb_here = lax.ppermute(coulomb, (Z, X, C), perm)
-    row_block = c * ny + y
+    nx = lax.axis_size(X)
+    ncore = lax.axis_size(C)
+    coulomb_here = lax.ppermute(coulomb, (Z, X, C), owner_perm(nz, nx, ncore, False))
+    row_block = (lax.axis_index(C) * nx + lax.axis_index(X)) * ny + y
     row_pos = row_block * rows_here + jnp.arange(rows_here, dtype=jnp.int32)
     col_pos = z * cols_here + jnp.arange(cols_here, dtype=jnp.int32)
     occ_row = row_pos // block_size % occupied
@@ -130,7 +140,7 @@
     denominator = gap_row[:, None] + gap_col[None, :]
     updated = (coulomb_here.astype(jnp.float32) + cycle_sum) / denominator
     out = jnp.where(allowed, updated, jnp.float32(0.0)).astype(jnp.bfloat16)
-    return lax.ppermute(out, (Z, X, C), perm)
+    return lax.ppermute(out, (Z, X, C), owner_perm(nz, nx, ncore, True))
 
 
 def solution(mesh):

time: 256 us -> 276 us (1.078); the launches traced: 255 us -> 271 us
  waiting for transfers between devices: 54.7 us -> 95.9 us
  blocking collectives: 134 us -> 108 us
    all_gather x1 -> x2, waiting for transfers between devices: 0.01 us -> 49.8 us  [the longest x1 49.8 us: local(): masked_all = lax.all_gather(masked, X, axis=0, tiled=True)]
    all_to_all x2, blocking collectives: 134 us -> 108 us  [local(): lax.all_to_all(piece, (C, X, Y), split_axis=0, concat_axis=0, tiled=True)]
    ppermute x2, waiting for transfers between devices: 36.2 us -> 27.6 us  [the longest x1 19.3 us: local(): lax.ppermute(coulomb, (Z, X, C), owner_perm(nz, nx, ncore, False))]
  transfers between devices with their start and end apart: 5 -> 6, of which waited for: 3 -> 4; matrix products, arithmetic and copies ran while one was open for 1% -> 1% of each run, Pallas kernels for 9% -> 8%
where the time goes in v6:
time: 276 us; the launch traced here: 271 us
  blocking collectives  108 us (39%)
  waiting for transfers between devices  95.9 us (35%)
  Pallas kernels  30.9 us (11%)
  starting transfers between devices  14.2 us (5%)
  between operations  13.3 us (5%)
  other arithmetic  6.16 us (2%)
    all_to_all x2, blocking collectives, local(): lax.all_to_all(piece, (C, X, Y), split_axis=0, concat_axis=0, tiled=True)  108 us
    all_gather x1, waiting for transfers between devices, local(): masked_all = lax.all_gather(masked, X, axis=0, tiled=True)  49.8 us
    ppermute x1, waiting for transfers between devices, local(): lax.ppermute(coulomb, (Z, X, C), owner_perm(nz, nx, ncore, False))  19.3 us
    reduce_scatter x2, waiting for transfers between devices, local(): lax.psum_scatter(partial_value, Z, scatter_dimension=1, tiled=True)  18.5 us
    pallas_call x2, Pallas kernels, product(): pl.pallas_call(product_kernel, out_shape=jax.ShapeDtypeStruct((rows, widt...  18.2 us
    pallas_call x1, Pallas kernels, stack_chunks(): pl.pallas_call(functools.partial(stack_kernel, widths, block), out_shape=...  12.7 us
    ppermute x1, waiting for transfers between devices, local(): return lax.ppermute(out, (Z, X, C), owner_perm(nz, nx, ncore, True))  8.26 us
    ppermute x1, starting transfers between devices, local(): return lax.ppermute(out, (Z, X, C), owner_perm(nz, nx, ncore, True))  7.28 us
  transfers between devices with their start and end apart: 6, of which 4 were waited for; matrix products, arithmetic and copies ran while one was open for 1% of the time, Pallas kernels for 8%

profile of v6, /device:TPU:7, one launch (start us, length us, event | category | flops | bytes accessed | tf_op | source)
XLA Modules:
  0.0 270.8 jit_solution(12142918067761891386)
XLA Ops:
  6.5 0.0 all-gather.3.cloned.1.call-start
  6.5 0.7 convert_element_type.10
  7.2 0.2 broadcast_in_dim.140
  7.4 0.3 reshape.123
  7.7 0.1 constant_dynamic-slice_fusion
  7.8 0.1 mul.41
  7.9 0.5 copy.12
  8.4 2.5 dynamic-slice_multiply_fusion
  11.0 0.0 all-gather.3.cloned.1.call-update
  11.0 0.0 all-gather.5.cloned.1.call-start
  11.0 49.8 %all-gather.3.cloned.1.call-done = bf16[1920,1024]{1,0:T(8,128)(2,1)} async-done(((bf16[480,1024]{1,0:T(8,128)(2,1)}), bf16[1920,1024]{1,0:T(8,128)(2,1)}) %all-gather.3.cloned.1.call-update) | async-done | bytes 3932176 | tf_op jit(solution)/shard_map/all_gather | solution.py:112
  60.8 0.0 all-gather.5.cloned.1.call-update
  60.8 0.0 reduce-scatter.5.cloned.1.call-start
  60.9 12.7 %shard_map.82 = (bf16[32,120,480]{2,1,0:T(8,128)(2,1)}, bf16[32,120,480]{2,1,0:T(8,128)(2,1)}) custom-call(bf16[120,30720]{1,0:T(8,128)(2,1)} %in_ref.1), custom_call_target="tpu_custom_call" | custom-call | tf_op jit(solution)/shard_map/pallas_call | solution.py:65
  73.5 55.2 %all_to_all.10 = bf16[32,120,480]{2,1,0:T(8,128)(2,1)} all-to-all(bf16[32,120,480]{2,1,0:T(8,128)(2,1)} %get-tuple-element.8), channel_id=1, replica_groups=mesh['z'=8,'y'=4,'x'=4,'core'=2] {'core','x','y'}, dimensions={0} | all-to-all | bytes 7372800 | tf_op jit(solution)/shard_map/all_to_all | solution.py:120
  128.8 0.0 all-gather.5.cloned.1.call-done.right_ref
  128.8 9.1 %shard_map.84 = f32[480,1024]{1,0:T(8,128)} custom-call(bf16[3840,480]{1,0:T(8,128)(2,1)} %bitcast.6, bf16[3840,1024]{1,0:T(8,128)(2,1)} %all-gather.5.cloned.1.call-done.right_ref), custom_call_target="tpu_custom_call" | custom-call | flops 3774873600 | bytes 13516800 | tf_op jit(solution)/shard_map/pallas_call | solution.py:37
  137.9 0.0 reduce-scatter.5.cloned.1.call-update
  137.9 0.0 reduce-scatter.3.cloned.1.call-start
  137.9 53.2 %all_to_all.11 = bf16[32,120,480]{2,1,0:T(8,128)(2,1)} all-to-all(bf16[32,120,480]{2,1,0:T(8,128)(2,1)} %get-tuple-element.7), channel_id=1, replica_groups=mesh['z'=8,'y'=4,'x'=4,'core'=2] {'core','x','y'}, dimensions={0} | all-to-all | bytes 7372800 | tf_op jit(solution)/shard_map/all_to_all | solution.py:120
  191.2 0.0 copy-start.4
  191.2 0.0 copy-start
  191.2 0.0 copy-start.1
  191.2 0.0 copy-start.2
  191.2 0.0 copy-start.3
  191.2 9.1 %shard_map.83 = f32[480,1024]{1,0:T(8,128)} custom-call(bf16[3840,480]{1,0:T(8,128)(2,1)} %bitcast.7, bf16[3840,1024]{1,0:T(8,128)(2,1)} %all-gather.5.cloned.1.call-done.right_ref), custom_call_target="tpu_custom_call" | custom-call | flops 3774873600 | bytes 13516800 | tf_op jit(solution)/shard_map/pallas_call | solution.py:37
  200.3 0.0 reduce-scatter.3.cloned.1.call-update
  200.3 0.0 copy-done.4
  200.3 6.8 %collective-permute-start = (bf16[960,128]{1,0:T(8,128)(2,1)S(1)}, bf16[960,128]{1,0:T(8,128)(2,1)S(1)}, u32[]{:S(2)}, u32[]{:S(2)}) collective-permute-start(bf16[960,128]{1,0:T(8,128)(2,1)S(1)} %copy-done.4), channel_id=1, source_target_pairs={{0,0},{128,1},{32,2},{160,3},{64,4},{192,5},{96,6},{224,7},{1,32},... | collective-permute-start | bytes 737288 | tf_op jit(solution)/shard_map/ppermute | solution.py:127
  207.2 0.0 copy-done
  207.2 0.1 select_reduce_fusion.6
  207.3 0.0 copy-done.1
  207.3 0.1 select_reduce_fusion.4
  207.5 0.2 select_reduce_fusion.2
  207.7 0.4 select_reduce_fusion
  208.0 0.0 copy-done.2
  208.1 0.1 select_reduce_fusion.7
  208.2 0.0 copy-done.3
  208.2 0.1 select_reduce_fusion.5
  208.3 0.2 select_reduce_fusion.3
  208.5 0.4 select_reduce_fusion.1
  208.8 19.3 %collective-permute-done = bf16[960,128]{1,0:T(8,128)(2,1)S(1)} collective-permute-done((bf16[960,128]{1,0:T(8,128)(2,1)S(1)}, bf16[960,128]{1,0:T(8,128)(2,1)S(1)}, u32[]{:S(2)}, u32[]{:S(2)}) %collective-permute-start) | collective-permute-done | bytes 245792 | tf_op jit(solution)/shard_map/ppermute | solution.py:127
  228.2 0.0 reduce-scatter.5.cloned.1.call-done
  228.2 18.5 %reduce-scatter.3.cloned.1.call-done = f32[480,128]{1,0:T(8,128)} async-done(((f32[480,1024]{1,0:T(8,128)}), f32[480,128]{1,0:T(8,128)}) %reduce-scatter.3.cloned.1.call-update) | async-done | bytes 245776 | tf_op jit(solution)/shard_map/reduce_scatter | solution.py:122
  246.6 1.4 fusion.2
  248.0 7.3 %collective-permute-start.1 = (bf16[960,128]{1,0:T(8,128)(2,1)S(1)}, bf16[960,128]{1,0:T(8,128)(2,1)S(1)}, u32[]{:S(2)}, u32[]{:S(2)}) collective-permute-start(bf16[960,128]{1,0:T(8,128)(2,1)S(1)} %fusion.2), channel_id=1, source_target_pairs={{0,0},{1,128},{2,32},{3,160},{4,64},{5,192},{6,96},{7,224},{32,1},... | collective-permute-start | bytes 737288 | tf_op jit(solution)/shard_map/ppermute | solution.py:143
  255.3 8.3 %collective-permute-done.1 = bf16[960,128]{1,0:T(8,128)(2,1)S(1)} collective-permute-done((bf16[960,128]{1,0:T(8,128)(2,1)S(1)}, bf16[960,128]{1,0:T(8,128)(2,1)S(1)}, u32[]{:S(2)}, u32[]{:S(2)}) %collective-permute-start.1) | collective-permute-done | bytes 245792 | tf_op jit(solution)/shard_map/ppermute | solution.py:143
  263.5 0.7 copy.14
  (6 shorter events, 0.1 us)
Async XLA Ops:
  6.5 54.3 %all-gather.3.cloned.1.call-start = ((), (), s32[]{:S(2)}) async-start(), calls=%async_computation.4 | async-start | bytes 4915200 | tf_op jit(solution)/shard_map/all_gather | solution.py:112
  11.0 117.8 %all-gather.5.cloned.1.call-start = ((), (), s32[]{:S(2)}) async-start(), calls=%async_computation.5 | async-start | bytes 11796480 | tf_op jit(solution)/shard_map/all_gather | solution.py:113
  60.8 167.3 %reduce-scatter.5.cloned.1.call-start = ((), (), s32[]{:S(2)}) async-start(), calls=%async_computation.7 | async-start | bytes 2211840 | tf_op jit(solution)/shard_map/reduce_scatter | solution.py:122
  137.9 108.7 %reduce-scatter.3.cloned.1.call-start = ((), (), s32[]{:S(2)}) async-start(), calls=%async_computation.6 | async-start | bytes 2211840 | tf_op jit(solution)/shard_map/reduce_scatter | solution.py:122
  191.2 9.2 %copy-start.4 = (bf16[960,128]{1,0:T(8,128)(2,1)S(1)}, bf16[960,128]{1,0:T(8,128)(2,1)}, u32[]{:S(2)}) copy-start(bf16[960,128]{1,0:T(8,128)(2,1)} %param.11) | copy-start | bytes 737284
  191.2 16.1 %copy-start = (f32[192]{0:T(256)S(1)}, f32[192]{0:T(256)}, u32[]{:S(2)}) copy-start(f32[192]{0:T(256)} %param.15) | copy-start | bytes 2308
  191.2 16.2 %copy-start.1 = (f32[240]{0:T(256)S(1)}, f32[240]{0:T(256)}, u32[]{:S(2)}) copy-start(f32[240]{0:T(256)} %param.14) | copy-start | bytes 2884
  191.2 16.9 %copy-start.2 = (s32[192]{0:T(256)S(1)}, s32[192]{0:T(256)}, u32[]{:S(2)}) copy-start(s32[192]{0:T(256)} %param.13) | copy-start | bytes 2308
  191.2 17.0 %copy-start.3 = (s32[240]{0:T(256)S(1)}, s32[240]{0:T(256)}, u32[]{:S(2)}) copy-start(s32[240]{0:T(256)} %param.12) | copy-start | bytes 2884
  200.3 27.8 %collective-permute-start = (bf16[960,128]{1,0:T(8,128)(2,1)S(1)}, bf16[960,128]{1,0:T(8,128)(2,1)S(1)}, u32[]{:S(2)}, u32[]{:S(2)}) collective-permute-start(bf16[960,128]{1,0:T(8,128)(2,1)S(1)} %copy-done.4), channel_id=1, source_target_pairs={{0,0},{128,1},{32,2},{160,3},{64,4},{192,5},{96,6},{224,7},{1,32},... | collective-permute-start | bytes 737288 | tf_op jit(solution)/shard_map/ppermute | solution.py:127
  248.0 15.5 %collective-permute-start.1 = (bf16[960,128]{1,0:T(8,128)(2,1)S(1)}, bf16[960,128]{1,0:T(8,128)(2,1)S(1)}, u32[]{:S(2)}, u32[]{:S(2)}) collective-permute-start(bf16[960,128]{1,0:T(8,128)(2,1)S(1)} %fusion.2), channel_id=1, source_target_pairs={{0,0},{1,128},{2,32},{3,160},{4,64},{5,192},{6,96},{7,224},{32,1},... | collective-permute-start | bytes 737288 | tf_op jit(solution)/shard_map/ppermute | solution.py:143
Sparse Core Ops, SparseCore 0:
  11.1 49.6 all-gather.2
  62.6 27.0 all-gather.4
  138.0 36.6 reduce-scatter.4
  200.5 46.1 reduce-scatter.2

commit v7 on v4

--- a/solution.py
+++ b/solution.py
@@ -1,3 +1,5 @@
+import functools
+
 import jax
 import jax.numpy as jnp
 from jax import lax
@@ -49,9 +51,26 @@
     )(left, right)
 
 
+def stack_kernel(start, width, block, in_ref, out_ref):
+    for half in range(2):
+        out_ref[half] = in_ref[:, half * block + start:half * block + start + width]
+
+
+def stack_chunk(amps, groups, start, width):
+    sub, total = amps.shape
+    block = total // groups
+    return pl.pallas_call(
+        functools.partial(stack_kernel, start, width, block),
+        out_shape=jax.ShapeDtypeStruct((groups, sub, width), amps.dtype),
+        grid=(groups // 2,),
+        in_specs=[pl.BlockSpec((sub, 2 * block), lambda h: (0, h))],
+        out_specs=pl.BlockSpec((2, sub, width), lambda h: (h, 0, 0)),
+    )(amps)
+
+
 def chunk_widths(total):
-    half = total // 2
-    return [half, total - half]
+    first = total * 5 // 8
+    return [first, total - first]
 
 
 def swap_perm(nz, nc):
@@ -86,9 +105,7 @@
     sums = []
     start = 0
     for width in chunk_widths(block):
-        piece = jnp.stack(
-            [amps[:, g * block + start:g * block + start + width] for g in range(groups)]
-        )
+        piece = stack_chunk(amps, groups, start, width)
         start += width
         plane_amps = lax.all_to_all(piece, (X, C, Y), split_axis=0, concat_axis=0, tiled=True)
         partial_value = product(plane_amps.reshape(groups * sub, width), masked_all)

time: 260 us -> 255 us (0.981)
  blocking collectives: 124 us -> 0 us
  waiting for transfers between devices: 54.7 us -> 160 us
  local copies, waits for them, and re-layouts: 27.5 us -> 3.47 us
  Pallas kernels: 18.3 us -> 41.1 us
  starting transfers between devices: 14.1 us -> 28.8 us
    all_to_all x2 -> x0, blocking collectives: 124 us -> none  [local(): lax.all_to_all(piece, (X, C, Y), split_axis=0, concat_axis=0, tiled=True)]
    all_to_all x0 -> x2, waiting for transfers between devices: none -> 102 us  [local(): lax.all_to_all(piece, (X, C, Y), split_axis=0, concat_axis=0, tiled=True)]
    pallas_call x0 -> x2, Pallas kernels: none -> 23 us  [stack_chunk(): pl.pallas_call(functools.partial(stack_kernel, start, width, block), out_...]
    unnamed x49 -> x13, local copies, waits for them, and re-layouts: 23.1 us -> 2.31 us
    all_to_all x0 -> x2, starting transfers between devices: none -> 15.4 us  [local(): lax.all_to_all(piece, (X, C, Y), split_axis=0, concat_axis=0, tiled=True)]
    mul x2, local copies, waits for them, and re-layouts: 3.6 us -> 0.61 us  [local(): ci_rows.reshape(span, jb_all // block_size, block_size)]
    reduce_scatter x2, waiting for transfers between devices: 18.5 us -> 21.4 us  [local(): lax.psum_scatter(partial_value, Z, scatter_dimension=1, tiled=True)]
  transfers between devices with their start and end apart: 5 -> 7, of which waited for: 3 -> 5; matrix products, arithmetic and copies ran while one was open for 9% -> 1% of each run, Pallas kernels for 4% -> 16%
where the time goes in v7:
time: 255 us; the launch traced here: 253 us
  waiting for transfers between devices  160 us (63%)
  Pallas kernels  41.1 us (16%)
  starting transfers between devices  28.8 us (11%)
  between operations  13.3 us (5%)
  other arithmetic  6.19 us (2%)
  local copies, waits for them, and re-layouts  3.47 us (1%)
    all_to_all x2, waiting for transfers between devices, local(): lax.all_to_all(piece, (X, C, Y), split_axis=0, concat_axis=0, tiled=True)  102 us
    pallas_call x2, Pallas kernels, stack_chunk(): pl.pallas_call(functools.partial(stack_kernel, start, width, block), out_...  23 us
    reduce_scatter x2, waiting for transfers between devices, local(): lax.psum_scatter(partial_value, Z, scatter_dimension=1, tiled=True)  21.4 us
    ppermute x1, waiting for transfers between devices, local(): coulomb_here = lax.ppermute(coulomb, (Z, X, C), perm)  19.1 us
    pallas_call x2, Pallas kernels, product(): pl.pallas_call(product_kernel, out_shape=jax.ShapeDtypeStruct((rows, widt...  18.2 us
    ppermute x1, waiting for transfers between devices, local(): return lax.ppermute(out, (Z, X, C), perm)  17.2 us
    all_to_all x2, starting transfers between devices, local(): lax.all_to_all(piece, (X, C, Y), split_axis=0, concat_axis=0, tiled=True)  15.4 us
    ppermute x1, starting transfers between devices, local(): coulomb_here = lax.ppermute(coulomb, (Z, X, C), perm)  6.69 us
  transfers between devices with their start and end apart: 7, of which 5 were waited for; matrix products, arithmetic and copies ran while one was open for 1% of the time, Pallas kernels for 16%

profile of v7, /device:TPU:7, one launch (start us, length us, event | category | flops | bytes accessed | tf_op | source)
XLA Modules:
  0.0 252.5 jit_solution(9929256380243643297)
XLA Ops:
  6.5 0.0 all-gather.2.cloned.1.call-start
  6.5 0.7 convert_element_type.10
  7.2 0.2 broadcast_in_dim.140
  7.4 0.3 reshape.123
  7.7 0.1 constant_dynamic-slice_fusion
  7.8 0.1 mul.41
  7.9 0.5 copy.12
  8.4 2.5 %dynamic-slice_multiply_fusion = bf16[480,1024]{1,0:T(8,128)(2,1)} fusion(bf16[480,1024]{1,0:T(8,128)(2,1)S(1)} %copy.12, bf16[3840,1024]{1,0:T(8,128)(2,1)} %param.9, s32[]{:T(128)S(6)} %select_n.113), kind=kLoop, calls=%fused_computation.1 | loop fusion | flops 1966080 | bytes 2949124 | tf_op jit(solution)/shard_map/mul | solution.py:99
  11.0 0.0 all-gather.2.cloned.1.call-update
  11.0 11.4 %shard_map.84 = bf16[32,120,360]{2,1,0:T(8,128)(2,1)} custom-call(bf16[120,30720]{1,0:T(8,128)(2,1)} %in_ref.3), custom_call_target="tpu_custom_call" | custom-call | tf_op jit(solution)/shard_map/pallas_call | solution.py:62
  22.4 7.9 %all-to-all-start.1 = ((bf16[32,120,360]{2,1,0:T(8,128)(2,1)}), bf16[32,120,360]{2,1,0:T(8,128)(2,1)S(1)}, u32[]{:S(2)}, u32[]{:S(2)}) async-start(bf16[32,120,360]{2,1,0:T(8,128)(2,1)} %shard_map.84), calls=%async_computation.2 | async-start | bytes 5898240 | tf_op jit(solution)/shard_map/all_to_all | solution.py:110
  30.3 11.6 %shard_map.82 = bf16[32,120,600]{2,1,0:T(8,128)(2,1)} custom-call(bf16[120,30720]{1,0:T(8,128)(2,1)} %in_ref.3), custom_call_target="tpu_custom_call" | custom-call | tf_op jit(solution)/shard_map/pallas_call | solution.py:62
  41.9 51.4 %all-to-all-done.1 = bf16[32,120,360]{2,1,0:T(8,128)(2,1)S(1)} async-done(((bf16[32,120,360]{2,1,0:T(8,128)(2,1)}), bf16[32,120,360]{2,1,0:T(8,128)(2,1)S(1)}, u32[]{:S(2)}, u32[]{:S(2)}) %all-to-all-start.1) | async-done | bytes 2764832 | tf_op jit(solution)/shard_map/all_to_all | solution.py:110
  93.3 0.0 copy-start
  93.3 1.6 copy-done
  94.9 7.4 %all-to-all-start = ((bf16[32,120,600]{2,1,0:T(8,128)(2,1)}), bf16[32,120,600]{2,1,0:T(8,128)(2,1)}, u32[]{:S(2)}, u32[]{:S(2)}) async-start(bf16[32,120,600]{2,1,0:T(8,128)(2,1)} %shard_map.82), calls=%async_computation | async-start | bytes 9830400 | tf_op jit(solution)/shard_map/all_to_all | solution.py:110
  102.4 0.0 reduce-scatter.5.cloned.1.call-start
  102.4 0.0 all-gather.2.cloned.1.call-done.right_ref
  102.4 8.0 %shard_map.85 = f32[360,1024]{1,0:T(8,128)} custom-call(bf16[3840,360]{1,0:T(8,128)(2,1)} %bitcast.5, bf16[3840,1024]{1,0:T(8,128)(2,1)} %all-gather.2.cloned.1.call-done.right_ref), custom_call_target="tpu_custom_call" | custom-call | flops 2831155200 | bytes 12103680 | tf_op jit(solution)/shard_map/pallas_call | solution.py:37
  110.4 0.0 reduce-scatter.5.cloned.1.call-update
  110.4 0.0 reduce-scatter.3.cloned.1.call-start
  110.5 50.4 %all-to-all-done = bf16[32,120,600]{2,1,0:T(8,128)(2,1)} async-done(((bf16[32,120,600]{2,1,0:T(8,128)(2,1)}), bf16[32,120,600]{2,1,0:T(8,128)(2,1)}, u32[]{:S(2)}, u32[]{:S(2)}) %all-to-all-start) | async-done | bytes 4608032 | tf_op jit(solution)/shard_map/all_to_all | solution.py:110
  160.9 0.0 copy-start.5
  160.9 0.0 copy-start.1
  160.9 0.0 copy-start.2
  160.9 0.0 copy-start.3
  160.9 0.0 copy-start.4
  160.9 10.2 %shard_map.83 = f32[600,1024]{1,0:T(8,128)} custom-call(bf16[3840,600]{1,0:T(8,128)(2,1)} %bitcast.left_ref, bf16[3840,1024]{1,0:T(8,128)(2,1)} %all-gather.2.cloned.1.call-done.right_ref), custom_call_target="tpu_custom_call" | custom-call | flops 4718592000 | bytes 14929920 | tf_op jit(solution)/shard_map/pallas_call | solution.py:37
  171.1 0.0 reduce-scatter.3.cloned.1.call-update
  171.2 0.0 copy-done.5
  171.2 6.7 %collective-permute-start = (bf16[960,128]{1,0:T(8,128)(2,1)S(1)}, bf16[960,128]{1,0:T(8,128)(2,1)S(1)}, u32[]{:S(2)}, u32[]{:S(2)}) collective-permute-start(bf16[960,128]{1,0:T(8,128)(2,1)S(1)} %copy-done.5), channel_id=1, source_target_pairs={{0,0},{1,32},{2,64},{3,96},{4,128},{5,160},{6,192},{7,224},{32,1},... | collective-permute-start | bytes 737288 | tf_op jit(solution)/shard_map/ppermute | solution.py:116
  177.9 0.0 copy-done.1
  177.9 0.1 select_reduce_fusion.4
  178.1 0.0 copy-done.2
  178.1 0.2 select_reduce_fusion.2
  178.2 0.0 copy-done.3
  178.3 0.2 select_reduce_fusion.3
  178.4 0.4 select_reduce_fusion
  178.8 0.0 copy-done.4
  178.8 0.4 select_reduce_fusion.1
  179.2 0.1 select_reduce_fusion.6
  179.3 0.1 select_reduce_fusion.7
  179.4 0.1 select_reduce_fusion.5
  179.5 19.1 %collective-permute-done = bf16[960,128]{1,0:T(8,128)(2,1)S(1)} collective-permute-done((bf16[960,128]{1,0:T(8,128)(2,1)S(1)}, bf16[960,128]{1,0:T(8,128)(2,1)S(1)}, u32[]{:S(2)}, u32[]{:S(2)}) %collective-permute-start) | collective-permute-done | bytes 245792 | tf_op jit(solution)/shard_map/ppermute | solution.py:116
  198.6 0.0 reduce-scatter.5.cloned.1.call-done
  198.6 21.4 %reduce-scatter.3.cloned.1.call-done = f32[600,128]{1,0:T(8,128)} async-done(((f32[600,1024]{1,0:T(8,128)}), f32[600,128]{1,0:T(8,128)}) %reduce-scatter.3.cloned.1.call-update) | async-done | bytes 307216 | tf_op jit(solution)/shard_map/reduce_scatter | solution.py:112
  220.0 1.4 fusion.2
  221.4 6.7 %collective-permute-start.1 = (bf16[960,128]{1,0:T(8,128)(2,1)S(1)}, bf16[960,128]{1,0:T(8,128)(2,1)S(1)}, u32[]{:S(2)}, u32[]{:S(2)}) collective-permute-start(bf16[960,128]{1,0:T(8,128)(2,1)S(1)} %fusion.2), channel_id=1, source_target_pairs={{0,0},{1,32},{2,64},{3,96},{4,128},{5,160},{6,192},{7,224},{32,1},... | collective-permute-start | bytes 737288 | tf_op jit(solution)/shard_map/ppermute | solution.py:132
  228.1 17.2 %collective-permute-done.1 = bf16[960,128]{1,0:T(8,128)(2,1)S(1)} collective-permute-done((bf16[960,128]{1,0:T(8,128)(2,1)S(1)}, bf16[960,128]{1,0:T(8,128)(2,1)S(1)}, u32[]{:S(2)}, u32[]{:S(2)}) %collective-permute-start.1) | collective-permute-done | bytes 245792 | tf_op jit(solution)/shard_map/ppermute | solution.py:132
  245.3 0.7 copy.14
  (6 shorter events, 0.1 us)
Async XLA Ops:
  6.5 95.9 %all-gather.2.cloned.1.call-start = ((), (), s32[]{:S(2)}) async-start(), calls=%async_computation.4 | async-start | bytes 8847360 | tf_op jit(solution)/shard_map/all_gather | solution.py:101
  22.4 71.0 %all-to-all-start.1 = ((bf16[32,120,360]{2,1,0:T(8,128)(2,1)}), bf16[32,120,360]{2,1,0:T(8,128)(2,1)S(1)}, u32[]{:S(2)}, u32[]{:S(2)}) async-start(bf16[32,120,360]{2,1,0:T(8,128)(2,1)} %shard_map.84), calls=%async_computation.2 | async-start | bytes 5898240 | tf_op jit(solution)/shard_map/all_to_all | solution.py:110
  93.3 1.6 copy-start
  94.9 66.0 %all-to-all-start = ((bf16[32,120,600]{2,1,0:T(8,128)(2,1)}), bf16[32,120,600]{2,1,0:T(8,128)(2,1)}, u32[]{:S(2)}, u32[]{:S(2)}) async-start(bf16[32,120,600]{2,1,0:T(8,128)(2,1)} %shard_map.82), calls=%async_computation | async-start | bytes 9830400 | tf_op jit(solution)/shard_map/all_to_all | solution.py:110
  102.4 96.3 %reduce-scatter.5.cloned.1.call-start = ((), (), s32[]{:S(2)}) async-start(), calls=%async_computation.6 | async-start | bytes 1658880 | tf_op jit(solution)/shard_map/reduce_scatter | solution.py:112
  110.4 109.6 %reduce-scatter.3.cloned.1.call-start = ((), (), s32[]{:S(2)}) async-start(), calls=%async_computation.5 | async-start | bytes 2764800 | tf_op jit(solution)/shard_map/reduce_scatter | solution.py:112
  160.9 10.3 %copy-start.5 = (bf16[960,128]{1,0:T(8,128)(2,1)S(1)}, bf16[960,128]{1,0:T(8,128)(2,1)}, u32[]{:S(2)}) copy-start(bf16[960,128]{1,0:T(8,128)(2,1)} %param.11) | copy-start | bytes 737284
  160.9 17.0 %copy-start.1 = (f32[240]{0:T(256)S(1)}, f32[240]{0:T(256)}, u32[]{:S(2)}) copy-start(f32[240]{0:T(256)} %param.14) | copy-start | bytes 2884
  160.9 17.1 %copy-start.2 = (f32[192]{0:T(256)S(1)}, f32[192]{0:T(256)}, u32[]{:S(2)}) copy-start(f32[192]{0:T(256)} %param.15) | copy-start | bytes 2308
  160.9 17.3 %copy-start.3 = (s32[192]{0:T(256)S(1)}, s32[192]{0:T(256)}, u32[]{:S(2)}) copy-start(s32[192]{0:T(256)} %param.13) | copy-start | bytes 2308
  160.9 17.9 %copy-start.4 = (s32[240]{0:T(256)S(1)}, s32[240]{0:T(256)}, u32[]{:S(2)}) copy-start(s32[240]{0:T(256)} %param.12) | copy-start | bytes 2884
  171.2 27.4 %collective-permute-start = (bf16[960,128]{1,0:T(8,128)(2,1)S(1)}, bf16[960,128]{1,0:T(8,128)(2,1)S(1)}, u32[]{:S(2)}, u32[]{:S(2)}) collective-permute-start(bf16[960,128]{1,0:T(8,128)(2,1)S(1)} %copy-done.5), channel_id=1, source_target_pairs={{0,0},{1,32},{2,64},{3,96},{4,128},{5,160},{6,192},{7,224},{32,1},... | collective-permute-start | bytes 737288 | tf_op jit(solution)/shard_map/ppermute | solution.py:116
  221.4 23.9 %collective-permute-start.1 = (bf16[960,128]{1,0:T(8,128)(2,1)S(1)}, bf16[960,128]{1,0:T(8,128)(2,1)S(1)}, u32[]{:S(2)}, u32[]{:S(2)}) collective-permute-start(bf16[960,128]{1,0:T(8,128)(2,1)S(1)} %fusion.2), channel_id=1, source_target_pairs={{0,0},{1,32},{2,64},{3,96},{4,128},{5,160},{6,192},{7,224},{32,1},... | collective-permute-start | bytes 737288 | tf_op jit(solution)/shard_map/ppermute | solution.py:132
Sparse Core Ops, SparseCore 0:
  11.1 80.2 all-gather.1
  110.5 37.4 reduce-scatter.4
  171.3 48.6 reduce-scatter.2

commit v8 on v7

--- a/solution.py
+++ b/solution.py
@@ -102,18 +102,20 @@
 
     groups = lax.axis_size((X, C, Y))
     block = amps.shape[1] // groups
+    perm = swap_perm(nz, ncol)
+    coulomb_here = lax.ppermute(coulomb, (Z, X, C), perm)
     sums = []
     start = 0
-    for width in chunk_widths(block):
+    for k, width in enumerate(chunk_widths(block)):
         piece = stack_chunk(amps, groups, start, width)
         start += width
+        if k == 1:
+            coulomb_here, piece = lax.optimization_barrier((coulomb_here, piece))
         plane_amps = lax.all_to_all(piece, (X, C, Y), split_axis=0, concat_axis=0, tiled=True)
         partial_value = product(plane_amps.reshape(groups * sub, width), masked_all)
         sums.append(lax.psum_scatter(partial_value, Z, scatter_dimension=1, tiled=True))
     cycle_sum = jnp.concatenate(sums, axis=0)
 
-    perm = swap_perm(nz, ncol)
-    coulomb_here = lax.ppermute(coulomb, (Z, X, C), perm)
     row_block = c * ny + y
     row_pos = row_block * rows_here + jnp.arange(rows_here, dtype=jnp.int32)
     col_pos = z * cols_here + jnp.arange(cols_here, dtype=jnp.int32)

time: 255 us -> 250 us (0.980)
  waiting for transfers between devices: 160 us -> 153 us
  starting transfers between devices: 28.8 us -> 31.7 us
    reduce_scatter x2, waiting for transfers between devices: 21.4 us -> 41.4 us  [local(): lax.psum_scatter(partial_value, Z, scatter_dimension=1, tiled=True)]
    ppermute x1, waiting for transfers between devices: 19.1 us -> 5.42 us  [local(): coulomb_here = lax.ppermute(coulomb, (Z, X, C), perm)]
    all_to_all x2, waiting for transfers between devices: 102 us -> 90 us  [local(): lax.all_to_all(piece, (X, C, Y), split_axis=0, concat_axis=0, tiled=True)]
  transfers between devices with their start and end apart: 7 -> 7, of which waited for: 5 -> 5; matrix products, arithmetic and copies ran while one was open for 1% -> 1% of each run, Pallas kernels for 16% -> 17%
where the time goes in v8:
time: 250 us; the launch traced here: 249 us
  waiting for transfers between devices  153 us (61%)
  Pallas kernels  41.5 us (17%)
  starting transfers between devices  31.7 us (13%)
  between operations  13.3 us (5%)
  other arithmetic  6.2 us (2%)
  local copies, waits for them, and re-layouts  3.47 us (1%)
    all_to_all x2, waiting for transfers between devices, local(): lax.all_to_all(piece, (X, C, Y), split_axis=0, concat_axis=0, tiled=True)  90 us
    reduce_scatter x2, waiting for transfers between devices, local(): lax.psum_scatter(partial_value, Z, scatter_dimension=1, tiled=True)  41.4 us
    pallas_call x2, Pallas kernels, stack_chunk(): pl.pallas_call(functools.partial(stack_kernel, start, width, block), out_...  23.3 us
    pallas_call x2, Pallas kernels, product(): pl.pallas_call(product_kernel, out_shape=jax.ShapeDtypeStruct((rows, widt...  18.2 us
    ppermute x1, waiting for transfers between devices, local(): return lax.ppermute(out, (Z, X, C), perm)  16.3 us
    all_to_all x2, starting transfers between devices, local(): lax.all_to_all(piece, (X, C, Y), split_axis=0, concat_axis=0, tiled=True)  15.7 us
    ppermute x1, starting transfers between devices, local(): coulomb_here = lax.ppermute(coulomb, (Z, X, C), perm)  7.96 us
    ppermute x1, starting transfers between devices, local(): return lax.ppermute(out, (Z, X, C), perm)  7.89 us
  transfers between devices with their start and end apart: 7, of which 5 were waited for; matrix products, arithmetic and copies ran while one was open for 1% of the time, Pallas kernels for 17%

profile of v8, /device:TPU:7, one launch (start us, length us, event | category | flops | bytes accessed | tf_op | source)
XLA Modules:
  0.0 249.3 jit_solution(7923302575956843429)
XLA Ops:
  6.5 0.0 all-gather.2.cloned.1.call-start
  6.5 0.7 convert_element_type.10
  7.2 0.2 broadcast_in_dim.140
  7.4 0.3 reshape.123
  7.7 0.1 constant_dynamic-slice_fusion
  7.8 0.1 mul.41
  7.9 0.0 copy-start.5
  7.9 0.5 copy.12
  8.4 2.5 %dynamic-slice_multiply_fusion = bf16[480,1024]{1,0:T(8,128)(2,1)} fusion(bf16[480,1024]{1,0:T(8,128)(2,1)S(1)} %copy.12, bf16[3840,1024]{1,0:T(8,128)(2,1)} %param.9, s32[]{:T(128)S(6)} %select_n.113), kind=kLoop, calls=%fused_computation.1 | loop fusion | flops 1966080 | bytes 2949124 | tf_op jit(solution)/shard_map/mul | solution.py:99
  11.0 0.0 all-gather.2.cloned.1.call-update
  11.0 0.0 copy-done.5
  11.0 8.0 %collective-permute-start = (bf16[960,128]{1,0:T(8,128)(2,1)S(1)}, bf16[960,128]{1,0:T(8,128)(2,1)S(1)}, u32[]{:S(2)}, u32[]{:S(2)}) collective-permute-start(bf16[960,128]{1,0:T(8,128)(2,1)S(1)} %copy-done.5), channel_id=1, source_target_pairs={{0,0},{1,32},{2,64},{3,96},{4,128},{5,160},{6,192},{7,224},{32,1},... | collective-permute-start | bytes 737288 | tf_op jit(solution)/shard_map/ppermute | solution.py:106
  19.0 11.5 %shard_map.82 = bf16[32,120,360]{2,1,0:T(8,128)(2,1)} custom-call(bf16[120,30720]{1,0:T(8,128)(2,1)} %in_ref.3), custom_call_target="tpu_custom_call" | custom-call | tf_op jit(solution)/shard_map/pallas_call | solution.py:62
  30.5 5.4 %collective-permute-done = bf16[960,128]{1,0:T(8,128)(2,1)S(1)} collective-permute-done((bf16[960,128]{1,0:T(8,128)(2,1)S(1)}, bf16[960,128]{1,0:T(8,128)(2,1)S(1)}, u32[]{:S(2)}, u32[]{:S(2)}) %collective-permute-start) | collective-permute-done | bytes 245792 | tf_op jit(solution)/shard_map/ppermute | solution.py:106
  35.9 7.1 %all-to-all-start.1 = ((bf16[32,120,360]{2,1,0:T(8,128)(2,1)}), bf16[32,120,360]{2,1,0:T(8,128)(2,1)S(1)}, u32[]{:S(2)}, u32[]{:S(2)}) async-start(bf16[32,120,360]{2,1,0:T(8,128)(2,1)} %shard_map.82), calls=%async_computation.2 | async-start | bytes 5898240 | tf_op jit(solution)/shard_map/all_to_all | solution.py:114
  43.0 11.8 %shard_map.83 = bf16[32,120,600]{2,1,0:T(8,128)(2,1)} custom-call(bf16[120,30720]{1,0:T(8,128)(2,1)} %in_ref.3), custom_call_target="tpu_custom_call" | custom-call | tf_op jit(solution)/shard_map/pallas_call | solution.py:62
  54.8 39.6 %all-to-all-done.1 = bf16[32,120,360]{2,1,0:T(8,128)(2,1)S(1)} async-done(((bf16[32,120,360]{2,1,0:T(8,128)(2,1)}), bf16[32,120,360]{2,1,0:T(8,128)(2,1)S(1)}, u32[]{:S(2)}, u32[]{:S(2)}) %all-to-all-start.1) | async-done | bytes 2764832 | tf_op jit(solution)/shard_map/all_to_all | solution.py:114
  94.4 0.0 copy-start
  94.4 1.6 copy-done
  96.0 8.6 %all-to-all-start = ((bf16[32,120,600]{2,1,0:T(8,128)(2,1)}), bf16[32,120,600]{2,1,0:T(8,128)(2,1)}, u32[]{:S(2)}, u32[]{:S(2)}) async-start(bf16[32,120,600]{2,1,0:T(8,128)(2,1)} %shard_map.83), calls=%async_computation | async-start | bytes 9830400 | tf_op jit(solution)/shard_map/all_to_all | solution.py:114
  104.6 0.0 reduce-scatter.5.cloned.1.call-start
  104.7 0.0 all-gather.2.cloned.1.call-done.right_ref
  104.7 8.0 %shard_map.85 = f32[360,1024]{1,0:T(8,128)} custom-call(bf16[3840,360]{1,0:T(8,128)(2,1)} %bitcast.5, bf16[3840,1024]{1,0:T(8,128)(2,1)} %all-gather.2.cloned.1.call-done.right_ref), custom_call_target="tpu_custom_call" | custom-call | flops 2831155200 | bytes 12103680 | tf_op jit(solution)/shard_map/pallas_call | solution.py:37
  112.7 0.0 reduce-scatter.5.cloned.1.call-update
  112.7 0.0 reduce-scatter.3.cloned.1.call-start
  112.7 50.4 %all-to-all-done = bf16[32,120,600]{2,1,0:T(8,128)(2,1)} async-done(((bf16[32,120,600]{2,1,0:T(8,128)(2,1)}), bf16[32,120,600]{2,1,0:T(8,128)(2,1)}, u32[]{:S(2)}, u32[]{:S(2)}) %all-to-all-start) | async-done | bytes 4608032 | tf_op jit(solution)/shard_map/all_to_all | solution.py:114
  163.2 0.0 copy-start.1
  163.2 0.0 copy-start.2
  163.2 0.0 copy-start.3
  163.2 0.0 copy-start.4
  163.2 10.2 %shard_map.84 = f32[600,1024]{1,0:T(8,128)} custom-call(bf16[3840,600]{1,0:T(8,128)(2,1)} %bitcast.left_ref, bf16[3840,1024]{1,0:T(8,128)(2,1)} %all-gather.2.cloned.1.call-done.right_ref), custom_call_target="tpu_custom_call" | custom-call | flops 4718592000 | bytes 14929920 | tf_op jit(solution)/shard_map/pallas_call | solution.py:37
  173.4 0.0 reduce-scatter.3.cloned.1.call-update
  173.4 0.0 copy-done.1
  173.4 0.2 select_reduce_fusion.2
  173.6 0.0 copy-done.2
  173.6 0.4 select_reduce_fusion
  174.0 0.0 copy-done.3
  174.0 0.2 select_reduce_fusion.3
  174.2 0.0 copy-done.4
  174.2 0.4 select_reduce_fusion.1
  174.6 0.1 select_reduce_fusion.6
  174.7 0.1 select_reduce_fusion.4
  174.8 0.1 select_reduce_fusion.7
  174.9 0.1 select_reduce_fusion.5
  175.1 0.0 reduce-scatter.5.cloned.1.call-done
  175.1 41.3 %reduce-scatter.3.cloned.1.call-done = f32[600,128]{1,0:T(8,128)} async-done(((f32[600,1024]{1,0:T(8,128)}), f32[600,128]{1,0:T(8,128)}) %reduce-scatter.3.cloned.1.call-update) | async-done | bytes 307216 | tf_op jit(solution)/shard_map/reduce_scatter | solution.py:116
  216.4 1.4 fusion.2
  217.8 7.9 %collective-permute-start.1 = (bf16[960,128]{1,0:T(8,128)(2,1)S(1)}, bf16[960,128]{1,0:T(8,128)(2,1)S(1)}, u32[]{:S(2)}, u32[]{:S(2)}) collective-permute-start(bf16[960,128]{1,0:T(8,128)(2,1)S(1)} %fusion.2), channel_id=1, source_target_pairs={{0,0},{1,32},{2,64},{3,96},{4,128},{5,160},{6,192},{7,224},{32,1},... | collective-permute-start | bytes 737288 | tf_op jit(solution)/shard_map/ppermute | solution.py:134
  225.7 16.3 %collective-permute-done.1 = bf16[960,128]{1,0:T(8,128)(2,1)S(1)} collective-permute-done((bf16[960,128]{1,0:T(8,128)(2,1)S(1)}, bf16[960,128]{1,0:T(8,128)(2,1)S(1)}, u32[]{:S(2)}, u32[]{:S(2)}) %collective-permute-start.1) | collective-permute-done | bytes 245792 | tf_op jit(solution)/shard_map/ppermute | solution.py:134
  242.1 0.7 copy.14
  (6 shorter events, 0.1 us)
Async XLA Ops:
  6.5 98.2 %all-gather.2.cloned.1.call-start = ((), (), s32[]{:S(2)}) async-start(), calls=%async_computation.4 | async-start | bytes 8847360 | tf_op jit(solution)/shard_map/all_gather | solution.py:101
  7.9 3.1 %copy-start.5 = (bf16[960,128]{1,0:T(8,128)(2,1)S(1)}, bf16[960,128]{1,0:T(8,128)(2,1)}, u32[]{:S(2)}) copy-start(bf16[960,128]{1,0:T(8,128)(2,1)} %param.11) | copy-start | bytes 737284
  11.0 24.9 %collective-permute-start = (bf16[960,128]{1,0:T(8,128)(2,1)S(1)}, bf16[960,128]{1,0:T(8,128)(2,1)S(1)}, u32[]{:S(2)}, u32[]{:S(2)}) collective-permute-start(bf16[960,128]{1,0:T(8,128)(2,1)S(1)} %copy-done.5), channel_id=1, source_target_pairs={{0,0},{1,32},{2,64},{3,96},{4,128},{5,160},{6,192},{7,224},{32,1},... | collective-permute-start | bytes 737288 | tf_op jit(solution)/shard_map/ppermute | solution.py:106
  35.9 58.5 %all-to-all-start.1 = ((bf16[32,120,360]{2,1,0:T(8,128)(2,1)}), bf16[32,120,360]{2,1,0:T(8,128)(2,1)S(1)}, u32[]{:S(2)}, u32[]{:S(2)}) async-start(bf16[32,120,360]{2,1,0:T(8,128)(2,1)} %shard_map.82), calls=%async_computation.2 | async-start | bytes 5898240 | tf_op jit(solution)/shard_map/all_to_all | solution.py:114
  94.4 1.6 copy-start
  96.0 67.2 %all-to-all-start = ((bf16[32,120,600]{2,1,0:T(8,128)(2,1)}), bf16[32,120,600]{2,1,0:T(8,128)(2,1)}, u32[]{:S(2)}, u32[]{:S(2)}) async-start(bf16[32,120,600]{2,1,0:T(8,128)(2,1)} %shard_map.83), calls=%async_computation | async-start | bytes 9830400 | tf_op jit(solution)/shard_map/all_to_all | solution.py:114
  104.6 70.5 %reduce-scatter.5.cloned.1.call-start = ((), (), s32[]{:S(2)}) async-start(), calls=%async_computation.6 | async-start | bytes 1658880 | tf_op jit(solution)/shard_map/reduce_scatter | solution.py:116
  112.7 103.8 %reduce-scatter.3.cloned.1.call-start = ((), (), s32[]{:S(2)}) async-start(), calls=%async_computation.5 | async-start | bytes 2764800 | tf_op jit(solution)/shard_map/reduce_scatter | solution.py:116
  163.2 10.3 %copy-start.1 = (f32[192]{0:T(256)S(1)}, f32[192]{0:T(256)}, u32[]{:S(2)}) copy-start(f32[192]{0:T(256)} %param.15) | copy-start | bytes 2308
  163.2 10.5 %copy-start.2 = (f32[240]{0:T(256)S(1)}, f32[240]{0:T(256)}, u32[]{:S(2)}) copy-start(f32[240]{0:T(256)} %param.14) | copy-start | bytes 2884
  163.2 10.8 %copy-start.3 = (s32[192]{0:T(256)S(1)}, s32[192]{0:T(256)}, u32[]{:S(2)}) copy-start(s32[192]{0:T(256)} %param.13) | copy-start | bytes 2308
  163.2 11.0 %copy-start.4 = (s32[240]{0:T(256)S(1)}, s32[240]{0:T(256)}, u32[]{:S(2)}) copy-start(s32[240]{0:T(256)} %param.12) | copy-start | bytes 2884
  217.8 24.2 %collective-permute-start.1 = (bf16[960,128]{1,0:T(8,128)(2,1)S(1)}, bf16[960,128]{1,0:T(8,128)(2,1)S(1)}, u32[]{:S(2)}, u32[]{:S(2)}) collective-permute-start(bf16[960,128]{1,0:T(8,128)(2,1)S(1)} %fusion.2), channel_id=1, source_target_pairs={{0,0},{1,32},{2,64},{3,96},{4,128},{5,160},{6,192},{7,224},{32,1},... | collective-permute-start | bytes 737288 | tf_op jit(solution)/shard_map/ppermute | solution.py:134
Sparse Core Ops, SparseCore 0:
  11.1 86.2 all-gather.1
  112.8 38.7 reduce-scatter.4
  173.5 42.8 reduce-scatter.2

commit v9 on v8

--- a/solution.py
+++ b/solution.py
@@ -77,6 +77,34 @@
     return [(z * nc + c, c * nz + z) for z in range(nz) for c in range(nc)]
 
 
+def gather_cols(piece):
+    nx = lax.axis_size(X)
+    x = lax.axis_index(X)
+    first = lax.axis_index(C) == 0
+    swap = [(0, 1), (1, 0)]
+    forward = [(i * 2, (i + 1) % nx * 2) for i in range(nx)]
+    backward = [(i * 2 + 1, (i - 1) % nx * 2 + 1) for i in range(nx)]
+    other = lax.ppermute(piece, C, swap)
+    chip = jnp.where(first, jnp.concatenate([piece, other]), jnp.concatenate([other, piece]))
+    near = lax.ppermute(chip, (X, C), forward + backward)
+    near_other = lax.ppermute(near, C, swap)
+    half = chip.shape[1] // 2
+    ahead = lax.ppermute(
+        jnp.where(first, near[:, :half], near[:, half:]), (X, C), forward + backward
+    )
+    ahead_other = lax.ppermute(ahead, C, swap)
+    far = jnp.where(
+        first,
+        jnp.concatenate([ahead, ahead_other], axis=1),
+        jnp.concatenate([ahead_other, ahead], axis=1),
+    )
+    following = jnp.where(first, near_other, near)
+    preceding = jnp.where(first, near, near_other)
+    chips = jnp.stack([chip, following, far, preceding])
+    chips = jnp.take(chips, (jnp.arange(nx) - x) % nx, axis=0)
+    return chips.reshape(nx * chip.shape[0], chip.shape[1])
+
+
 def local(amps, cycle_int, tile_mask, coulomb, occ_irrep, vir_irrep, occ_energy, vir_energy):
     block_size = BLK
     occupied = occ_energy.shape[0]
@@ -98,7 +126,7 @@
     masked = (
         ci_rows.reshape(span, jb_all // block_size, block_size) * mask_rows[:, :, None]
     ).reshape(span, jb_all)
-    masked_all = lax.all_gather(masked, COL, axis=0, tiled=True)
+    masked_all = gather_cols(masked)
 
     groups = lax.axis_size((X, C, Y))
     block = amps.shape[1] // groups

time: 250 us -> 297 us (1.19)
  local copies, waits for them, and re-layouts: 3.47 us -> 38.2 us
  other arithmetic: 6.2 us -> 31 us
  waiting for transfers between devices: 153 us -> 134 us
  starting transfers between devices: 31.7 us -> 37.4 us
    all_to_all x2, waiting for transfers between devices: 90 us -> 16.7 us  [local(): lax.all_to_all(piece, (X, C, Y), split_axis=0, concat_axis=0, tiled=True)]
    ppermute x0 -> x5, waiting for transfers between devices: none -> 41.5 us  [the longest x1 39.3 us: gather_cols(): lax.ppermute(jnp.where(first, near[:, :half], near[:, half:]), (X, C), fo...]
    gather x0 -> x2, local copies, waits for them, and re-layouts: none -> 19.5 us  [gather_cols(): chips = jnp.take(chips, (jnp.arange(nx) - x) % nx, axis=0)]
    select_n x0 -> x6, other arithmetic: none -> 18.7 us  [the longest x2 7.47 us: gather_cols(): chips = jnp.take(chips, (jnp.arange(nx) - x) % nx, axis=0)]
    reduce_scatter x2, waiting for transfers between devices: 41.4 us -> 54.1 us  [local(): lax.psum_scatter(partial_value, Z, scatter_dimension=1, tiled=True)]
    ppermute x0 -> x5, local copies, waits for them, and re-layouts: none -> 11 us  [the longest x1 3.9 us: gather_cols(): near_other = lax.ppermute(near, C, swap)]
    another operation x0 -> x2, other arithmetic: none -> 9.18 us  [gather_cols(): chips = jnp.stack([chip, following, far, preceding])]
    ppermute x0 -> x5, starting transfers between devices: none -> 5.14 us  [the longest x1 3.22 us: gather_cols(): near_other = lax.ppermute(near, C, swap)]
  transfers between devices with their start and end apart: 7 -> 11, of which waited for: 5 -> 7; matrix products, arithmetic and copies ran while one was open for 1% -> 19% of each run, Pallas kernels for 17% -> 14%
where the time goes in v9:
time: 297 us; the launch traced here: 296 us
  waiting for transfers between devices  134 us (45%)
  Pallas kernels  41.2 us (14%)
  local copies, waits for them, and re-layouts  38.2 us (13%)
  starting transfers between devices  37.4 us (13%)
  other arithmetic  31 us (10%)
  between operations  13.7 us (5%)
    reduce_scatter x2, waiting for transfers between devices, local(): lax.psum_scatter(partial_value, Z, scatter_dimension=1, tiled=True)  54.1 us
    ppermute x1, waiting for transfers between devices, gather_cols(): lax.ppermute(jnp.where(first, near[:, :half], near[:, half:]), (X, C), fo...  39.3 us
    pallas_call x2, Pallas kernels, stack_chunk(): pl.pallas_call(functools.partial(stack_kernel, start, width, block), out_...  23 us
    gather x2, local copies, waits for them, and re-layouts, gather_cols(): chips = jnp.take(chips, (jnp.arange(nx) - x) % nx, axis=0)  19.5 us
    pallas_call x2, Pallas kernels, product(): pl.pallas_call(product_kernel, out_shape=jax.ShapeDtypeStruct((rows, widt...  18.2 us
    all_to_all x2, waiting for transfers between devices, local(): lax.all_to_all(piece, (X, C, Y), split_axis=0, concat_axis=0, tiled=True)  16.7 us
    ppermute x1, waiting for transfers between devices, local(): return lax.ppermute(out, (Z, X, C), perm)  16.4 us
    all_to_all x2, starting transfers between devices, local(): lax.all_to_all(piece, (X, C, Y), split_axis=0, concat_axis=0, tiled=True)  15.9 us
  transfers between devices with their start and end apart: 11, of which 7 were waited for; matrix products, arithmetic and copies ran while one was open for 19% of the time, Pallas kernels for 14%

profile of v9, /device:TPU:7, one launch (start us, length us, event | category | flops | bytes accessed | tf_op | source)
XLA Modules:
  0.0 295.5 jit_solution(1602121991304047457)
XLA Ops:
  6.5 1.3 constant_dynamic-slice_fusion
  7.8 0.5 copy.40
  8.4 0.0 copy-done.2
  8.4 0.2 broadcast_in_dim.157
  8.6 0.3 reshape.290
  8.9 0.1 constant_dynamic-slice_fusion.1
  9.0 0.1 bitcast_multiply_fusion
  9.0 0.5 copy.28
  9.6 0.8 collective-permute-start.1
  10.3 2.2 collective-permute-done.1
  12.5 0.5 copy.29
  13.1 2.8 maximum_select_fusion.1
  15.9 4.0 %copy.32 = bf16[960,1024]{1,0:T(8,128)(2,1)} copy(bf16[960,1024]{0,1:T(8,128)(2,1)} %maximum_select_fusion.1) | data formatting | bytes 3932160 | tf_op jit(solution)/shard_map/jit(_where)/select_n | solution.py:88
  19.9 0.5 collective-permute-start.2
  20.5 8.6 %collective-permute-start = (bf16[960,128]{1,0:T(8,128)(2,1)S(1)}, bf16[960,128]{1,0:T(8,128)(2,1)S(1)}, u32[]{:S(2)}, u32[]{:S(2)}) collective-permute-start(bf16[960,128]{1,0:T(8,128)(2,1)S(1)} %copy-done.7), channel_id=1, source_target_pairs={{0,0},{1,32},{2,64},{3,96},{4,128},{5,160},{6,192},{7,224},{32,1},... | collective-permute-start | bytes 737288 | tf_op jit(solution)/shard_map/ppermute | solution.py:134
  29.1 11.4 %shard_map.82 = bf16[32,120,360]{2,1,0:T(8,128)(2,1)} custom-call(bf16[120,30720]{1,0:T(8,128)(2,1)} %in_ref.3), custom_call_target="tpu_custom_call" | custom-call | tf_op jit(solution)/shard_map/pallas_call | solution.py:62
  40.4 5.3 %collective-permute-done = bf16[960,128]{1,0:T(8,128)(2,1)S(1)} collective-permute-done((bf16[960,128]{1,0:T(8,128)(2,1)S(1)}, bf16[960,128]{1,0:T(8,128)(2,1)S(1)}, u32[]{:S(2)}, u32[]{:S(2)}) %collective-permute-start) | collective-permute-done | bytes 245792 | tf_op jit(solution)/shard_map/ppermute | solution.py:134
  45.7 7.2 %all-to-all-start.1 = ((bf16[32,120,360]{2,1,0:T(8,128)(2,1)}), bf16[32,120,360]{2,1,0:T(8,128)(2,1)}, u32[]{:S(2)}, u32[]{:S(2)}) async-start(bf16[32,120,360]{2,1,0:T(8,128)(2,1)} %shard_map.82), calls=%async_computation.2 | async-start | bytes 5898240 | tf_op jit(solution)/shard_map/all_to_all | solution.py:142
  52.9 0.0 collective-permute-done.2
  52.9 1.6 slice_select_fusion
  54.5 0.6 collective-permute-start.4
  55.1 3.2 %collective-permute-start.3 = (bf16[960,1024]{1,0:T(8,128)(2,1)}, bf16[960,1024]{1,0:T(8,128)(2,1)}, u32[]{:S(2)}, u32[]{:S(2)}) collective-permute-start(bf16[960,1024]{1,0:T(8,128)(2,1)} %collective-permute-done.2), channel_id=1, source_target_pairs={{0,1},{1,0},{2,3},{3,2},{4,5},{5,4},{6,7},{7,6},{8,9},{9,8},{10,11... | collective-permute-start | bytes 5898248 | tf_op jit(solution)/shard_map/ppermute | solution.py:90
  58.3 39.3 %collective-permute-done.4 = bf16[960,512]{1,0:T(8,128)(2,1)} collective-permute-done((bf16[960,512]{1,0:T(8,128)(2,1)S(1)}, bf16[960,512]{1,0:T(8,128)(2,1)}, u32[]{:S(2)}, u32[]{:S(2)}) %collective-permute-start.4) | collective-permute-done | bytes 983072 | tf_op jit(solution)/shard_map/ppermute | solution.py:92
  97.6 0.0 collective-permute-start.5
  97.6 11.6 %shard_map.83 = bf16[32,120,600]{2,1,0:T(8,128)(2,1)} custom-call(bf16[120,30720]{1,0:T(8,128)(2,1)} %in_ref.3), custom_call_target="tpu_custom_call" | custom-call | tf_op jit(solution)/shard_map/pallas_call | solution.py:62
  109.3 0.1 broadcast_in_dim.154
  109.3 0.1 broadcast_in_dim.155
  109.4 2.8 maximum_select_fusion
  112.3 2.8 copy.34
  115.1 1.5 copy.35
  116.6 0.0 collective-permute-done.5
  116.6 2.2 copy.36
  118.8 0.0 collective-permute-done.3
  118.8 3.9 %copy.33 = bf16[960,1024]{0,1:T(8,128)(2,1)} copy(bf16[960,1024]{1,0:T(8,128)(2,1)} %collective-permute-done.3) | data formatting | bytes 3932160 | tf_op jit(solution)/shard_map/ppermute | solution.py:90
  122.7 4.0 %maximum_select_fusion.2 = bf16[1,960,1024]{1,2,0:T(8,128)(2,1)} fusion(bf16[1,960,512]{1,2,0:T(8,128)(2,1)} %bitcast.21, bf16[1,960,512]{1,2,0:T(8,128)(2,1)S(1)} %bitcast.20, pred[]{:T(512)S(6)} %eq.55), kind=kLoop, calls=%fused_computation.5 | loop fusion | flops 8847360 | bytes 3932161 | tf_op jit(solution)/shard_map/jit(_where)/select_n | solution.py:96
  126.7 2.5 select_bitcast_fusion.1
  129.2 0.0 all-to-all-done.1
  129.2 8.7 %all-to-all-start = ((bf16[32,120,600]{2,1,0:T(8,128)(2,1)}), bf16[32,120,600]{2,1,0:T(8,128)(2,1)}, u32[]{:S(2)}, u32[]{:S(2)}) async-start(bf16[32,120,600]{2,1,0:T(8,128)(2,1)} %shard_map.83), calls=%async_computation | async-start | bytes 9830400 | tf_op jit(solution)/shard_map/all_to_all | solution.py:142
  138.0 0.2 reduce-scatter.5.cloned.1.call-start
  138.2 0.0 copy-done.1
  138.2 6.7 %pad_maximum_fusion = bf16[4,960,1024]{1,2,0:T(8,128)(2,1)} fusion(bf16[1,960,1024]{1,2,0:T(8,128)(2,1)} %get-tuple-element.10, bf16[1,960,1024]{1,2,0:T(8,128)(2,1)} %maximum_select_fusion.2, bf16[1,960,1024]{1,2,0:T(8,128)(2,1)} %get-tuple-element.9, bf16[1,960,1024]{1,2,0:T(8,128)(2,1)S(1)} %copy-done.1), kind=kLoop, calls=%fused_computation.1 | loop fusion | flops 11796480 | bytes 15728640 | tf_op jit(solution)/shard_map/stack | solution.py:103
  144.9 8.0 %gather_fusion = bf16[4,960,1024]{1,2,0:T(8,128)(2,1)} fusion(bf16[4,960,1024]{1,2,0:T(8,128)(2,1)} %pad_maximum_fusion, s32[1024]{0:T(1024)S(1)} %pad_clamp_fusion), kind=kCustom, calls=%fused_computation | custom fusion | bytes 15728656 | tf_op jit(solution)/shard_map/jit(_take)/gather | solution.py:104
  152.9 11.5 %copy.39 = bf16[4,960,1024]{2,1,0:T(8,128)(2,1)} copy(bf16[4,960,1024]{1,2,0:T(8,128)(2,1)} %gather_fusion) | data formatting | bytes 15728640 | tf_op jit(solution)/shard_map/jit(_take)/gather | solution.py:104
  164.3 7.5 %bitcast_select_fusion.right_ref = bf16[3840,1024]{1,0:T(8,128)(2,1)} fusion(bf16[4,960,1024]{2,1,0:T(8,128)(2,1)} %copy.39, pred[3840]{0:T(1024)(128)(4,1)S(1)} %broadcast_in_dim.155), kind=kLoop, calls=%fused_computation.2 | loop fusion | flops 3932160 | bytes 15732480 | tf_op jit(solution)/shard_map/jit(_take)/select_n | solution.py:104
  171.8 7.9 %shard_map.85 = f32[360,1024]{1,0:T(8,128)} custom-call(bf16[3840,360]{1,0:T(8,128)(2,1)} %bitcast.10.left_ref, bf16[3840,1024]{1,0:T(8,128)(2,1)} %bitcast_select_fusion.right_ref), custom_call_target="tpu_custom_call" | custom-call | flops 2831155200 | bytes 12103680 | tf_op jit(solution)/shard_map/pallas_call | solution.py:37
  179.7 0.0 reduce-scatter.5.cloned.1.call-update
  179.8 0.0 reduce-scatter.3.cloned.1.call-start
  179.8 16.7 %all-to-all-done = bf16[32,120,600]{2,1,0:T(8,128)(2,1)} async-done(((bf16[32,120,600]{2,1,0:T(8,128)(2,1)}), bf16[32,120,600]{2,1,0:T(8,128)(2,1)}, u32[]{:S(2)}, u32[]{:S(2)}) %all-to-all-start) | async-done | bytes 4608032 | tf_op jit(solution)/shard_map/all_to_all | solution.py:142
  196.5 10.3 %shard_map.84 = f32[600,1024]{1,0:T(8,128)} custom-call(bf16[3840,600]{1,0:T(8,128)(2,1)} %bitcast.left_ref, bf16[3840,1024]{1,0:T(8,128)(2,1)} %bitcast_select_fusion.right_ref), custom_call_target="tpu_custom_call" | custom-call | flops 4718592000 | bytes 14929920 | tf_op jit(solution)/shard_map/pallas_call | solution.py:37
  206.8 0.0 reduce-scatter.3.cloned.1.call-update
  206.9 0.2 select_reduce_fusion.2
  207.1 0.4 select_reduce_fusion
  207.5 0.2 select_reduce_fusion.3
  207.7 0.4 select_reduce_fusion.1
  208.0 0.1 select_reduce_fusion.6
  208.2 0.1 select_reduce_fusion.4
  208.3 0.1 select_reduce_fusion.7
  208.4 0.1 select_reduce_fusion.5
  208.5 9.5 %reduce-scatter.5.cloned.1.call-done = f32[360,128]{1,0:T(8,128)} async-done(((f32[360,1024]{1,0:T(8,128)}), f32[360,128]{1,0:T(8,128)}) %reduce-scatter.5.cloned.1.call-update) | async-done | bytes 184336 | tf_op jit(solution)/shard_map/reduce_scatter | solution.py:144
  218.0 44.6 %reduce-scatter.3.cloned.1.call-done = f32[600,128]{1,0:T(8,128)} async-done(((f32[600,1024]{1,0:T(8,128)}), f32[600,128]{1,0:T(8,128)}) %reduce-scatter.3.cloned.1.call-update) | async-done | bytes 307216 | tf_op jit(solution)/shard_map/reduce_scatter | solution.py:144
  262.6 1.4 fusion.2
  264.0 7.5 %collective-permute-start.6 = (bf16[960,128]{1,0:T(8,128)(2,1)S(1)}, bf16[960,128]{1,0:T(8,128)(2,1)S(1)}, u32[]{:S(2)}, u32[]{:S(2)}) collective-permute-start(bf16[960,128]{1,0:T(8,128)(2,1)S(1)} %fusion.2), channel_id=1, source_target_pairs={{0,0},{1,32},{2,64},{3,96},{4,128},{5,160},{6,192},{7,224},{32,1},... | collective-permute-start | bytes 737288 | tf_op jit(solution)/shard_map/ppermute | solution.py:162
  271.5 16.4 %collective-permute-done.6 = bf16[960,128]{1,0:T(8,128)(2,1)S(1)} collective-permute-done((bf16[960,128]{1,0:T(8,128)(2,1)S(1)}, bf16[960,128]{1,0:T(8,128)(2,1)S(1)}, u32[]{:S(2)}, u32[]{:S(2)}) %collective-permute-start.6) | collective-permute-done | bytes 245792 | tf_op jit(solution)/shard_map/ppermute | solution.py:162
  288.0 0.7 copy.42
  (24 shorter events, 0.1 us)
Async XLA Ops:
  6.5 1.8 copy-start.2
  9.6 3.0 %collective-permute-start.1 = (bf16[480,1024]{1,0:T(8,128)(2,1)S(1)}, bf16[480,1024]{1,0:T(8,128)(2,1)S(1)}, u32[]{:S(2)}, u32[]{:S(2)}) collective-permute-start(bf16[480,1024]{1,0:T(8,128)(2,1)S(1)} %copy.28), channel_id=1, source_target_pairs={{0,1},{1,0},{2,3},{3,2},{4,5},{5,4},{6,7},{7,6},{8,9},{9,8},{10,11... | collective-permute-start | bytes 2949128 | tf_op jit(solution)/shard_map/ppermute | solution.py:87
  15.9 4.5 %copy-start.7 = (bf16[960,128]{1,0:T(8,128)(2,1)S(1)}, bf16[960,128]{1,0:T(8,128)(2,1)}, u32[]{:S(2)}) copy-start(bf16[960,128]{1,0:T(8,128)(2,1)} %param.11) | copy-start | bytes 737284
  19.9 33.0 %collective-permute-start.2 = (bf16[960,1024]{1,0:T(8,128)(2,1)}, bf16[960,1024]{1,0:T(8,128)(2,1)}, u32[]{:S(2)}, u32[]{:S(2)}) collective-permute-start(bf16[960,1024]{1,0:T(8,128)(2,1)} %copy.32), channel_id=1, source_target_pairs={{0,2},{2,4},{4,6},{6,0},{1,7},{3,1},{5,3},{7,5},{8,10},{10,12},{12... | collective-permute-start | bytes 5898248 | tf_op jit(solution)/shard_map/ppermute | solution.py:89
  20.5 25.3 %collective-permute-start = (bf16[960,128]{1,0:T(8,128)(2,1)S(1)}, bf16[960,128]{1,0:T(8,128)(2,1)S(1)}, u32[]{:S(2)}, u32[]{:S(2)}) collective-permute-start(bf16[960,128]{1,0:T(8,128)(2,1)S(1)} %copy-done.7), channel_id=1, source_target_pairs={{0,0},{1,32},{2,64},{3,96},{4,128},{5,160},{6,192},{7,224},{32,1},... | collective-permute-start | bytes 737288 | tf_op jit(solution)/shard_map/ppermute | solution.py:134
  45.7 83.5 %all-to-all-start.1 = ((bf16[32,120,360]{2,1,0:T(8,128)(2,1)}), bf16[32,120,360]{2,1,0:T(8,128)(2,1)}, u32[]{:S(2)}, u32[]{:S(2)}) async-start(bf16[32,120,360]{2,1,0:T(8,128)(2,1)} %shard_map.82), calls=%async_computation.2 | async-start | bytes 5898240 | tf_op jit(solution)/shard_map/all_to_all | solution.py:142
  54.5 43.1 %collective-permute-start.4 = (bf16[960,512]{1,0:T(8,128)(2,1)S(1)}, bf16[960,512]{1,0:T(8,128)(2,1)}, u32[]{:S(2)}, u32[]{:S(2)}) collective-permute-start(bf16[960,512]{1,0:T(8,128)(2,1)S(1)} %slice_select_fusion), channel_id=1, source_target_pairs={{0,2},{2,4},{4,6},{6,0},{1,7},{3,1},{5,3},{7,5},{8,10},{10,12},{12... | collective-permute-start | bytes 2949128 | tf_op jit(solution)/shard_map/ppermute | solution.py:92
  55.1 63.7 %collective-permute-start.3 = (bf16[960,1024]{1,0:T(8,128)(2,1)}, bf16[960,1024]{1,0:T(8,128)(2,1)}, u32[]{:S(2)}, u32[]{:S(2)}) collective-permute-start(bf16[960,1024]{1,0:T(8,128)(2,1)} %collective-permute-done.2), channel_id=1, source_target_pairs={{0,1},{1,0},{2,3},{3,2},{4,5},{5,4},{6,7},{7,6},{8,9},{9,8},{10,11... | collective-permute-start | bytes 5898248 | tf_op jit(solution)/shard_map/ppermute | solution.py:90
  97.6 19.0 %collective-permute-start.5 = (bf16[960,512]{1,0:T(8,128)(2,1)}, bf16[960,512]{1,0:T(8,128)(2,1)}, u32[]{:S(2)}, u32[]{:S(2)}) collective-permute-start(bf16[960,512]{1,0:T(8,128)(2,1)} %collective-permute-done.4), channel_id=1, source_target_pairs={{0,1},{1,0},{2,3},{3,2},{4,5},{5,4},{6,7},{7,6},{8,9},{9,8},{10,11... | collective-permute-start | bytes 2949128 | tf_op jit(solution)/shard_map/ppermute | solution.py:95
  122.7 4.0 %copy-start = (bf16[960,1024]{0,1:T(8,128)(2,1)S(1)}, bf16[960,1024]{0,1:T(8,128)(2,1)}, u32[]{:S(2)}) copy-start(bf16[960,1024]{0,1:T(8,128)(2,1)} %copy.33) | copy-start | bytes 5898244
  129.2 9.0 %copy-start.1 = (bf16[1,960,1024]{1,2,0:T(8,128)(2,1)S(1)}, bf16[1,960,1024]{1,2,0:T(8,128)(2,1)}, u32[]{:S(2)}) copy-start(bf16[1,960,1024]{1,2,0:T(8,128)(2,1)} %maximum_select_fusion) | copy-start | bytes 5898244
  129.2 67.3 %all-to-all-start = ((bf16[32,120,600]{2,1,0:T(8,128)(2,1)}), bf16[32,120,600]{2,1,0:T(8,128)(2,1)}, u32[]{:S(2)}, u32[]{:S(2)}) async-start(bf16[32,120,600]{2,1,0:T(8,128)(2,1)} %shard_map.83), calls=%async_computation | async-start | bytes 9830400 | tf_op jit(solution)/shard_map/all_to_all | solution.py:142
  138.0 80.0 %reduce-scatter.5.cloned.1.call-start = ((), (), s32[]{:S(2)}) async-start(), calls=%async_computation.5 | async-start | bytes 1658880 | tf_op jit(solution)/shard_map/reduce_scatter | solution.py:144
  179.8 82.9 %reduce-scatter.3.cloned.1.call-start = ((), (), s32[]{:S(2)}) async-start(), calls=%async_computation.4 | async-start | bytes 2764800 | tf_op jit(solution)/shard_map/reduce_scatter | solution.py:144
  196.5 10.4 %copy-start.3 = (f32[192]{0:T(256)S(1)}, f32[192]{0:T(256)}, u32[]{:S(2)}) copy-start(f32[192]{0:T(256)} %param.15) | copy-start | bytes 2308
  196.5 10.6 %copy-start.4 = (f32[240]{0:T(256)S(1)}, f32[240]{0:T(256)}, u32[]{:S(2)}) copy-start(f32[240]{0:T(256)} %param.14) | copy-start | bytes 2884
  196.5 10.9 %copy-start.5 = (s32[192]{0:T(256)S(1)}, s32[192]{0:T(256)}, u32[]{:S(2)}) copy-start(s32[192]{0:T(256)} %param.13) | copy-start | bytes 2308
  196.5 11.1 %copy-start.6 = (s32[240]{0:T(256)S(1)}, s32[240]{0:T(256)}, u32[]{:S(2)}) copy-start(s32[240]{0:T(256)} %param.12) | copy-start | bytes 2884
  264.0 24.0 %collective-permute-start.6 = (bf16[960,128]{1,0:T(8,128)(2,1)S(1)}, bf16[960,128]{1,0:T(8,128)(2,1)S(1)}, u32[]{:S(2)}, u32[]{:S(2)}) collective-permute-start(bf16[960,128]{1,0:T(8,128)(2,1)S(1)} %fusion.2), channel_id=1, source_target_pairs={{0,0},{1,32},{2,64},{3,96},{4,128},{5,160},{6,192},{7,224},{32,1},... | collective-permute-start | bytes 737288 | tf_op jit(solution)/shard_map/ppermute | solution.py:162
Sparse Core Ops, SparseCore 0:
  179.9 38.0 reduce-scatter.4
  220.6 41.9 reduce-scatter.2

commit v10 on v8

--- a/solution.py
+++ b/solution.py
@@ -69,8 +69,8 @@
 
 
 def chunk_widths(total):
-    first = total * 5 // 8
-    return [first, total - first]
+    last = total * 4 // 15
+    return [total - last, last]
 
 
 def swap_perm(nz, nc):

time: 250 us -> 260 us (1.040)
  local copies, waits for them, and re-layouts: 3.47 us -> 19.8 us
  waiting for transfers between devices: 153 us -> 146 us
    pallas_call x0 -> x1, local copies, waits for them, and re-layouts: none -> 8.3 us  [stack_chunk(): pl.pallas_call(functools.partial(stack_kernel, start, width, block), out_...]
    all_to_all x0 -> x1, local copies, waits for them, and re-layouts: none -> 8.28 us  [local(): lax.all_to_all(piece, (X, C, Y), split_axis=0, concat_axis=0, tiled=True)]
    all_to_all x2, waiting for transfers between devices: 90 us -> 82 us  [local(): lax.all_to_all(piece, (X, C, Y), split_axis=0, concat_axis=0, tiled=True)]
  transfers between devices with their start and end apart: 7 -> 7, of which waited for: 5 -> 5; matrix products, arithmetic and copies ran while one was open for 1% -> 7% of each run, Pallas kernels for 17% -> 16%
where the time goes in v10:
time: 260 us; the launch traced here: 259 us
  waiting for transfers between devices  146 us (56%)
  Pallas kernels  41.4 us (16%)
  starting transfers between devices  31.8 us (12%)
  local copies, waits for them, and re-layouts  19.8 us (8%)
  between operations  13.3 us (5%)
  other arithmetic  6.29 us (2%)
    all_to_all x2, waiting for transfers between devices, local(): lax.all_to_all(piece, (X, C, Y), split_axis=0, concat_axis=0, tiled=True)  82 us
    reduce_scatter x2, waiting for transfers between devices, local(): lax.psum_scatter(partial_value, Z, scatter_dimension=1, tiled=True)  42.2 us
    pallas_call x2, Pallas kernels, stack_chunk(): pl.pallas_call(functools.partial(stack_kernel, start, width, block), out_...  23.1 us
    pallas_call x2, Pallas kernels, product(): pl.pallas_call(product_kernel, out_shape=jax.ShapeDtypeStruct((rows, widt...  18.3 us
    ppermute x1, waiting for transfers between devices, local(): return lax.ppermute(out, (Z, X, C), perm)  16.4 us
    all_to_all x2, starting transfers between devices, local(): lax.all_to_all(piece, (X, C, Y), split_axis=0, concat_axis=0, tiled=True)  16.2 us
    pallas_call x1, local copies, waits for them, and re-layouts, stack_chunk(): pl.pallas_call(functools.partial(stack_kernel, start, width, block), out_...  8.3 us
    all_to_all x1, local copies, waits for them, and re-layouts, local(): lax.all_to_all(piece, (X, C, Y), split_axis=0, concat_axis=0, tiled=True)  8.28 us
  transfers between devices with their start and end apart: 7, of which 5 were waited for; matrix products, arithmetic and copies ran while one was open for 7% of the time, Pallas kernels for 16%

profile of v10, /device:TPU:7, one launch (start us, length us, event | category | flops | bytes accessed | tf_op | source)
XLA Modules:
  0.0 259.1 jit_solution(11170020725267494136)
XLA Ops:
  6.5 0.0 copy-start.5
  6.5 0.0 all-gather.2.cloned.1.call-start
  6.5 0.7 convert_element_type.10
  7.3 0.2 broadcast_in_dim.140
  7.5 0.3 reshape.123
  7.8 0.1 constant_dynamic-slice_fusion
  7.8 0.1 mul.41
  7.9 0.5 copy.17
  8.5 2.6 %dynamic-slice_multiply_fusion = bf16[480,1024]{1,0:T(8,128)(2,1)} fusion(bf16[480,1024]{1,0:T(8,128)(2,1)S(1)} %copy.17, bf16[3840,1024]{1,0:T(8,128)(2,1)} %param.9, s32[]{:T(128)S(6)} %select_n.113), kind=kLoop, calls=%fused_computation.1 | loop fusion | flops 1966080 | bytes 2949124 | tf_op jit(solution)/shard_map/mul | solution.py:99
  11.1 0.0 all-gather.2.cloned.1.call-update
  11.1 0.0 copy-done.5
  11.1 8.0 %collective-permute-start = (bf16[960,128]{1,0:T(8,128)(2,1)S(1)}, bf16[960,128]{1,0:T(8,128)(2,1)S(1)}, u32[]{:S(2)}, u32[]{:S(2)}) collective-permute-start(bf16[960,128]{1,0:T(8,128)(2,1)S(1)} %copy-done.5), channel_id=1, source_target_pairs={{0,0},{1,32},{2,64},{3,96},{4,128},{5,160},{6,192},{7,224},{32,1},... | collective-permute-start | bytes 737288 | tf_op jit(solution)/shard_map/ppermute | solution.py:106
  19.1 11.1 %shard_map.82 = bf16[32,120,256]{2,1,0:T(8,128)(2,1)} custom-call(bf16[120,30720]{1,0:T(8,128)(2,1)} %in_ref.3), custom_call_target="tpu_custom_call" | custom-call | tf_op jit(solution)/shard_map/pallas_call | solution.py:62
  30.2 5.8 %collective-permute-done = bf16[960,128]{1,0:T(8,128)(2,1)S(1)} collective-permute-done((bf16[960,128]{1,0:T(8,128)(2,1)S(1)}, bf16[960,128]{1,0:T(8,128)(2,1)S(1)}, u32[]{:S(2)}, u32[]{:S(2)}) %collective-permute-start) | collective-permute-done | bytes 245792 | tf_op jit(solution)/shard_map/ppermute | solution.py:106
  36.0 7.1 %all-to-all-start.1 = ((bf16[32,120,256]{2,1,0:T(8,128)(2,1)}), bf16[32,120,256]{2,1,0:T(8,128)(2,1)S(1)}, u32[]{:S(2)}, u32[]{:S(2)}) async-start(bf16[32,120,256]{2,1,0:T(8,128)(2,1)} %shard_map.82), calls=%async_computation.2 | async-start | bytes 3932160 | tf_op jit(solution)/shard_map/all_to_all | solution.py:114
  43.1 12.0 %shard_map.83 = bf16[32,120,704]{2,1,0:T(8,128)(2,1)} custom-call(bf16[120,30720]{1,0:T(8,128)(2,1)} %in_ref.3), custom_call_target="tpu_custom_call" | custom-call | tf_op jit(solution)/shard_map/pallas_call | solution.py:62
  55.1 8.3 %copy.15 = bf16[32,120,704]{1,2,0:T(8,128)(2,1)} copy(bf16[32,120,704]{2,1,0:T(8,128)(2,1)} %shard_map.83) | data formatting | bytes 10813440 | tf_op jit(solution)/shard_map/pallas_call | solution.py:62
  63.4 19.7 %all-to-all-done.1 = bf16[32,120,256]{2,1,0:T(8,128)(2,1)S(1)} async-done(((bf16[32,120,256]{2,1,0:T(8,128)(2,1)}), bf16[32,120,256]{2,1,0:T(8,128)(2,1)S(1)}, u32[]{:S(2)}, u32[]{:S(2)}) %all-to-all-start.1) | async-done | bytes 1966112 | tf_op jit(solution)/shard_map/all_to_all | solution.py:114
  83.1 0.0 copy-start
  83.1 1.4 copy-done
  84.5 9.1 %all-to-all-start = ((bf16[32,120,704]{1,2,0:T(8,128)(2,1)}), bf16[32,120,704]{1,2,0:T(8,128)(2,1)}, u32[]{:S(2)}, u32[]{:S(2)}) async-start(bf16[32,120,704]{1,2,0:T(8,128)(2,1)} %copy.15), calls=%async_computation | async-start | bytes 11534336 | tf_op jit(solution)/shard_map/all_to_all | solution.py:114
  93.6 0.0 reduce-scatter.5.cloned.1.call-start
  93.6 0.0 all-gather.2.cloned.1.call-done.right_ref
  93.6 6.9 %shard_map.85 = f32[256,1024]{1,0:T(8,128)} custom-call(bf16[3840,256]{1,0:T(8,128)(2,1)} %bitcast.5, bf16[3840,1024]{1,0:T(8,128)(2,1)} %all-gather.2.cloned.1.call-done.right_ref), custom_call_target="tpu_custom_call" | custom-call | flops 2013265920 | bytes 10878976 | tf_op jit(solution)/shard_map/pallas_call | solution.py:37
  100.5 0.0 reduce-scatter.5.cloned.1.call-update
  100.5 0.0 reduce-scatter.3.cloned.1.call-start
  100.6 62.3 %all-to-all-done = bf16[32,120,704]{1,2,0:T(8,128)(2,1)} async-done(((bf16[32,120,704]{1,2,0:T(8,128)(2,1)}), bf16[32,120,704]{1,2,0:T(8,128)(2,1)}, u32[]{:S(2)}, u32[]{:S(2)}) %all-to-all-start) | async-done | bytes 5406752 | tf_op jit(solution)/shard_map/all_to_all | solution.py:114
  162.9 8.3 %copy.16 = bf16[32,120,704]{2,1,0:T(8,128)(2,1)} copy(bf16[32,120,704]{1,2,0:T(8,128)(2,1)} %all-to-all-done) | data formatting | bytes 10813440 | tf_op jit(solution)/shard_map/all_to_all | solution.py:114
  171.2 0.0 copy-start.1
  171.2 0.0 copy-start.2
  171.2 0.0 copy-start.3
  171.2 0.0 copy-start.4
  171.2 11.4 %shard_map.84 = f32[704,1024]{1,0:T(8,128)} custom-call(bf16[3840,704]{1,0:T(8,128)(2,1)} %bitcast.6, bf16[3840,1024]{1,0:T(8,128)(2,1)} %all-gather.2.cloned.1.call-done.right_ref), custom_call_target="tpu_custom_call" | custom-call | flops 5536481280 | bytes 16154624 | tf_op jit(solution)/shard_map/pallas_call | solution.py:37
  182.6 0.0 reduce-scatter.3.cloned.1.call-update
  182.7 0.0 copy-done.1
  182.7 0.2 select_reduce_fusion.2
  182.9 0.0 copy-done.2
  182.9 0.4 select_reduce_fusion
  183.3 0.0 copy-done.3
  183.3 0.2 select_reduce_fusion.3
  183.4 0.0 copy-done.4
  183.5 0.4 select_reduce_fusion.1
  183.9 0.1 select_reduce_fusion.6
  184.0 0.1 select_reduce_fusion.4
  184.1 0.1 select_reduce_fusion.7
  184.2 0.1 select_reduce_fusion.5
  184.3 0.0 reduce-scatter.5.cloned.1.call-done
  184.3 42.2 %reduce-scatter.3.cloned.1.call-done = f32[704,128]{1,0:T(8,128)} async-done(((f32[704,1024]{1,0:T(8,128)}), f32[704,128]{1,0:T(8,128)}) %reduce-scatter.3.cloned.1.call-update) | async-done | bytes 360464 | tf_op jit(solution)/shard_map/reduce_scatter | solution.py:116
  226.5 1.4 fusion.2
  227.9 7.6 %collective-permute-start.1 = (bf16[960,128]{1,0:T(8,128)(2,1)S(1)}, bf16[960,128]{1,0:T(8,128)(2,1)S(1)}, u32[]{:S(2)}, u32[]{:S(2)}) collective-permute-start(bf16[960,128]{1,0:T(8,128)(2,1)S(1)} %fusion.2), channel_id=1, source_target_pairs={{0,0},{1,32},{2,64},{3,96},{4,128},{5,160},{6,192},{7,224},{32,1},... | collective-permute-start | bytes 737288 | tf_op jit(solution)/shard_map/ppermute | solution.py:134
  235.5 16.4 %collective-permute-done.1 = bf16[960,128]{1,0:T(8,128)(2,1)S(1)} collective-permute-done((bf16[960,128]{1,0:T(8,128)(2,1)S(1)}, bf16[960,128]{1,0:T(8,128)(2,1)S(1)}, u32[]{:S(2)}, u32[]{:S(2)}) %collective-permute-start.1) | collective-permute-done | bytes 245792 | tf_op jit(solution)/shard_map/ppermute | solution.py:134
  251.8 0.7 copy.19
  (6 shorter events, 0.1 us)
Async XLA Ops:
  6.5 4.6 %copy-start.5 = (bf16[960,128]{1,0:T(8,128)(2,1)S(1)}, bf16[960,128]{1,0:T(8,128)(2,1)}, u32[]{:S(2)}) copy-start(bf16[960,128]{1,0:T(8,128)(2,1)} %param.11) | copy-start | bytes 737284
  6.5 87.1 %all-gather.2.cloned.1.call-start = ((), (), s32[]{:S(2)}) async-start(), calls=%async_computation.4 | async-start | bytes 8847360 | tf_op jit(solution)/shard_map/all_gather | solution.py:101
  11.1 24.9 %collective-permute-start = (bf16[960,128]{1,0:T(8,128)(2,1)S(1)}, bf16[960,128]{1,0:T(8,128)(2,1)S(1)}, u32[]{:S(2)}, u32[]{:S(2)}) collective-permute-start(bf16[960,128]{1,0:T(8,128)(2,1)S(1)} %copy-done.5), channel_id=1, source_target_pairs={{0,0},{1,32},{2,64},{3,96},{4,128},{5,160},{6,192},{7,224},{32,1},... | collective-permute-start | bytes 737288 | tf_op jit(solution)/shard_map/ppermute | solution.py:106
  36.0 47.1 %all-to-all-start.1 = ((bf16[32,120,256]{2,1,0:T(8,128)(2,1)}), bf16[32,120,256]{2,1,0:T(8,128)(2,1)S(1)}, u32[]{:S(2)}, u32[]{:S(2)}) async-start(bf16[32,120,256]{2,1,0:T(8,128)(2,1)} %shard_map.82), calls=%async_computation.2 | async-start | bytes 3932160 | tf_op jit(solution)/shard_map/all_to_all | solution.py:114
  83.1 1.4 copy-start
  84.5 78.4 %all-to-all-start = ((bf16[32,120,704]{1,2,0:T(8,128)(2,1)}), bf16[32,120,704]{1,2,0:T(8,128)(2,1)}, u32[]{:S(2)}, u32[]{:S(2)}) async-start(bf16[32,120,704]{1,2,0:T(8,128)(2,1)} %copy.15), calls=%async_computation | async-start | bytes 11534336 | tf_op jit(solution)/shard_map/all_to_all | solution.py:114
  93.6 90.8 %reduce-scatter.5.cloned.1.call-start = ((), (), s32[]{:S(2)}) async-start(), calls=%async_computation.6 | async-start | bytes 1179648 | tf_op jit(solution)/shard_map/reduce_scatter | solution.py:116
  100.5 126.0 %reduce-scatter.3.cloned.1.call-start = ((), (), s32[]{:S(2)}) async-start(), calls=%async_computation.5 | async-start | bytes 3244032 | tf_op jit(solution)/shard_map/reduce_scatter | solution.py:116
  171.2 11.5 %copy-start.1 = (f32[192]{0:T(256)S(1)}, f32[192]{0:T(256)}, u32[]{:S(2)}) copy-start(f32[192]{0:T(256)} %param.15) | copy-start | bytes 2308
  171.2 11.7 %copy-start.2 = (f32[240]{0:T(256)S(1)}, f32[240]{0:T(256)}, u32[]{:S(2)}) copy-start(f32[240]{0:T(256)} %param.14) | copy-start | bytes 2884
  171.2 12.0 %copy-start.3 = (s32[192]{0:T(256)S(1)}, s32[192]{0:T(256)}, u32[]{:S(2)}) copy-start(s32[192]{0:T(256)} %param.13) | copy-start | bytes 2308
  171.2 12.2 %copy-start.4 = (s32[240]{0:T(256)S(1)}, s32[240]{0:T(256)}, u32[]{:S(2)}) copy-start(s32[240]{0:T(256)} %param.12) | copy-start | bytes 2884
  227.9 23.9 %collective-permute-start.1 = (bf16[960,128]{1,0:T(8,128)(2,1)S(1)}, bf16[960,128]{1,0:T(8,128)(2,1)S(1)}, u32[]{:S(2)}, u32[]{:S(2)}) collective-permute-start(bf16[960,128]{1,0:T(8,128)(2,1)S(1)} %fusion.2), channel_id=1, source_target_pairs={{0,0},{1,32},{2,64},{3,96},{4,128},{5,160},{6,192},{7,224},{32,1},... | collective-permute-start | bytes 737288 | tf_op jit(solution)/shard_map/ppermute | solution.py:134
Sparse Core Ops, SparseCore 0:
  11.2 75.6 all-gather.1
  100.7 36.2 reduce-scatter.4
  182.8 43.7 reduce-scatter.2

commit v11 on v8

--- a/solution.py
+++ b/solution.py
@@ -110,7 +110,10 @@
         piece = stack_chunk(amps, groups, start, width)
         start += width
         if k == 1:
-            coulomb_here, piece = lax.optimization_barrier((coulomb_here, piece))
+            coulomb_here, piece, partial_value = lax.optimization_barrier(
+                (coulomb_here, piece, partial_value)
+            )
+            sums[-1] = lax.psum_scatter(partial_value, Z, scatter_dimension=1, tiled=True)
         plane_amps = lax.all_to_all(piece, (X, C, Y), split_axis=0, concat_axis=0, tiled=True)
         partial_value = product(plane_amps.reshape(groups * sub, width), masked_all)
         sums.append(lax.psum_scatter(partial_value, Z, scatter_dimension=1, tiled=True))

time: 250 us -> 258 us (1.032)
  blocking collectives: 0 us -> 49.7 us
  waiting for transfers between devices: 153 us -> 122 us
  starting transfers between devices: 31.7 us -> 23 us
    all_to_all x0 -> x1, blocking collectives: none -> 49.7 us  [local(): lax.all_to_all(piece, (X, C, Y), split_axis=0, concat_axis=0, tiled=True)]
    all_to_all x2 -> x1, waiting for transfers between devices: 90 us -> 69.8 us  [local(): lax.all_to_all(piece, (X, C, Y), split_axis=0, concat_axis=0, tiled=True)]
    all_to_all x2 -> x1, starting transfers between devices: 15.7 us -> 8.11 us  [local(): lax.all_to_all(piece, (X, C, Y), split_axis=0, concat_axis=0, tiled=True)]
    reduce_scatter x2, waiting for transfers between devices: 41.4 us -> 34.3 us  [local(): lax.psum_scatter(partial_value, Z, scatter_dimension=1, tiled=True)]
    ppermute x1, waiting for transfers between devices: 5.42 us -> 0.01 us  [local(): coulomb_here = lax.ppermute(coulomb, (Z, X, C), perm)]
  transfers between devices with their start and end apart: 7 -> 6, of which waited for: 5 -> 4; matrix products, arithmetic and copies ran while one was open for 1% -> 1% of each run, Pallas kernels for 17% -> 16%
where the time goes in v11:
time: 258 us
  waiting for transfers between devices  122 us (47%)
  blocking collectives  49.7 us (19%)
  Pallas kernels  41.3 us (16%)
  starting transfers between devices  23 us (9%)
  between operations  13.3 us (5%)
  other arithmetic  6.2 us (2%)
    all_to_all x1, waiting for transfers between devices, local(): lax.all_to_all(piece, (X, C, Y), split_axis=0, concat_axis=0, tiled=True)  69.8 us
    all_to_all x1, blocking collectives, local(): lax.all_to_all(piece, (X, C, Y), split_axis=0, concat_axis=0, tiled=True)  49.7 us
    reduce_scatter x2, waiting for transfers between devices, local(): lax.psum_scatter(partial_value, Z, scatter_dimension=1, tiled=True)  34.3 us
    pallas_call x2, Pallas kernels, stack_chunk(): pl.pallas_call(functools.partial(stack_kernel, start, width, block), out_...  23 us
    pallas_call x2, Pallas kernels, product(): pl.pallas_call(product_kernel, out_shape=jax.ShapeDtypeStruct((rows, widt...  18.3 us
    ppermute x1, waiting for transfers between devices, local(): return lax.ppermute(out, (Z, X, C), perm)  16.1 us
    all_to_all x1, starting transfers between devices, local(): lax.all_to_all(piece, (X, C, Y), split_axis=0, concat_axis=0, tiled=True)  8.11 us
    ppermute x1, starting transfers between devices, local(): coulomb_here = lax.ppermute(coulomb, (Z, X, C), perm)  7.42 us
  transfers between devices with their start and end apart: 6, of which 4 were waited for; matrix products, arithmetic and copies ran while one was open for 1% of the time, Pallas kernels for 16%

profile of v11, /device:TPU:7, one launch (start us, length us, event | category | flops | bytes accessed | tf_op | source)
XLA Modules:
  0.0 257.5 jit_solution(4211344670799504412)
XLA Ops:
  6.5 0.0 all-gather.2.cloned.1.call-start
  6.5 0.7 convert_element_type.9
  7.2 0.2 broadcast_in_dim.140
  7.4 0.3 reshape.123
  7.7 0.1 constant_dynamic-slice_fusion
  7.8 0.1 mul.41
  7.9 0.5 copy.12
  8.4 2.5 dynamic-slice_multiply_fusion
  11.0 0.0 all-gather.2.cloned.1.call-update
  11.0 11.6 %shard_map.83 = bf16[32,120,600]{2,1,0:T(8,128)(2,1)} custom-call(bf16[120,30720]{1,0:T(8,128)(2,1)} %in_ref.3), custom_call_target="tpu_custom_call" | custom-call | tf_op jit(solution)/shard_map/pallas_call | solution.py:62
  22.6 0.0 copy-start.5
  22.6 8.1 %all-to-all-start = ((bf16[32,120,600]{2,1,0:T(8,128)(2,1)}), bf16[32,120,600]{2,1,0:T(8,128)(2,1)}, u32[]{:S(2)}, u32[]{:S(2)}) async-start(bf16[32,120,600]{2,1,0:T(8,128)(2,1)} %shard_map.83), calls=%async_computation | async-start | bytes 9830400 | tf_op jit(solution)/shard_map/all_to_all | solution.py:117
  30.7 0.0 reduce-scatter.3.cloned.1.call-start
  30.8 0.0 copy-done.5
  30.8 7.4 %collective-permute-start = (bf16[960,128]{1,0:T(8,128)(2,1)S(1)}, bf16[960,128]{1,0:T(8,128)(2,1)S(1)}, u32[]{:S(2)}, u32[]{:S(2)}) collective-permute-start(bf16[960,128]{1,0:T(8,128)(2,1)S(1)} %copy-done.5), channel_id=1, source_target_pairs={{0,0},{1,32},{2,64},{3,96},{4,128},{5,160},{6,192},{7,224},{32,1},... | collective-permute-start | bytes 737288 | tf_op jit(solution)/shard_map/ppermute | solution.py:106
  38.2 11.4 %shard_map.82 = bf16[32,120,360]{2,1,0:T(8,128)(2,1)} custom-call(bf16[120,30720]{1,0:T(8,128)(2,1)} %in_ref.3), custom_call_target="tpu_custom_call" | custom-call | tf_op jit(solution)/shard_map/pallas_call | solution.py:62
  49.6 69.8 %all-to-all-done = bf16[32,120,600]{2,1,0:T(8,128)(2,1)} async-done(((bf16[32,120,600]{2,1,0:T(8,128)(2,1)}), bf16[32,120,600]{2,1,0:T(8,128)(2,1)}, u32[]{:S(2)}, u32[]{:S(2)}) %all-to-all-start) | async-done | bytes 4608032 | tf_op jit(solution)/shard_map/all_to_all | solution.py:117
  119.4 1.9 all-gather.2.cloned.1.call-done.right_ref
  121.3 0.0 copy-start
  121.3 10.3 %shard_map.84 = f32[600,1024]{1,0:T(8,128)} custom-call(bf16[3840,600]{1,0:T(8,128)(2,1)} %bitcast.left_ref, bf16[3840,1024]{1,0:T(8,128)(2,1)} %all-gather.2.cloned.1.call-done.right_ref), custom_call_target="tpu_custom_call" | custom-call | flops 4718592000 | bytes 14929920 | tf_op jit(solution)/shard_map/pallas_call | solution.py:37
  131.6 0.0 collective-permute-done
  131.6 0.0 reduce-scatter.3.cloned.1.call-update
  131.6 0.0 reduce-scatter.5.cloned.1.call-start
  131.7 0.0 copy-done
  131.7 49.7 %all_to_all.10 = bf16[32,120,360]{2,1,0:T(8,128)(2,1)} all-to-all(bf16[32,120,360]{2,1,0:T(8,128)(2,1)S(1)} %copy-done), channel_id=1, replica_groups=mesh['z'=8,'y'=4,'x'=4,'core'=2] {'x','core','y'}, dimensions={0} | all-to-all | bytes 5529600 | tf_op jit(solution)/shard_map/all_to_all | solution.py:117
  181.4 0.0 copy-start.1
  181.4 0.0 copy-start.2
  181.4 0.0 copy-start.3
  181.4 0.0 copy-start.4
  181.4 8.0 %shard_map.85 = f32[360,1024]{1,0:T(8,128)} custom-call(bf16[3840,360]{1,0:T(8,128)(2,1)} %bitcast.5, bf16[3840,1024]{1,0:T(8,128)(2,1)} %all-gather.2.cloned.1.call-done.right_ref), custom_call_target="tpu_custom_call" | custom-call | flops 2831155200 | bytes 12103680 | tf_op jit(solution)/shard_map/pallas_call | solution.py:37
  189.4 0.0 reduce-scatter.5.cloned.1.call-update
  189.4 0.0 copy-done.1
  189.5 0.2 select_reduce_fusion.2
  189.6 0.0 copy-done.2
  189.7 0.4 select_reduce_fusion
  190.0 0.0 copy-done.3
  190.0 0.2 select_reduce_fusion.3
  190.2 0.0 copy-done.4
  190.2 0.4 select_reduce_fusion.1
  190.6 0.1 select_reduce_fusion.6
  190.7 0.1 select_reduce_fusion.4
  190.9 0.1 select_reduce_fusion.7
  191.0 0.1 select_reduce_fusion.5
  191.1 0.0 reduce-scatter.3.cloned.1.call-done
  191.1 34.3 %reduce-scatter.5.cloned.1.call-done = f32[360,128]{1,0:T(8,128)} async-done(((f32[360,1024]{1,0:T(8,128)}), f32[360,128]{1,0:T(8,128)}) %reduce-scatter.5.cloned.1.call-update) | async-done | bytes 184336 | tf_op jit(solution)/shard_map/reduce_scatter | solution.py:119
  225.4 1.4 fusion.2
  226.8 7.4 %collective-permute-start.1 = (bf16[960,128]{1,0:T(8,128)(2,1)S(1)}, bf16[960,128]{1,0:T(8,128)(2,1)S(1)}, u32[]{:S(2)}, u32[]{:S(2)}) collective-permute-start(bf16[960,128]{1,0:T(8,128)(2,1)S(1)} %fusion.2), channel_id=1, source_target_pairs={{0,0},{1,32},{2,64},{3,96},{4,128},{5,160},{6,192},{7,224},{32,1},... | collective-permute-start | bytes 737288 | tf_op jit(solution)/shard_map/ppermute | solution.py:137
  234.2 16.1 %collective-permute-done.1 = bf16[960,128]{1,0:T(8,128)(2,1)S(1)} collective-permute-done((bf16[960,128]{1,0:T(8,128)(2,1)S(1)}, bf16[960,128]{1,0:T(8,128)(2,1)S(1)}, u32[]{:S(2)}, u32[]{:S(2)}) %collective-permute-start.1) | collective-permute-done | bytes 245792 | tf_op jit(solution)/shard_map/ppermute | solution.py:137
  250.3 0.7 copy.14
  (6 shorter events, 0.1 us)
Async XLA Ops:
  6.5 114.8 %all-gather.2.cloned.1.call-start = ((), (), s32[]{:S(2)}) async-start(), calls=%async_computation.4 | async-start | bytes 8847360 | tf_op jit(solution)/shard_map/all_gather | solution.py:101
  22.6 8.2 %copy-start.5 = (bf16[960,128]{1,0:T(8,128)(2,1)S(1)}, bf16[960,128]{1,0:T(8,128)(2,1)}, u32[]{:S(2)}) copy-start(bf16[960,128]{1,0:T(8,128)(2,1)} %param.11) | copy-start | bytes 737284
  22.6 96.8 %all-to-all-start = ((bf16[32,120,600]{2,1,0:T(8,128)(2,1)}), bf16[32,120,600]{2,1,0:T(8,128)(2,1)}, u32[]{:S(2)}, u32[]{:S(2)}) async-start(bf16[32,120,600]{2,1,0:T(8,128)(2,1)} %shard_map.83), calls=%async_computation | async-start | bytes 9830400 | tf_op jit(solution)/shard_map/all_to_all | solution.py:117
  30.7 160.4 %reduce-scatter.3.cloned.1.call-start = ((), (), s32[]{:S(2)}) async-start(), calls=%async_computation.5 | async-start | bytes 2764800 | tf_op jit(solution)/shard_map/reduce_scatter | solution.py:116
  30.8 100.8 %collective-permute-start = (bf16[960,128]{1,0:T(8,128)(2,1)S(1)}, bf16[960,128]{1,0:T(8,128)(2,1)S(1)}, u32[]{:S(2)}, u32[]{:S(2)}) collective-permute-start(bf16[960,128]{1,0:T(8,128)(2,1)S(1)} %copy-done.5), channel_id=1, source_target_pairs={{0,0},{1,32},{2,64},{3,96},{4,128},{5,160},{6,192},{7,224},{32,1},... | collective-permute-start | bytes 737288 | tf_op jit(solution)/shard_map/ppermute | solution.py:106
  121.3 10.4 %copy-start = (bf16[32,120,360]{2,1,0:T(8,128)(2,1)S(1)}, bf16[32,120,360]{2,1,0:T(8,128)(2,1)}, u32[]{:S(2)}) copy-start(bf16[32,120,360]{2,1,0:T(8,128)(2,1)} %shard_map.82) | copy-start | bytes 8294404
  131.6 93.8 %reduce-scatter.5.cloned.1.call-start = ((), (), s32[]{:S(2)}) async-start(), calls=%async_computation.6 | async-start | bytes 1658880 | tf_op jit(solution)/shard_map/reduce_scatter | solution.py:119
  181.4 8.1 %copy-start.1 = (f32[192]{0:T(256)S(1)}, f32[192]{0:T(256)}, u32[]{:S(2)}) copy-start(f32[192]{0:T(256)} %param.15) | copy-start | bytes 2308
  181.4 8.3 %copy-start.2 = (f32[240]{0:T(256)S(1)}, f32[240]{0:T(256)}, u32[]{:S(2)}) copy-start(f32[240]{0:T(256)} %param.14) | copy-start | bytes 2884
  181.4 8.6 %copy-start.3 = (s32[192]{0:T(256)S(1)}, s32[192]{0:T(256)}, u32[]{:S(2)}) copy-start(s32[192]{0:T(256)} %param.13) | copy-start | bytes 2308
  181.4 8.8 %copy-start.4 = (s32[240]{0:T(256)S(1)}, s32[240]{0:T(256)}, u32[]{:S(2)}) copy-start(s32[240]{0:T(256)} %param.12) | copy-start | bytes 2884
  226.8 23.5 %collective-permute-start.1 = (bf16[960,128]{1,0:T(8,128)(2,1)S(1)}, bf16[960,128]{1,0:T(8,128)(2,1)S(1)}, u32[]{:S(2)}, u32[]{:S(2)}) collective-permute-start(bf16[960,128]{1,0:T(8,128)(2,1)S(1)} %fusion.2), channel_id=1, source_target_pairs={{0,0},{1,32},{2,64},{3,96},{4,128},{5,160},{6,192},{7,224},{32,1},... | collective-permute-start | bytes 737288 | tf_op jit(solution)/shard_map/ppermute | solution.py:137
Sparse Core Ops, SparseCore 0:
  11.1 110.1 all-gather.1
  131.7 48.0 reduce-scatter.2
  189.5 35.8 reduce-scatter.4

commit v12 on v8

--- a/solution.py
+++ b/solution.py
@@ -52,19 +52,20 @@
 
 
 def stack_kernel(start, width, block, in_ref, out_ref):
-    for half in range(2):
-        out_ref[half] = in_ref[:, half * block + start:half * block + start + width]
+    for g in range(out_ref.shape[0]):
+        out_ref[g] = in_ref[:, g * block + start:g * block + start + width]
 
 
 def stack_chunk(amps, groups, start, width):
     sub, total = amps.shape
     block = total // groups
+    step = 8
     return pl.pallas_call(
         functools.partial(stack_kernel, start, width, block),
         out_shape=jax.ShapeDtypeStruct((groups, sub, width), amps.dtype),
-        grid=(groups // 2,),
-        in_specs=[pl.BlockSpec((sub, 2 * block), lambda h: (0, h))],
-        out_specs=pl.BlockSpec((2, sub, width), lambda h: (h, 0, 0)),
+        grid=(groups // step,),
+        in_specs=[pl.BlockSpec((sub, step * block), lambda h: (0, h))],
+        out_specs=pl.BlockSpec((step, sub, width), lambda h: (h, 0, 0)),
     )(amps)
 
 

time: 250 us -> 250 us (level)
  waiting for transfers between devices: 153 us -> 165 us
  Pallas kernels: 41.5 us -> 30.2 us
    pallas_call x2, Pallas kernels: 23.3 us -> 12 us  [stack_chunk(): pl.pallas_call(functools.partial(stack_kernel, start, width, block), out_...]
    ppermute x1, waiting for transfers between devices: 5.42 us -> 11.2 us  [local(): coulomb_here = lax.ppermute(coulomb, (Z, X, C), perm)]
    all_to_all x2, waiting for transfers between devices: 90 us -> 95.5 us  [local(): lax.all_to_all(piece, (X, C, Y), split_axis=0, concat_axis=0, tiled=True)]
  transfers between devices with their start and end apart: 7 -> 7, of which waited for: 5 -> 5; matrix products, arithmetic and copies ran while one was open for 1% -> 1% of each run, Pallas kernels for 17% -> 12%
where the time goes in v12:
time: 250 us; the launch traced here: 249 us
  waiting for transfers between devices  165 us (66%)
  starting transfers between devices  31.3 us (13%)
  Pallas kernels  30.2 us (12%)
  between operations  13.3 us (5%)
  other arithmetic  6.2 us (2%)
  local copies, waits for them, and re-layouts  3.47 us (1%)
    all_to_all x2, waiting for transfers between devices, local(): lax.all_to_all(piece, (X, C, Y), split_axis=0, concat_axis=0, tiled=True)  95.5 us
    reduce_scatter x2, waiting for transfers between devices, local(): lax.psum_scatter(partial_value, Z, scatter_dimension=1, tiled=True)  41.6 us
    pallas_call x2, Pallas kernels, product(): pl.pallas_call(product_kernel, out_shape=jax.ShapeDtypeStruct((rows, widt...  18.2 us
    ppermute x1, waiting for transfers between devices, local(): return lax.ppermute(out, (Z, X, C), perm)  16.5 us
    all_to_all x2, starting transfers between devices, local(): lax.all_to_all(piece, (X, C, Y), split_axis=0, concat_axis=0, tiled=True)  15.7 us
    pallas_call x2, Pallas kernels, stack_chunk(): pl.pallas_call(functools.partial(stack_kernel, start, width, block), out_...  12 us
    ppermute x1, waiting for transfers between devices, local(): coulomb_here = lax.ppermute(coulomb, (Z, X, C), perm)  11.2 us
    ppermute x1, starting transfers between devices, local(): coulomb_here = lax.ppermute(coulomb, (Z, X, C), perm)  7.96 us
  transfers between devices with their start and end apart: 7, of which 5 were waited for; matrix products, arithmetic and copies ran while one was open for 1% of the time, Pallas kernels for 12%

profile of v12, /device:TPU:7, one launch (start us, length us, event | category | flops | bytes accessed | tf_op | source)
XLA Modules:
  0.0 249.4 jit_solution(5653516560237870637)
XLA Ops:
  6.5 0.0 all-gather.2.cloned.1.call-start
  6.5 0.7 convert_element_type.10
  7.2 0.2 broadcast_in_dim.140
  7.4 0.3 reshape.123
  7.7 0.1 constant_dynamic-slice_fusion
  7.8 0.1 mul.41
  7.9 0.0 copy-start.5
  7.9 0.5 copy.12
  8.4 2.5 %dynamic-slice_multiply_fusion = bf16[480,1024]{1,0:T(8,128)(2,1)} fusion(bf16[480,1024]{1,0:T(8,128)(2,1)S(1)} %copy.12, bf16[3840,1024]{1,0:T(8,128)(2,1)} %param.9, s32[]{:T(128)S(6)} %select_n.113), kind=kLoop, calls=%fused_computation.1 | loop fusion | flops 1966080 | bytes 2949124 | tf_op jit(solution)/shard_map/mul | solution.py:100
  11.0 0.0 all-gather.2.cloned.1.call-update
  11.0 0.0 copy-done.5
  11.0 8.0 %collective-permute-start = (bf16[960,128]{1,0:T(8,128)(2,1)S(1)}, bf16[960,128]{1,0:T(8,128)(2,1)S(1)}, u32[]{:S(2)}, u32[]{:S(2)}) collective-permute-start(bf16[960,128]{1,0:T(8,128)(2,1)S(1)} %copy-done.5), channel_id=1, source_target_pairs={{0,0},{1,32},{2,64},{3,96},{4,128},{5,160},{6,192},{7,224},{32,1},... | collective-permute-start | bytes 737288 | tf_op jit(solution)/shard_map/ppermute | solution.py:107
  19.0 5.7 %shard_map.82 = bf16[32,120,360]{2,1,0:T(8,128)(2,1)} custom-call(bf16[120,30720]{1,0:T(8,128)(2,1)} %in_ref.3), custom_call_target="tpu_custom_call" | custom-call | tf_op jit(solution)/shard_map/pallas_call | solution.py:63
  24.7 11.2 %collective-permute-done = bf16[960,128]{1,0:T(8,128)(2,1)S(1)} collective-permute-done((bf16[960,128]{1,0:T(8,128)(2,1)S(1)}, bf16[960,128]{1,0:T(8,128)(2,1)S(1)}, u32[]{:S(2)}, u32[]{:S(2)}) %collective-permute-start) | collective-permute-done | bytes 245792 | tf_op jit(solution)/shard_map/ppermute | solution.py:107
  35.9 7.1 %all-to-all-start.1 = ((bf16[32,120,360]{2,1,0:T(8,128)(2,1)}), bf16[32,120,360]{2,1,0:T(8,128)(2,1)S(1)}, u32[]{:S(2)}, u32[]{:S(2)}) async-start(bf16[32,120,360]{2,1,0:T(8,128)(2,1)} %shard_map.82), calls=%async_computation.2 | async-start | bytes 5898240 | tf_op jit(solution)/shard_map/all_to_all | solution.py:115
  43.0 6.3 %shard_map.83 = bf16[32,120,600]{2,1,0:T(8,128)(2,1)} custom-call(bf16[120,30720]{1,0:T(8,128)(2,1)} %in_ref.3), custom_call_target="tpu_custom_call" | custom-call | tf_op jit(solution)/shard_map/pallas_call | solution.py:63
  49.3 45.1 %all-to-all-done.1 = bf16[32,120,360]{2,1,0:T(8,128)(2,1)S(1)} async-done(((bf16[32,120,360]{2,1,0:T(8,128)(2,1)}), bf16[32,120,360]{2,1,0:T(8,128)(2,1)S(1)}, u32[]{:S(2)}, u32[]{:S(2)}) %all-to-all-start.1) | async-done | bytes 2764832 | tf_op jit(solution)/shard_map/all_to_all | solution.py:115
  94.4 0.0 copy-start
  94.4 1.6 copy-done
  96.0 8.6 %all-to-all-start = ((bf16[32,120,600]{2,1,0:T(8,128)(2,1)}), bf16[32,120,600]{2,1,0:T(8,128)(2,1)}, u32[]{:S(2)}, u32[]{:S(2)}) async-start(bf16[32,120,600]{2,1,0:T(8,128)(2,1)} %shard_map.83), calls=%async_computation | async-start | bytes 9830400 | tf_op jit(solution)/shard_map/all_to_all | solution.py:115
  104.6 0.0 reduce-scatter.5.cloned.1.call-start
  104.7 0.0 all-gather.2.cloned.1.call-done.right_ref
  104.7 8.0 %shard_map.85 = f32[360,1024]{1,0:T(8,128)} custom-call(bf16[3840,360]{1,0:T(8,128)(2,1)} %bitcast.5, bf16[3840,1024]{1,0:T(8,128)(2,1)} %all-gather.2.cloned.1.call-done.right_ref), custom_call_target="tpu_custom_call" | custom-call | flops 2831155200 | bytes 12103680 | tf_op jit(solution)/shard_map/pallas_call | solution.py:37
  112.7 0.0 reduce-scatter.5.cloned.1.call-update
  112.7 0.0 reduce-scatter.3.cloned.1.call-start
  112.7 50.4 %all-to-all-done = bf16[32,120,600]{2,1,0:T(8,128)(2,1)} async-done(((bf16[32,120,600]{2,1,0:T(8,128)(2,1)}), bf16[32,120,600]{2,1,0:T(8,128)(2,1)}, u32[]{:S(2)}, u32[]{:S(2)}) %all-to-all-start) | async-done | bytes 4608032 | tf_op jit(solution)/shard_map/all_to_all | solution.py:115
  163.2 0.0 copy-start.1
  163.2 0.0 copy-start.2
  163.2 0.0 copy-start.3
  163.2 0.0 copy-start.4
  163.2 10.2 %shard_map.84 = f32[600,1024]{1,0:T(8,128)} custom-call(bf16[3840,600]{1,0:T(8,128)(2,1)} %bitcast.left_ref, bf16[3840,1024]{1,0:T(8,128)(2,1)} %all-gather.2.cloned.1.call-done.right_ref), custom_call_target="tpu_custom_call" | custom-call | flops 4718592000 | bytes 14929920 | tf_op jit(solution)/shard_map/pallas_call | solution.py:37
  173.4 0.0 reduce-scatter.3.cloned.1.call-update
  173.4 0.0 copy-done.1
  173.4 0.2 select_reduce_fusion.2
  173.6 0.0 copy-done.2
  173.6 0.4 select_reduce_fusion
  174.0 0.0 copy-done.3
  174.0 0.2 select_reduce_fusion.3
  174.2 0.0 copy-done.4
  174.2 0.4 select_reduce_fusion.1
  174.6 0.1 select_reduce_fusion.6
  174.7 0.1 select_reduce_fusion.4
  174.8 0.1 select_reduce_fusion.7
  174.9 0.1 select_reduce_fusion.5
  175.1 0.0 reduce-scatter.5.cloned.1.call-done
  175.1 41.6 %reduce-scatter.3.cloned.1.call-done = f32[600,128]{1,0:T(8,128)} async-done(((f32[600,1024]{1,0:T(8,128)}), f32[600,128]{1,0:T(8,128)}) %reduce-scatter.3.cloned.1.call-update) | async-done | bytes 307216 | tf_op jit(solution)/shard_map/reduce_scatter | solution.py:117
  216.7 1.4 fusion.2
  218.1 7.5 %collective-permute-start.1 = (bf16[960,128]{1,0:T(8,128)(2,1)S(1)}, bf16[960,128]{1,0:T(8,128)(2,1)S(1)}, u32[]{:S(2)}, u32[]{:S(2)}) collective-permute-start(bf16[960,128]{1,0:T(8,128)(2,1)S(1)} %fusion.2), channel_id=1, source_target_pairs={{0,0},{1,32},{2,64},{3,96},{4,128},{5,160},{6,192},{7,224},{32,1},... | collective-permute-start | bytes 737288 | tf_op jit(solution)/shard_map/ppermute | solution.py:135
  225.6 16.5 %collective-permute-done.1 = bf16[960,128]{1,0:T(8,128)(2,1)S(1)} collective-permute-done((bf16[960,128]{1,0:T(8,128)(2,1)S(1)}, bf16[960,128]{1,0:T(8,128)(2,1)S(1)}, u32[]{:S(2)}, u32[]{:S(2)}) %collective-permute-start.1) | collective-permute-done | bytes 245792 | tf_op jit(solution)/shard_map/ppermute | solution.py:135
  242.2 0.7 copy.14
  (6 shorter events, 0.1 us)
Async XLA Ops:
  6.5 98.1 %all-gather.2.cloned.1.call-start = ((), (), s32[]{:S(2)}) async-start(), calls=%async_computation.4 | async-start | bytes 8847360 | tf_op jit(solution)/shard_map/all_gather | solution.py:102
  7.9 3.1 %copy-start.5 = (bf16[960,128]{1,0:T(8,128)(2,1)S(1)}, bf16[960,128]{1,0:T(8,128)(2,1)}, u32[]{:S(2)}) copy-start(bf16[960,128]{1,0:T(8,128)(2,1)} %param.11) | copy-start | bytes 737284
  11.0 24.9 %collective-permute-start = (bf16[960,128]{1,0:T(8,128)(2,1)S(1)}, bf16[960,128]{1,0:T(8,128)(2,1)S(1)}, u32[]{:S(2)}, u32[]{:S(2)}) collective-permute-start(bf16[960,128]{1,0:T(8,128)(2,1)S(1)} %copy-done.5), channel_id=1, source_target_pairs={{0,0},{1,32},{2,64},{3,96},{4,128},{5,160},{6,192},{7,224},{32,1},... | collective-permute-start | bytes 737288 | tf_op jit(solution)/shard_map/ppermute | solution.py:107
  35.9 58.5 %all-to-all-start.1 = ((bf16[32,120,360]{2,1,0:T(8,128)(2,1)}), bf16[32,120,360]{2,1,0:T(8,128)(2,1)S(1)}, u32[]{:S(2)}, u32[]{:S(2)}) async-start(bf16[32,120,360]{2,1,0:T(8,128)(2,1)} %shard_map.82), calls=%async_computation.2 | async-start | bytes 5898240 | tf_op jit(solution)/shard_map/all_to_all | solution.py:115
  94.4 1.6 copy-start
  96.0 67.2 %all-to-all-start = ((bf16[32,120,600]{2,1,0:T(8,128)(2,1)}), bf16[32,120,600]{2,1,0:T(8,128)(2,1)}, u32[]{:S(2)}, u32[]{:S(2)}) async-start(bf16[32,120,600]{2,1,0:T(8,128)(2,1)} %shard_map.83), calls=%async_computation | async-start | bytes 9830400 | tf_op jit(solution)/shard_map/all_to_all | solution.py:115
  104.6 70.5 %reduce-scatter.5.cloned.1.call-start = ((), (), s32[]{:S(2)}) async-start(), calls=%async_computation.6 | async-start | bytes 1658880 | tf_op jit(solution)/shard_map/reduce_scatter | solution.py:117
  112.7 104.0 %reduce-scatter.3.cloned.1.call-start = ((), (), s32[]{:S(2)}) async-start(), calls=%async_computation.5 | async-start | bytes 2764800 | tf_op jit(solution)/shard_map/reduce_scatter | solution.py:117
  163.2 10.3 %copy-start.1 = (f32[192]{0:T(256)S(1)}, f32[192]{0:T(256)}, u32[]{:S(2)}) copy-start(f32[192]{0:T(256)} %param.15) | copy-start | bytes 2308
  163.2 10.5 %copy-start.2 = (f32[240]{0:T(256)S(1)}, f32[240]{0:T(256)}, u32[]{:S(2)}) copy-start(f32[240]{0:T(256)} %param.14) | copy-start | bytes 2884
  163.2 10.8 %copy-start.3 = (s32[192]{0:T(256)S(1)}, s32[192]{0:T(256)}, u32[]{:S(2)}) copy-start(s32[192]{0:T(256)} %param.13) | copy-start | bytes 2308
  163.2 11.0 %copy-start.4 = (s32[240]{0:T(256)S(1)}, s32[240]{0:T(256)}, u32[]{:S(2)}) copy-start(s32[240]{0:T(256)} %param.12) | copy-start | bytes 2884
  218.1 24.1 %collective-permute-start.1 = (bf16[960,128]{1,0:T(8,128)(2,1)S(1)}, bf16[960,128]{1,0:T(8,128)(2,1)S(1)}, u32[]{:S(2)}, u32[]{:S(2)}) collective-permute-start(bf16[960,128]{1,0:T(8,128)(2,1)S(1)} %fusion.2), channel_id=1, source_target_pairs={{0,0},{1,32},{2,64},{3,96},{4,128},{5,160},{6,192},{7,224},{32,1},... | collective-permute-start | bytes 737288 | tf_op jit(solution)/shard_map/ppermute | solution.py:135
Sparse Core Ops, SparseCore 0:
  11.1 86.2 all-gather.1
  112.8 38.8 reduce-scatter.4
  173.5 43.1 reduce-scatter.2

commit v13 on v12

--- a/solution.py
+++ b/solution.py
@@ -103,23 +103,18 @@
 
     groups = lax.axis_size((X, C, Y))
     block = amps.shape[1] // groups
-    perm = swap_perm(nz, ncol)
-    coulomb_here = lax.ppermute(coulomb, (Z, X, C), perm)
     sums = []
     start = 0
     for k, width in enumerate(chunk_widths(block)):
         piece = stack_chunk(amps, groups, start, width)
         start += width
-        if k == 1:
-            coulomb_here, piece = lax.optimization_barrier((coulomb_here, piece))
         plane_amps = lax.all_to_all(piece, (X, C, Y), split_axis=0, concat_axis=0, tiled=True)
         partial_value = product(plane_amps.reshape(groups * sub, width), masked_all)
         sums.append(lax.psum_scatter(partial_value, Z, scatter_dimension=1, tiled=True))
-    cycle_sum = jnp.concatenate(sums, axis=0)
+    cycle_sum = lax.ppermute(jnp.concatenate(sums, axis=0), (Z, X, C), swap_perm(nz, ncol))
 
-    row_block = c * ny + y
-    row_pos = row_block * rows_here + jnp.arange(rows_here, dtype=jnp.int32)
-    col_pos = z * cols_here + jnp.arange(cols_here, dtype=jnp.int32)
+    row_pos = lax.axis_index(ROW) * rows_here + jnp.arange(rows_here, dtype=jnp.int32)
+    col_pos = c * cols_here + jnp.arange(cols_here, dtype=jnp.int32)
     occ_row = row_pos // block_size % occupied
     vir_row = block_size * (row_pos // (occupied * block_size)) + row_pos % block_size
     occ_col = col_pos // block_size % occupied
@@ -130,9 +125,9 @@
     gap_row = lookup(vir_row, vir_energy) - lookup(occ_row, occ_energy)
     gap_col = lookup(vir_col, vir_energy) - lookup(occ_col, occ_energy)
     denominator = gap_row[:, None] + gap_col[None, :]
-    updated = (coulomb_here.astype(jnp.float32) + cycle_sum) / denominator
+    updated = (coulomb.astype(jnp.float32) + cycle_sum) / denominator
     out = jnp.where(allowed, updated, jnp.float32(0.0)).astype(jnp.bfloat16)
-    return lax.ppermute(out, (Z, X, C), perm)
+    return out
 
 
 def solution(mesh):

time: 250 us -> 259 us (1.036)
  waiting for transfers between devices: 165 us -> 180 us
  starting transfers between devices: 31.3 us -> 24.4 us
    all_to_all x2, waiting for transfers between devices: 95.5 us -> 105 us  [local(): lax.all_to_all(piece, (X, C, Y), split_axis=0, concat_axis=0, tiled=True)]
    ppermute x2 -> x1, starting transfers between devices: 15.5 us -> 7.56 us  [local(): lax.ppermute(jnp.concatenate(sums, axis=0), (Z, X, C), swap_perm(nz, ncol))]
    ppermute x2 -> x1, waiting for transfers between devices: 27.7 us -> 31.5 us  [local(): lax.ppermute(jnp.concatenate(sums, axis=0), (Z, X, C), swap_perm(nz, ncol))]
  transfers between devices with their start and end apart: 7 -> 6, of which waited for: 5 -> 4; matrix products, arithmetic and copies ran while one was open for 1% -> 1% of each run, Pallas kernels for 12% -> 12%
where the time goes in v13:
time: 259 us; the launch traced here: 258 us
  waiting for transfers between devices  180 us (69%)
  Pallas kernels  30.7 us (12%)
  starting transfers between devices  24.4 us (9%)
  between operations  13.3 us (5%)
  other arithmetic  6.93 us (3%)
  local copies, waits for them, and re-layouts  2.78 us (1%)
    all_to_all x2, waiting for transfers between devices, local(): lax.all_to_all(piece, (X, C, Y), split_axis=0, concat_axis=0, tiled=True)  105 us
    reduce_scatter x2, waiting for transfers between devices, local(): lax.psum_scatter(partial_value, Z, scatter_dimension=1, tiled=True)  43.8 us
    ppermute x1, waiting for transfers between devices, local(): lax.ppermute(jnp.concatenate(sums, axis=0), (Z, X, C), swap_perm(nz, ncol))  31.5 us
    pallas_call x2, Pallas kernels, product(): pl.pallas_call(product_kernel, out_shape=jax.ShapeDtypeStruct((rows, widt...  18.2 us
    all_to_all x2, starting transfers between devices, local(): lax.all_to_all(piece, (X, C, Y), split_axis=0, concat_axis=0, tiled=True)  16.8 us
    pallas_call x2, Pallas kernels, stack_chunk(): pl.pallas_call(functools.partial(stack_kernel, start, width, block), out_...  12.5 us
    ppermute x1, starting transfers between devices, local(): lax.ppermute(jnp.concatenate(sums, axis=0), (Z, X, C), swap_perm(nz, ncol))  7.56 us
  transfers between devices with their start and end apart: 6, of which 4 were waited for; matrix products, arithmetic and copies ran while one was open for 1% of the time, Pallas kernels for 12%

profile of v13, /device:TPU:7, one launch (start us, length us, event | category | flops | bytes accessed | tf_op | source)
XLA Modules:
  0.0 258.5 jit_solution(15483662742879239646)
XLA Ops:
  6.5 0.0 all-gather.2.cloned.1.call-start
  6.5 0.7 convert_element_type.10
  7.2 0.2 broadcast_in_dim.140
  7.4 0.3 reshape.123
  7.7 0.1 constant_dynamic-slice_fusion
  7.8 0.1 mul.41
  7.9 0.5 copy.12
  8.4 2.5 dynamic-slice_multiply_fusion
  11.0 0.0 all-gather.2.cloned.1.call-update
  11.0 5.7 %shard_map.84 = bf16[32,120,360]{2,1,0:T(8,128)(2,1)} custom-call(bf16[120,30720]{1,0:T(8,128)(2,1)} %in_ref.3), custom_call_target="tpu_custom_call" | custom-call | tf_op jit(solution)/shard_map/pallas_call | solution.py:63
  16.7 7.9 %all-to-all-start.1 = ((bf16[32,120,360]{2,1,0:T(8,128)(2,1)}), bf16[32,120,360]{2,1,0:T(8,128)(2,1)S(1)}, u32[]{:S(2)}, u32[]{:S(2)}) async-start(bf16[32,120,360]{2,1,0:T(8,128)(2,1)} %shard_map.84), calls=%async_computation.2 | async-start | bytes 5898240 | tf_op jit(solution)/shard_map/all_to_all | solution.py:111
  24.6 6.8 %shard_map.82 = bf16[32,120,600]{2,1,0:T(8,128)(2,1)} custom-call(bf16[120,30720]{1,0:T(8,128)(2,1)} %in_ref.3), custom_call_target="tpu_custom_call" | custom-call | tf_op jit(solution)/shard_map/pallas_call | solution.py:63
  31.5 54.6 %all-to-all-done.1 = bf16[32,120,360]{2,1,0:T(8,128)(2,1)S(1)} async-done(((bf16[32,120,360]{2,1,0:T(8,128)(2,1)}), bf16[32,120,360]{2,1,0:T(8,128)(2,1)S(1)}, u32[]{:S(2)}, u32[]{:S(2)}) %all-to-all-start.1) | async-done | bytes 2764832 | tf_op jit(solution)/shard_map/all_to_all | solution.py:111
  86.0 0.0 copy-start
  86.0 1.6 copy-done
  87.6 8.8 %all-to-all-start = ((bf16[32,120,600]{2,1,0:T(8,128)(2,1)}), bf16[32,120,600]{2,1,0:T(8,128)(2,1)}, u32[]{:S(2)}, u32[]{:S(2)}) async-start(bf16[32,120,600]{2,1,0:T(8,128)(2,1)} %shard_map.82), calls=%async_computation | async-start | bytes 9830400 | tf_op jit(solution)/shard_map/all_to_all | solution.py:111
  96.5 0.0 reduce-scatter.5.cloned.1.call-start
  96.5 0.0 all-gather.2.cloned.1.call-done.right_ref
  96.6 8.0 %shard_map.85 = f32[360,1024]{1,0:T(8,128)} custom-call(bf16[3840,360]{1,0:T(8,128)(2,1)} %bitcast.5, bf16[3840,1024]{1,0:T(8,128)(2,1)} %all-gather.2.cloned.1.call-done.right_ref), custom_call_target="tpu_custom_call" | custom-call | flops 2831155200 | bytes 12103680 | tf_op jit(solution)/shard_map/pallas_call | solution.py:37
  104.5 0.0 reduce-scatter.5.cloned.1.call-update
  104.6 0.0 reduce-scatter.3.cloned.1.call-start
  104.6 50.4 %all-to-all-done = bf16[32,120,600]{2,1,0:T(8,128)(2,1)} async-done(((bf16[32,120,600]{2,1,0:T(8,128)(2,1)}), bf16[32,120,600]{2,1,0:T(8,128)(2,1)}, u32[]{:S(2)}, u32[]{:S(2)}) %all-to-all-start) | async-done | bytes 4608032 | tf_op jit(solution)/shard_map/all_to_all | solution.py:111
  155.0 0.0 copy-start.2
  155.0 0.0 copy-start.4
  155.0 0.0 copy-start.3
  155.0 0.0 copy-start.5
  155.1 10.2 %shard_map.83 = f32[600,1024]{1,0:T(8,128)} custom-call(bf16[3840,600]{1,0:T(8,128)(2,1)} %bitcast.left_ref, bf16[3840,1024]{1,0:T(8,128)(2,1)} %all-gather.2.cloned.1.call-done.right_ref), custom_call_target="tpu_custom_call" | custom-call | flops 4718592000 | bytes 14929920 | tf_op jit(solution)/shard_map/pallas_call | solution.py:37
  165.3 0.0 copy-start.1
  165.3 0.0 reduce-scatter.3.cloned.1.call-update
  165.3 0.0 copy-done.2
  165.3 0.2 select_reduce_fusion.2
  165.5 0.0 copy-done.4
  165.5 0.2 select_reduce_fusion.3
  165.7 0.0 copy-done.3
  165.7 0.4 select_reduce_fusion
  166.1 0.0 copy-done.5
  166.1 0.4 select_reduce_fusion.1
  166.4 0.0 reduce-scatter.5.cloned.1.call-done
  166.5 43.8 %reduce-scatter.3.cloned.1.call-done = f32[600,128]{1,0:T(8,128)} async-done(((f32[600,1024]{1,0:T(8,128)}), f32[600,128]{1,0:T(8,128)}) %reduce-scatter.3.cloned.1.call-update) | async-done | bytes 307216 | tf_op jit(solution)/shard_map/reduce_scatter | solution.py:113
  210.2 1.1 pad_maximum_fusion
  211.3 7.6 %collective-permute-start = (f32[960,128]{1,0:T(8,128)S(1)}, f32[960,128]{1,0:T(8,128)S(1)}, u32[]{:S(2)}, u32[]{:S(2)}) collective-permute-start(f32[960,128]{1,0:T(8,128)S(1)} %pad_maximum_fusion), channel_id=1, source_target_pairs={{0,0},{1,32},{2,64},{3,96},{4,128},{5,160},{6,192},{7,224},{32,1},... | collective-permute-start | bytes 1474568 | tf_op jit(solution)/shard_map/ppermute | solution.py:114
  219.0 0.1 select_reduce_fusion.6
  219.1 0.1 select_reduce_fusion.4
  219.2 0.1 select_reduce_fusion.7
  219.3 0.1 select_reduce_fusion.5
  219.4 31.5 %collective-permute-done = f32[960,128]{1,0:T(8,128)S(1)} collective-permute-done((f32[960,128]{1,0:T(8,128)S(1)}, f32[960,128]{1,0:T(8,128)S(1)}, u32[]{:S(2)}, u32[]{:S(2)}) %collective-permute-start) | collective-permute-done | bytes 491552 | tf_op jit(solution)/shard_map/ppermute | solution.py:114
  250.9 0.0 copy-done.1
  250.9 1.0 select_convert_fusion
  (6 shorter events, 0.1 us)
Async XLA Ops:
  6.5 90.0 %all-gather.2.cloned.1.call-start = ((), (), s32[]{:S(2)}) async-start(), calls=%async_computation.4 | async-start | bytes 8847360 | tf_op jit(solution)/shard_map/all_gather | solution.py:102
  16.7 69.3 %all-to-all-start.1 = ((bf16[32,120,360]{2,1,0:T(8,128)(2,1)}), bf16[32,120,360]{2,1,0:T(8,128)(2,1)S(1)}, u32[]{:S(2)}, u32[]{:S(2)}) async-start(bf16[32,120,360]{2,1,0:T(8,128)(2,1)} %shard_map.84), calls=%async_computation.2 | async-start | bytes 5898240 | tf_op jit(solution)/shard_map/all_to_all | solution.py:111
  86.0 1.6 copy-start
  87.6 67.4 %all-to-all-start = ((bf16[32,120,600]{2,1,0:T(8,128)(2,1)}), bf16[32,120,600]{2,1,0:T(8,128)(2,1)}, u32[]{:S(2)}, u32[]{:S(2)}) async-start(bf16[32,120,600]{2,1,0:T(8,128)(2,1)} %shard_map.82), calls=%async_computation | async-start | bytes 9830400 | tf_op jit(solution)/shard_map/all_to_all | solution.py:111
  96.5 70.0 %reduce-scatter.5.cloned.1.call-start = ((), (), s32[]{:S(2)}) async-start(), calls=%async_computation.6 | async-start | bytes 1658880 | tf_op jit(solution)/shard_map/reduce_scatter | solution.py:113
  104.6 105.7 %reduce-scatter.3.cloned.1.call-start = ((), (), s32[]{:S(2)}) async-start(), calls=%async_computation.5 | async-start | bytes 2764800 | tf_op jit(solution)/shard_map/reduce_scatter | solution.py:113
  155.0 10.3 %copy-start.2 = (f32[192]{0:T(256)S(1)}, f32[192]{0:T(256)}, u32[]{:S(2)}) copy-start(f32[192]{0:T(256)} %param.15) | copy-start | bytes 2308
  155.0 10.5 %copy-start.4 = (s32[192]{0:T(256)S(1)}, s32[192]{0:T(256)}, u32[]{:S(2)}) copy-start(s32[192]{0:T(256)} %param.13) | copy-start | bytes 2308
  155.0 10.7 %copy-start.3 = (f32[240]{0:T(256)S(1)}, f32[240]{0:T(256)}, u32[]{:S(2)}) copy-start(f32[240]{0:T(256)} %param.14) | copy-start | bytes 2884
  155.0 11.0 %copy-start.5 = (s32[240]{0:T(256)S(1)}, s32[240]{0:T(256)}, u32[]{:S(2)}) copy-start(s32[240]{0:T(256)} %param.12) | copy-start | bytes 2884
  165.3 85.7 %copy-start.1 = (bf16[960,128]{1,0:T(8,128)(2,1)S(1)}, bf16[960,128]{1,0:T(8,128)(2,1)}, u32[]{:S(2)}) copy-start(bf16[960,128]{1,0:T(8,128)(2,1)} %param.11) | copy-start | bytes 737284
  211.3 39.6 %collective-permute-start = (f32[960,128]{1,0:T(8,128)S(1)}, f32[960,128]{1,0:T(8,128)S(1)}, u32[]{:S(2)}, u32[]{:S(2)}) collective-permute-start(f32[960,128]{1,0:T(8,128)S(1)} %pad_maximum_fusion), channel_id=1, source_target_pairs={{0,0},{1,32},{2,64},{3,96},{4,128},{5,160},{6,192},{7,224},{32,1},... | collective-permute-start | bytes 1474568 | tf_op jit(solution)/shard_map/ppermute | solution.py:114
Sparse Core Ops, SparseCore 0:
  11.1 80.5 all-gather.1
  104.7 40.4 reduce-scatter.4
  165.4 44.7 reduce-scatter.2

commit v14 on v12

--- a/solution.py
+++ b/solution.py
@@ -33,7 +33,7 @@
 def product(left, right):
     depth, rows = left.shape
     width = right.shape[1]
-    tile = 256
+    tile = 512
     return pl.pallas_call(
         product_kernel,
         out_shape=jax.ShapeDtypeStruct((rows, width), jnp.float32),

time: 250 us -> 250 us (level)
  no operation moved by 1% of the time
where the time goes in v14:
time: 250 us; the launch traced here: 249 us
  waiting for transfers between devices  165 us (66%)
  starting transfers between devices  31.3 us (13%)
  Pallas kernels  29.2 us (12%)
  between operations  13.3 us (5%)
  other arithmetic  6.2 us (2%)
  local copies, waits for them, and re-layouts  3.47 us (1%)
    all_to_all x2, waiting for transfers between devices, local(): lax.all_to_all(piece, (X, C, Y), split_axis=0, concat_axis=0, tiled=True)  96.2 us
    reduce_scatter x2, waiting for transfers between devices, local(): lax.psum_scatter(partial_value, Z, scatter_dimension=1, tiled=True)  41.6 us
    pallas_call x2, Pallas kernels, product(): pl.pallas_call(product_kernel, out_shape=jax.ShapeDtypeStruct((rows, widt...  17.2 us
    ppermute x1, waiting for transfers between devices, local(): return lax.ppermute(out, (Z, X, C), perm)  16.3 us
    all_to_all x2, starting transfers between devices, local(): lax.all_to_all(piece, (X, C, Y), split_axis=0, concat_axis=0, tiled=True)  15.7 us
    pallas_call x2, Pallas kernels, stack_chunk(): pl.pallas_call(functools.partial(stack_kernel, start, width, block), out_...  12 us
    ppermute x1, waiting for transfers between devices, local(): coulomb_here = lax.ppermute(coulomb, (Z, X, C), perm)  11.2 us
    ppermute x1, starting transfers between devices, local(): coulomb_here = lax.ppermute(coulomb, (Z, X, C), perm)  7.96 us
  transfers between devices with their start and end apart: 7, of which 5 were waited for; matrix products, arithmetic and copies ran while one was open for 1% of the time, Pallas kernels for 12%

profile of v14, /device:TPU:7, one launch (start us, length us, event | category | flops | bytes accessed | tf_op | source)
XLA Modules:
  0.0 248.9 jit_solution(9872692905018378061)
XLA Ops:
  6.5 0.0 all-gather.2.cloned.1.call-start
  6.5 0.7 convert_element_type.10
  7.2 0.2 broadcast_in_dim.140
  7.4 0.3 reshape.123
  7.7 0.1 constant_dynamic-slice_fusion
  7.8 0.1 mul.41
  7.9 0.0 copy-start.5
  7.9 0.5 copy.12
  8.4 2.5 %dynamic-slice_multiply_fusion = bf16[480,1024]{1,0:T(8,128)(2,1)} fusion(bf16[480,1024]{1,0:T(8,128)(2,1)S(1)} %copy.12, bf16[3840,1024]{1,0:T(8,128)(2,1)} %param.9, s32[]{:T(128)S(6)} %select_n.113), kind=kLoop, calls=%fused_computation.1 | loop fusion | flops 1966080 | bytes 2949124 | tf_op jit(solution)/shard_map/mul | solution.py:100
  11.0 0.0 all-gather.2.cloned.1.call-update
  11.0 0.0 copy-done.5
  11.0 8.0 %collective-permute-start = (bf16[960,128]{1,0:T(8,128)(2,1)S(1)}, bf16[960,128]{1,0:T(8,128)(2,1)S(1)}, u32[]{:S(2)}, u32[]{:S(2)}) collective-permute-start(bf16[960,128]{1,0:T(8,128)(2,1)S(1)} %copy-done.5), channel_id=1, source_target_pairs={{0,0},{1,32},{2,64},{3,96},{4,128},{5,160},{6,192},{7,224},{32,1},... | collective-permute-start | bytes 737288 | tf_op jit(solution)/shard_map/ppermute | solution.py:107
  19.0 5.7 %shard_map.82 = bf16[32,120,360]{2,1,0:T(8,128)(2,1)} custom-call(bf16[120,30720]{1,0:T(8,128)(2,1)} %in_ref.3), custom_call_target="tpu_custom_call" | custom-call | tf_op jit(solution)/shard_map/pallas_call | solution.py:63
  24.7 11.2 %collective-permute-done = bf16[960,128]{1,0:T(8,128)(2,1)S(1)} collective-permute-done((bf16[960,128]{1,0:T(8,128)(2,1)S(1)}, bf16[960,128]{1,0:T(8,128)(2,1)S(1)}, u32[]{:S(2)}, u32[]{:S(2)}) %collective-permute-start) | collective-permute-done | bytes 245792 | tf_op jit(solution)/shard_map/ppermute | solution.py:107
  35.9 7.1 %all-to-all-start.1 = ((bf16[32,120,360]{2,1,0:T(8,128)(2,1)}), bf16[32,120,360]{2,1,0:T(8,128)(2,1)S(1)}, u32[]{:S(2)}, u32[]{:S(2)}) async-start(bf16[32,120,360]{2,1,0:T(8,128)(2,1)} %shard_map.82), calls=%async_computation.2 | async-start | bytes 5898240 | tf_op jit(solution)/shard_map/all_to_all | solution.py:115
  43.0 6.3 %shard_map.83 = bf16[32,120,600]{2,1,0:T(8,128)(2,1)} custom-call(bf16[120,30720]{1,0:T(8,128)(2,1)} %in_ref.3), custom_call_target="tpu_custom_call" | custom-call | tf_op jit(solution)/shard_map/pallas_call | solution.py:63
  49.3 45.1 %all-to-all-done.1 = bf16[32,120,360]{2,1,0:T(8,128)(2,1)S(1)} async-done(((bf16[32,120,360]{2,1,0:T(8,128)(2,1)}), bf16[32,120,360]{2,1,0:T(8,128)(2,1)S(1)}, u32[]{:S(2)}, u32[]{:S(2)}) %all-to-all-start.1) | async-done | bytes 2764832 | tf_op jit(solution)/shard_map/all_to_all | solution.py:115
  94.4 0.0 copy-start
  94.4 1.6 copy-done
  96.0 8.6 %all-to-all-start = ((bf16[32,120,600]{2,1,0:T(8,128)(2,1)}), bf16[32,120,600]{2,1,0:T(8,128)(2,1)}, u32[]{:S(2)}, u32[]{:S(2)}) async-start(bf16[32,120,600]{2,1,0:T(8,128)(2,1)} %shard_map.83), calls=%async_computation | async-start | bytes 9830400 | tf_op jit(solution)/shard_map/all_to_all | solution.py:115
  104.6 0.0 reduce-scatter.5.cloned.1.call-start
  104.7 0.0 all-gather.2.cloned.1.call-done.right_ref
  104.7 7.2 %shard_map.85 = f32[360,1024]{1,0:T(8,128)} custom-call(bf16[3840,360]{1,0:T(8,128)(2,1)} %bitcast.5, bf16[3840,1024]{1,0:T(8,128)(2,1)} %all-gather.2.cloned.1.call-done.right_ref), custom_call_target="tpu_custom_call" | custom-call | flops 2831155200 | bytes 12103680 | tf_op jit(solution)/shard_map/pallas_call | solution.py:37
  111.9 0.0 reduce-scatter.5.cloned.1.call-update
  112.0 0.0 reduce-scatter.3.cloned.1.call-start
  112.0 51.2 %all-to-all-done = bf16[32,120,600]{2,1,0:T(8,128)(2,1)} async-done(((bf16[32,120,600]{2,1,0:T(8,128)(2,1)}), bf16[32,120,600]{2,1,0:T(8,128)(2,1)}, u32[]{:S(2)}, u32[]{:S(2)}) %all-to-all-start) | async-done | bytes 4608032 | tf_op jit(solution)/shard_map/all_to_all | solution.py:115
  163.2 0.0 copy-start.1
  163.2 0.0 copy-start.2
  163.2 0.0 copy-start.3
  163.2 0.0 copy-start.4
  163.2 9.9 %shard_map.84 = f32[600,1024]{1,0:T(8,128)} custom-call(bf16[3840,600]{1,0:T(8,128)(2,1)} %bitcast.left_ref, bf16[3840,1024]{1,0:T(8,128)(2,1)} %all-gather.2.cloned.1.call-done.right_ref), custom_call_target="tpu_custom_call" | custom-call | flops 4718592000 | bytes 14929920 | tf_op jit(solution)/shard_map/pallas_call | solution.py:37
  173.1 0.0 reduce-scatter.3.cloned.1.call-update
  173.2 0.0 copy-done.1
  173.2 0.2 select_reduce_fusion.2
  173.3 0.0 copy-done.2
  173.4 0.4 select_reduce_fusion
  173.7 0.0 copy-done.3
  173.7 0.2 select_reduce_fusion.3
  173.9 0.0 copy-done.4
  173.9 0.4 select_reduce_fusion.1
  174.3 0.1 select_reduce_fusion.6
  174.4 0.1 select_reduce_fusion.4
  174.6 0.1 select_reduce_fusion.7
  174.7 0.1 select_reduce_fusion.5
  174.8 0.0 reduce-scatter.5.cloned.1.call-done
  174.8 41.6 %reduce-scatter.3.cloned.1.call-done = f32[600,128]{1,0:T(8,128)} async-done(((f32[600,1024]{1,0:T(8,128)}), f32[600,128]{1,0:T(8,128)}) %reduce-scatter.3.cloned.1.call-update) | async-done | bytes 307216 | tf_op jit(solution)/shard_map/reduce_scatter | solution.py:117
  216.4 1.4 fusion.2
  217.8 7.6 %collective-permute-start.1 = (bf16[960,128]{1,0:T(8,128)(2,1)S(1)}, bf16[960,128]{1,0:T(8,128)(2,1)S(1)}, u32[]{:S(2)}, u32[]{:S(2)}) collective-permute-start(bf16[960,128]{1,0:T(8,128)(2,1)S(1)} %fusion.2), channel_id=1, source_target_pairs={{0,0},{1,32},{2,64},{3,96},{4,128},{5,160},{6,192},{7,224},{32,1},... | collective-permute-start | bytes 737288 | tf_op jit(solution)/shard_map/ppermute | solution.py:135
  225.4 16.3 %collective-permute-done.1 = bf16[960,128]{1,0:T(8,128)(2,1)S(1)} collective-permute-done((bf16[960,128]{1,0:T(8,128)(2,1)S(1)}, bf16[960,128]{1,0:T(8,128)(2,1)S(1)}, u32[]{:S(2)}, u32[]{:S(2)}) %collective-permute-start.1) | collective-permute-done | bytes 245792 | tf_op jit(solution)/shard_map/ppermute | solution.py:135
  241.7 0.7 copy.14
  (6 shorter events, 0.1 us)
Async XLA Ops:
  6.5 98.1 %all-gather.2.cloned.1.call-start = ((), (), s32[]{:S(2)}) async-start(), calls=%async_computation.4 | async-start | bytes 8847360 | tf_op jit(solution)/shard_map/all_gather | solution.py:102
  7.9 3.1 %copy-start.5 = (bf16[960,128]{1,0:T(8,128)(2,1)S(1)}, bf16[960,128]{1,0:T(8,128)(2,1)}, u32[]{:S(2)}) copy-start(bf16[960,128]{1,0:T(8,128)(2,1)} %param.11) | copy-start | bytes 737284
  11.0 24.9 %collective-permute-start = (bf16[960,128]{1,0:T(8,128)(2,1)S(1)}, bf16[960,128]{1,0:T(8,128)(2,1)S(1)}, u32[]{:S(2)}, u32[]{:S(2)}) collective-permute-start(bf16[960,128]{1,0:T(8,128)(2,1)S(1)} %copy-done.5), channel_id=1, source_target_pairs={{0,0},{1,32},{2,64},{3,96},{4,128},{5,160},{6,192},{7,224},{32,1},... | collective-permute-start | bytes 737288 | tf_op jit(solution)/shard_map/ppermute | solution.py:107
  35.9 58.5 %all-to-all-start.1 = ((bf16[32,120,360]{2,1,0:T(8,128)(2,1)}), bf16[32,120,360]{2,1,0:T(8,128)(2,1)S(1)}, u32[]{:S(2)}, u32[]{:S(2)}) async-start(bf16[32,120,360]{2,1,0:T(8,128)(2,1)} %shard_map.82), calls=%async_computation.2 | async-start | bytes 5898240 | tf_op jit(solution)/shard_map/all_to_all | solution.py:115
  94.4 1.6 copy-start
  96.0 67.2 %all-to-all-start = ((bf16[32,120,600]{2,1,0:T(8,128)(2,1)}), bf16[32,120,600]{2,1,0:T(8,128)(2,1)}, u32[]{:S(2)}, u32[]{:S(2)}) async-start(bf16[32,120,600]{2,1,0:T(8,128)(2,1)} %shard_map.83), calls=%async_computation | async-start | bytes 9830400 | tf_op jit(solution)/shard_map/all_to_all | solution.py:115
  104.6 70.2 %reduce-scatter.5.cloned.1.call-start = ((), (), s32[]{:S(2)}) async-start(), calls=%async_computation.6 | async-start | bytes 1658880 | tf_op jit(solution)/shard_map/reduce_scatter | solution.py:117
  112.0 104.5 %reduce-scatter.3.cloned.1.call-start = ((), (), s32[]{:S(2)}) async-start(), calls=%async_computation.5 | async-start | bytes 2764800 | tf_op jit(solution)/shard_map/reduce_scatter | solution.py:117
  163.2 10.0 %copy-start.1 = (f32[192]{0:T(256)S(1)}, f32[192]{0:T(256)}, u32[]{:S(2)}) copy-start(f32[192]{0:T(256)} %param.15) | copy-start | bytes 2308
  163.2 10.2 %copy-start.2 = (f32[240]{0:T(256)S(1)}, f32[240]{0:T(256)}, u32[]{:S(2)}) copy-start(f32[240]{0:T(256)} %param.14) | copy-start | bytes 2884
  163.2 10.6 %copy-start.3 = (s32[192]{0:T(256)S(1)}, s32[192]{0:T(256)}, u32[]{:S(2)}) copy-start(s32[192]{0:T(256)} %param.13) | copy-start | bytes 2308
  163.2 10.8 %copy-start.4 = (s32[240]{0:T(256)S(1)}, s32[240]{0:T(256)}, u32[]{:S(2)}) copy-start(s32[240]{0:T(256)} %param.12) | copy-start | bytes 2884
  217.8 23.9 %collective-permute-start.1 = (bf16[960,128]{1,0:T(8,128)(2,1)S(1)}, bf16[960,128]{1,0:T(8,128)(2,1)S(1)}, u32[]{:S(2)}, u32[]{:S(2)}) collective-permute-start(bf16[960,128]{1,0:T(8,128)(2,1)S(1)} %fusion.2), channel_id=1, source_target_pairs={{0,0},{1,32},{2,64},{3,96},{4,128},{5,160},{6,192},{7,224},{32,1},... | collective-permute-start | bytes 737288 | tf_op jit(solution)/shard_map/ppermute | solution.py:135
Sparse Core Ops, SparseCore 0:
  11.1 86.2 all-gather.1
  112.1 38.7 reduce-scatter.4
  173.2 43.1 reduce-scatter.2

commit v15 on v14

--- a/solution.py
+++ b/solution.py
@@ -33,7 +33,7 @@
 def product(left, right):
     depth, rows = left.shape
     width = right.shape[1]
-    tile = 512
+    tile = 1024
     return pl.pallas_call(
         product_kernel,
         out_shape=jax.ShapeDtypeStruct((rows, width), jnp.float32),

time: 250 us -> 251 us (level)
  transfers between devices with their start and end apart: 7 -> 7, of which waited for: 5 -> 5; matrix products, arithmetic and copies ran while one was open for 1% -> 1% of each run, Pallas kernels for 12% -> 13%
where the time goes in v15:
time: 251 us; the launch traced here: 250 us
  waiting for transfers between devices  164 us (65%)
  starting transfers between devices  31.5 us (13%)
  Pallas kernels  31.5 us (13%)
  between operations  13.3 us (5%)
  other arithmetic  6.2 us (2%)
  local copies, waits for them, and re-layouts  3.47 us (1%)
    all_to_all x2, waiting for transfers between devices, local(): lax.all_to_all(piece, (X, C, Y), split_axis=0, concat_axis=0, tiled=True)  95.1 us
    reduce_scatter x2, waiting for transfers between devices, local(): lax.psum_scatter(partial_value, Z, scatter_dimension=1, tiled=True)  41.6 us
    pallas_call x2, Pallas kernels, product(): pl.pallas_call(product_kernel, out_shape=jax.ShapeDtypeStruct((rows, widt...  19.5 us
    ppermute x1, waiting for transfers between devices, local(): return lax.ppermute(out, (Z, X, C), perm)  16.3 us
    all_to_all x2, starting transfers between devices, local(): lax.all_to_all(piece, (X, C, Y), split_axis=0, concat_axis=0, tiled=True)  15.7 us
    pallas_call x2, Pallas kernels, stack_chunk(): pl.pallas_call(functools.partial(stack_kernel, start, width, block), out_...  12 us
    ppermute x1, waiting for transfers between devices, local(): coulomb_here = lax.ppermute(coulomb, (Z, X, C), perm)  11.2 us
    ppermute x1, starting transfers between devices, local(): coulomb_here = lax.ppermute(coulomb, (Z, X, C), perm)  7.96 us
  transfers between devices with their start and end apart: 7, of which 5 were waited for; matrix products, arithmetic and copies ran while one was open for 1% of the time, Pallas kernels for 13%

profile of v15, /device:TPU:7, one launch (start us, length us, event | category | flops | bytes accessed | tf_op | source)
XLA Modules:
  0.0 250.3 jit_solution(15514214916095003678)
XLA Ops:
  6.5 0.0 all-gather.2.cloned.1.call-start
  6.5 0.7 convert_element_type.10
  7.2 0.2 broadcast_in_dim.140
  7.4 0.3 reshape.123
  7.7 0.1 constant_dynamic-slice_fusion
  7.8 0.1 mul.41
  7.9 0.0 copy-start.5
  7.9 0.5 copy.12
  8.4 2.5 %dynamic-slice_multiply_fusion = bf16[480,1024]{1,0:T(8,128)(2,1)} fusion(bf16[480,1024]{1,0:T(8,128)(2,1)S(1)} %copy.12, bf16[3840,1024]{1,0:T(8,128)(2,1)} %param.9, s32[]{:T(128)S(6)} %select_n.113), kind=kLoop, calls=%fused_computation.1 | loop fusion | flops 1966080 | bytes 2949124 | tf_op jit(solution)/shard_map/mul | solution.py:100
  11.0 0.0 all-gather.2.cloned.1.call-update
  11.0 0.0 copy-done.5
  11.0 8.0 %collective-permute-start = (bf16[960,128]{1,0:T(8,128)(2,1)S(1)}, bf16[960,128]{1,0:T(8,128)(2,1)S(1)}, u32[]{:S(2)}, u32[]{:S(2)}) collective-permute-start(bf16[960,128]{1,0:T(8,128)(2,1)S(1)} %copy-done.5), channel_id=1, source_target_pairs={{0,0},{1,32},{2,64},{3,96},{4,128},{5,160},{6,192},{7,224},{32,1},... | collective-permute-start | bytes 737288 | tf_op jit(solution)/shard_map/ppermute | solution.py:107
  19.0 5.7 %shard_map.82 = bf16[32,120,360]{2,1,0:T(8,128)(2,1)} custom-call(bf16[120,30720]{1,0:T(8,128)(2,1)} %in_ref.3), custom_call_target="tpu_custom_call" | custom-call | tf_op jit(solution)/shard_map/pallas_call | solution.py:63
  24.7 11.2 %collective-permute-done = bf16[960,128]{1,0:T(8,128)(2,1)S(1)} collective-permute-done((bf16[960,128]{1,0:T(8,128)(2,1)S(1)}, bf16[960,128]{1,0:T(8,128)(2,1)S(1)}, u32[]{:S(2)}, u32[]{:S(2)}) %collective-permute-start) | collective-permute-done | bytes 245792 | tf_op jit(solution)/shard_map/ppermute | solution.py:107
  35.9 7.1 %all-to-all-start.1 = ((bf16[32,120,360]{2,1,0:T(8,128)(2,1)}), bf16[32,120,360]{2,1,0:T(8,128)(2,1)S(1)}, u32[]{:S(2)}, u32[]{:S(2)}) async-start(bf16[32,120,360]{2,1,0:T(8,128)(2,1)} %shard_map.82), calls=%async_computation.2 | async-start | bytes 5898240 | tf_op jit(solution)/shard_map/all_to_all | solution.py:115
  43.0 6.3 %shard_map.83 = bf16[32,120,600]{2,1,0:T(8,128)(2,1)} custom-call(bf16[120,30720]{1,0:T(8,128)(2,1)} %in_ref.3), custom_call_target="tpu_custom_call" | custom-call | tf_op jit(solution)/shard_map/pallas_call | solution.py:63
  49.3 45.1 %all-to-all-done.1 = bf16[32,120,360]{2,1,0:T(8,128)(2,1)S(1)} async-done(((bf16[32,120,360]{2,1,0:T(8,128)(2,1)}), bf16[32,120,360]{2,1,0:T(8,128)(2,1)S(1)}, u32[]{:S(2)}, u32[]{:S(2)}) %all-to-all-start.1) | async-done | bytes 2764832 | tf_op jit(solution)/shard_map/all_to_all | solution.py:115
  94.4 0.0 copy-start
  94.4 1.6 copy-done
  96.0 8.6 %all-to-all-start = ((bf16[32,120,600]{2,1,0:T(8,128)(2,1)}), bf16[32,120,600]{2,1,0:T(8,128)(2,1)}, u32[]{:S(2)}, u32[]{:S(2)}) async-start(bf16[32,120,600]{2,1,0:T(8,128)(2,1)} %shard_map.83), calls=%async_computation | async-start | bytes 9830400 | tf_op jit(solution)/shard_map/all_to_all | solution.py:115
  104.6 0.0 reduce-scatter.5.cloned.1.call-start
  104.7 0.0 all-gather.2.cloned.1.call-done.right_ref
  104.7 8.4 %shard_map.85 = f32[360,1024]{1,0:T(8,128)} custom-call(bf16[3840,360]{1,0:T(8,128)(2,1)} %bitcast.5, bf16[3840,1024]{1,0:T(8,128)(2,1)} %all-gather.2.cloned.1.call-done.right_ref), custom_call_target="tpu_custom_call" | custom-call | flops 2831155200 | bytes 12103680 | tf_op jit(solution)/shard_map/pallas_call | solution.py:37
  113.0 0.0 reduce-scatter.5.cloned.1.call-update
  113.1 0.0 reduce-scatter.3.cloned.1.call-start
  113.1 50.0 %all-to-all-done = bf16[32,120,600]{2,1,0:T(8,128)(2,1)} async-done(((bf16[32,120,600]{2,1,0:T(8,128)(2,1)}), bf16[32,120,600]{2,1,0:T(8,128)(2,1)}, u32[]{:S(2)}, u32[]{:S(2)}) %all-to-all-start) | async-done | bytes 4608032 | tf_op jit(solution)/shard_map/all_to_all | solution.py:115
  163.2 0.0 copy-start.1
  163.2 0.0 copy-start.2
  163.2 0.0 copy-start.3
  163.2 0.0 copy-start.4
  163.2 11.2 %shard_map.84 = f32[600,1024]{1,0:T(8,128)} custom-call(bf16[3840,600]{1,0:T(8,128)(2,1)} %bitcast.left_ref, bf16[3840,1024]{1,0:T(8,128)(2,1)} %all-gather.2.cloned.1.call-done.right_ref), custom_call_target="tpu_custom_call" | custom-call | flops 4718592000 | bytes 14929920 | tf_op jit(solution)/shard_map/pallas_call | solution.py:37
  174.4 0.0 reduce-scatter.3.cloned.1.call-update
  174.4 0.0 copy-done.1
  174.4 0.2 select_reduce_fusion.2
  174.6 0.0 copy-done.2
  174.6 0.4 select_reduce_fusion
  175.0 0.0 copy-done.3
  175.0 0.2 select_reduce_fusion.3
  175.2 0.0 copy-done.4
  175.2 0.4 select_reduce_fusion.1
  175.6 0.1 select_reduce_fusion.6
  175.7 0.1 select_reduce_fusion.4
  175.8 0.1 select_reduce_fusion.7
  175.9 0.1 select_reduce_fusion.5
  176.1 0.0 reduce-scatter.5.cloned.1.call-done
  176.1 41.6 %reduce-scatter.3.cloned.1.call-done = f32[600,128]{1,0:T(8,128)} async-done(((f32[600,1024]{1,0:T(8,128)}), f32[600,128]{1,0:T(8,128)}) %reduce-scatter.3.cloned.1.call-update) | async-done | bytes 307216 | tf_op jit(solution)/shard_map/reduce_scatter | solution.py:117
  217.6 1.4 fusion.2
  219.0 7.8 %collective-permute-start.1 = (bf16[960,128]{1,0:T(8,128)(2,1)S(1)}, bf16[960,128]{1,0:T(8,128)(2,1)S(1)}, u32[]{:S(2)}, u32[]{:S(2)}) collective-permute-start(bf16[960,128]{1,0:T(8,128)(2,1)S(1)} %fusion.2), channel_id=1, source_target_pairs={{0,0},{1,32},{2,64},{3,96},{4,128},{5,160},{6,192},{7,224},{32,1},... | collective-permute-start | bytes 737288 | tf_op jit(solution)/shard_map/ppermute | solution.py:135
  226.8 16.3 %collective-permute-done.1 = bf16[960,128]{1,0:T(8,128)(2,1)S(1)} collective-permute-done((bf16[960,128]{1,0:T(8,128)(2,1)S(1)}, bf16[960,128]{1,0:T(8,128)(2,1)S(1)}, u32[]{:S(2)}, u32[]{:S(2)}) %collective-permute-start.1) | collective-permute-done | bytes 245792 | tf_op jit(solution)/shard_map/ppermute | solution.py:135
  243.1 0.7 copy.14
  (6 shorter events, 0.1 us)
Async XLA Ops:
  6.5 98.1 %all-gather.2.cloned.1.call-start = ((), (), s32[]{:S(2)}) async-start(), calls=%async_computation.4 | async-start | bytes 8847360 | tf_op jit(solution)/shard_map/all_gather | solution.py:102
  7.9 3.1 %copy-start.5 = (bf16[960,128]{1,0:T(8,128)(2,1)S(1)}, bf16[960,128]{1,0:T(8,128)(2,1)}, u32[]{:S(2)}) copy-start(bf16[960,128]{1,0:T(8,128)(2,1)} %param.11) | copy-start | bytes 737284
  11.0 24.9 %collective-permute-start = (bf16[960,128]{1,0:T(8,128)(2,1)S(1)}, bf16[960,128]{1,0:T(8,128)(2,1)S(1)}, u32[]{:S(2)}, u32[]{:S(2)}) collective-permute-start(bf16[960,128]{1,0:T(8,128)(2,1)S(1)} %copy-done.5), channel_id=1, source_target_pairs={{0,0},{1,32},{2,64},{3,96},{4,128},{5,160},{6,192},{7,224},{32,1},... | collective-permute-start | bytes 737288 | tf_op jit(solution)/shard_map/ppermute | solution.py:107
  35.9 58.5 %all-to-all-start.1 = ((bf16[32,120,360]{2,1,0:T(8,128)(2,1)}), bf16[32,120,360]{2,1,0:T(8,128)(2,1)S(1)}, u32[]{:S(2)}, u32[]{:S(2)}) async-start(bf16[32,120,360]{2,1,0:T(8,128)(2,1)} %shard_map.82), calls=%async_computation.2 | async-start | bytes 5898240 | tf_op jit(solution)/shard_map/all_to_all | solution.py:115
  94.4 1.6 copy-start
  96.0 67.2 %all-to-all-start = ((bf16[32,120,600]{2,1,0:T(8,128)(2,1)}), bf16[32,120,600]{2,1,0:T(8,128)(2,1)}, u32[]{:S(2)}, u32[]{:S(2)}) async-start(bf16[32,120,600]{2,1,0:T(8,128)(2,1)} %shard_map.83), calls=%async_computation | async-start | bytes 9830400 | tf_op jit(solution)/shard_map/all_to_all | solution.py:115
  104.6 71.5 %reduce-scatter.5.cloned.1.call-start = ((), (), s32[]{:S(2)}) async-start(), calls=%async_computation.6 | async-start | bytes 1658880 | tf_op jit(solution)/shard_map/reduce_scatter | solution.py:117
  113.1 104.6 %reduce-scatter.3.cloned.1.call-start = ((), (), s32[]{:S(2)}) async-start(), calls=%async_computation.5 | async-start | bytes 2764800 | tf_op jit(solution)/shard_map/reduce_scatter | solution.py:117
  163.2 11.3 %copy-start.1 = (f32[192]{0:T(256)S(1)}, f32[192]{0:T(256)}, u32[]{:S(2)}) copy-start(f32[192]{0:T(256)} %param.15) | copy-start | bytes 2308
  163.2 11.4 %copy-start.2 = (f32[240]{0:T(256)S(1)}, f32[240]{0:T(256)}, u32[]{:S(2)}) copy-start(f32[240]{0:T(256)} %param.14) | copy-start | bytes 2884
  163.2 11.8 %copy-start.3 = (s32[192]{0:T(256)S(1)}, s32[192]{0:T(256)}, u32[]{:S(2)}) copy-start(s32[192]{0:T(256)} %param.13) | copy-start | bytes 2308
  163.2 12.0 %copy-start.4 = (s32[240]{0:T(256)S(1)}, s32[240]{0:T(256)}, u32[]{:S(2)}) copy-start(s32[240]{0:T(256)} %param.12) | copy-start | bytes 2884
  219.0 24.0 %collective-permute-start.1 = (bf16[960,128]{1,0:T(8,128)(2,1)S(1)}, bf16[960,128]{1,0:T(8,128)(2,1)S(1)}, u32[]{:S(2)}, u32[]{:S(2)}) collective-permute-start(bf16[960,128]{1,0:T(8,128)(2,1)S(1)} %fusion.2), channel_id=1, source_target_pairs={{0,0},{1,32},{2,64},{3,96},{4,128},{5,160},{6,192},{7,224},{32,1},... | collective-permute-start | bytes 737288 | tf_op jit(solution)/shard_map/ppermute | solution.py:135
Sparse Core Ops, SparseCore 0:
  11.1 86.2 all-gather.1
  113.2 38.8 reduce-scatter.4
  174.5 43.0 reduce-scatter.2

commit v16 on v14

--- a/solution.py
+++ b/solution.py
@@ -70,7 +70,7 @@
 
 
 def chunk_widths(total):
-    first = total * 5 // 8
+    first = total * 7 // 12
     return [first, total - first]
 
 

time: 250 us -> 255 us (1.020)
  local copies, waits for them, and re-layouts: 3.47 us -> 30.4 us
  waiting for transfers between devices: 165 us -> 146 us
  starting transfers between devices: 31.3 us -> 28.4 us
    all_to_all x2, waiting for transfers between devices: 96.2 us -> 78.1 us  [local(): lax.all_to_all(piece, (X, C, Y), split_axis=0, concat_axis=0, tiled=True)]
    all_to_all x0 -> x2, local copies, waits for them, and re-layouts: none -> 15 us  [local(): lax.all_to_all(piece, (X, C, Y), split_axis=0, concat_axis=0, tiled=True)]
    pallas_call x0 -> x1, local copies, waits for them, and re-layouts: none -> 7.39 us  [stack_chunk(): pl.pallas_call(functools.partial(stack_kernel, start, width, block), out_...]
    optimization_barrier x0 -> x1, local copies, waits for them, and re-layouts: none -> 6.09 us  [local(): coulomb_here, piece = lax.optimization_barrier((coulomb_here, piece))]
    all_to_all x2, starting transfers between devices: 15.7 us -> 12.6 us  [local(): lax.all_to_all(piece, (X, C, Y), split_axis=0, concat_axis=0, tiled=True)]
  transfers between devices with their start and end apart: 7 -> 7, of which waited for: 5 -> 5; matrix products, arithmetic and copies ran while one was open for 1% -> 12% of each run, Pallas kernels for 12% -> 12%
where the time goes in v16:
time: 255 us; the launch traced here: 254 us
  waiting for transfers between devices  146 us (57%)
  local copies, waits for them, and re-layouts  30.4 us (12%)
  Pallas kernels  29.4 us (12%)
  starting transfers between devices  28.4 us (11%)
  between operations  13.3 us (5%)
  other arithmetic  6.23 us (2%)
    all_to_all x2, waiting for transfers between devices, local(): lax.all_to_all(piece, (X, C, Y), split_axis=0, concat_axis=0, tiled=True)  78.1 us
    reduce_scatter x2, waiting for transfers between devices, local(): lax.psum_scatter(partial_value, Z, scatter_dimension=1, tiled=True)  41.1 us
    pallas_call x2, Pallas kernels, product(): pl.pallas_call(product_kernel, out_shape=jax.ShapeDtypeStruct((rows, widt...  17.4 us
    ppermute x1, waiting for transfers between devices, local(): return lax.ppermute(out, (Z, X, C), perm)  16.1 us
    all_to_all x2, local copies, waits for them, and re-layouts, local(): lax.all_to_all(piece, (X, C, Y), split_axis=0, concat_axis=0, tiled=True)  15 us
    all_to_all x2, starting transfers between devices, local(): lax.all_to_all(piece, (X, C, Y), split_axis=0, concat_axis=0, tiled=True)  12.6 us
    pallas_call x2, Pallas kernels, stack_chunk(): pl.pallas_call(functools.partial(stack_kernel, start, width, block), out_...  12.1 us
    ppermute x1, waiting for transfers between devices, local(): coulomb_here = lax.ppermute(coulomb, (Z, X, C), perm)  11 us
  transfers between devices with their start and end apart: 7, of which 5 were waited for; matrix products, arithmetic and copies ran while one was open for 12% of the time, Pallas kernels for 12%

profile of v16, /device:TPU:7, one launch (start us, length us, event | category | flops | bytes accessed | tf_op | source)
XLA Modules:
  0.0 254.0 jit_solution(12252066328922697365)
XLA Ops:
  6.5 0.0 copy-start.4
  6.5 0.0 all-gather.2.cloned.1.call-start
  6.5 0.7 convert_element_type.10
  7.3 0.2 broadcast_in_dim.140
  7.5 0.3 reshape.123
  7.8 0.1 constant_dynamic-slice_fusion
  7.8 0.1 mul.41
  7.9 0.5 copy.19
  8.5 2.5 dynamic-slice_multiply_fusion
  11.0 0.0 all-gather.2.cloned.1.call-update
  11.0 0.0 copy-done.4
  11.0 8.0 %collective-permute-start = (bf16[960,128]{1,0:T(8,128)(2,1)S(1)}, bf16[960,128]{1,0:T(8,128)(2,1)S(1)}, u32[]{:S(2)}, u32[]{:S(2)}) collective-permute-start(bf16[960,128]{1,0:T(8,128)(2,1)S(1)} %copy-done.4), channel_id=1, source_target_pairs={{0,0},{1,32},{2,64},{3,96},{4,128},{5,160},{6,192},{7,224},{32,1},... | collective-permute-start | bytes 737288 | tf_op jit(solution)/shard_map/ppermute | solution.py:107
  19.0 6.0 %shard_map.82 = bf16[32,120,400]{2,1,0:T(8,128)(2,1)} custom-call(bf16[120,30720]{1,0:T(8,128)(2,1)} %in_ref.3), custom_call_target="tpu_custom_call" | custom-call | tf_op jit(solution)/shard_map/pallas_call | solution.py:63
  25.0 11.0 %collective-permute-done = bf16[960,128]{1,0:T(8,128)(2,1)S(1)} collective-permute-done((bf16[960,128]{1,0:T(8,128)(2,1)S(1)}, bf16[960,128]{1,0:T(8,128)(2,1)S(1)}, u32[]{:S(2)}, u32[]{:S(2)}) %collective-permute-start) | collective-permute-done | bytes 245792 | tf_op jit(solution)/shard_map/ppermute | solution.py:107
  35.9 6.1 %copy.20 = bf16[32,120,400]{1,2,0:T(8,128)(2,1)} copy(bf16[32,120,400]{2,1,0:T(8,128)(2,1)} %shard_map.82) | data formatting | bytes 6144000 | tf_op jit(solution)/shard_map/optimization_barrier | solution.py:114
  42.0 7.1 %all-to-all-start.1 = ((bf16[32,120,400]{1,2,0:T(8,128)(2,1)}), bf16[32,120,400]{1,2,0:T(8,128)(2,1)S(1)}, u32[]{:S(2)}, u32[]{:S(2)}) async-start(bf16[32,120,400]{1,2,0:T(8,128)(2,1)} %copy.20), calls=%async_computation.2 | async-start | bytes 6553600 | tf_op jit(solution)/shard_map/all_to_all | solution.py:115
  49.1 6.1 %shard_map.83 = bf16[32,120,560]{2,1,0:T(8,128)(2,1)} custom-call(bf16[120,30720]{1,0:T(8,128)(2,1)} %in_ref.3), custom_call_target="tpu_custom_call" | custom-call | tf_op jit(solution)/shard_map/pallas_call | solution.py:63
  55.2 7.4 %copy.17 = bf16[32,120,560]{1,2,0:T(8,128)(2,1)} copy(bf16[32,120,560]{2,1,0:T(8,128)(2,1)} %shard_map.83) | data formatting | bytes 8601600 | tf_op jit(solution)/shard_map/pallas_call | solution.py:63
  62.6 39.0 %all-to-all-done.1 = bf16[32,120,400]{1,2,0:T(8,128)(2,1)S(1)} async-done(((bf16[32,120,400]{1,2,0:T(8,128)(2,1)}), bf16[32,120,400]{1,2,0:T(8,128)(2,1)S(1)}, u32[]{:S(2)}, u32[]{:S(2)}) %all-to-all-start.1) | async-done | bytes 3072032 | tf_op jit(solution)/shard_map/all_to_all | solution.py:115
  101.7 5.5 %all-to-all-start = ((bf16[32,120,560]{1,2,0:T(8,128)(2,1)}), bf16[32,120,560]{1,2,0:T(8,128)(2,1)}, u32[]{:S(2)}, u32[]{:S(2)}) async-start(bf16[32,120,560]{1,2,0:T(8,128)(2,1)} %copy.17), calls=%async_computation | async-start | bytes 9175040 | tf_op jit(solution)/shard_map/all_to_all | solution.py:115
  107.1 0.0 reduce-scatter.5.cloned.1.call-start
  107.2 7.6 %copy.21 = bf16[32,120,400]{2,1,0:T(8,128)(2,1)} copy(bf16[32,120,400]{1,2,0:T(8,128)(2,1)S(1)} %all-to-all-done.1) | data formatting | bytes 6144000 | tf_op jit(solution)/shard_map/all_to_all | solution.py:115
  114.8 0.0 all-gather.2.cloned.1.call-done.right_ref
  114.8 7.8 %shard_map.85 = f32[400,1024]{1,0:T(8,128)} custom-call(bf16[3840,400]{1,0:T(8,128)(2,1)} %bitcast.5, bf16[3840,1024]{1,0:T(8,128)(2,1)} %all-gather.2.cloned.1.call-done.right_ref), custom_call_target="tpu_custom_call" | custom-call | flops 3145728000 | bytes 12574720 | tf_op jit(solution)/shard_map/pallas_call | solution.py:37
  122.6 0.0 reduce-scatter.5.cloned.1.call-update
  122.6 0.0 reduce-scatter.3.cloned.1.call-start
  122.7 39.1 %all-to-all-done = bf16[32,120,560]{1,2,0:T(8,128)(2,1)} async-done(((bf16[32,120,560]{1,2,0:T(8,128)(2,1)}), bf16[32,120,560]{1,2,0:T(8,128)(2,1)}, u32[]{:S(2)}, u32[]{:S(2)}) %all-to-all-start) | async-done | bytes 4300832 | tf_op jit(solution)/shard_map/all_to_all | solution.py:115
  161.7 7.4 %copy.18 = bf16[32,120,560]{2,1,0:T(8,128)(2,1)} copy(bf16[32,120,560]{1,2,0:T(8,128)(2,1)} %all-to-all-done) | data formatting | bytes 8601600 | tf_op jit(solution)/shard_map/all_to_all | solution.py:115
  169.2 0.0 copy-start
  169.2 0.0 copy-start.1
  169.2 0.0 copy-start.2
  169.2 0.0 copy-start.3
  169.2 9.5 %shard_map.84 = f32[560,1024]{1,0:T(8,128)} custom-call(bf16[3840,560]{1,0:T(8,128)(2,1)} %bitcast.6, bf16[3840,1024]{1,0:T(8,128)(2,1)} %all-gather.2.cloned.1.call-done.right_ref), custom_call_target="tpu_custom_call" | custom-call | flops 4404019200 | bytes 14458880 | tf_op jit(solution)/shard_map/pallas_call | solution.py:37
  178.7 0.0 reduce-scatter.3.cloned.1.call-update
  178.8 0.0 copy-done
  178.8 0.2 select_reduce_fusion.2
  179.0 0.0 copy-done.1
  179.0 0.4 select_reduce_fusion
  179.4 0.0 copy-done.2
  179.4 0.2 select_reduce_fusion.3
  179.6 0.0 copy-done.3
  179.6 0.4 select_reduce_fusion.1
  180.0 0.1 select_reduce_fusion.6
  180.1 0.1 select_reduce_fusion.4
  180.2 0.1 select_reduce_fusion.7
  180.3 0.1 select_reduce_fusion.5
  180.4 0.0 reduce-scatter.5.cloned.1.call-done
  180.5 41.1 %reduce-scatter.3.cloned.1.call-done = f32[560,128]{1,0:T(8,128)} async-done(((f32[560,1024]{1,0:T(8,128)}), f32[560,128]{1,0:T(8,128)}) %reduce-scatter.3.cloned.1.call-update) | async-done | bytes 286736 | tf_op jit(solution)/shard_map/reduce_scatter | solution.py:117
  221.5 1.4 fusion.2
  222.9 7.7 %collective-permute-start.1 = (bf16[960,128]{1,0:T(8,128)(2,1)S(1)}, bf16[960,128]{1,0:T(8,128)(2,1)S(1)}, u32[]{:S(2)}, u32[]{:S(2)}) collective-permute-start(bf16[960,128]{1,0:T(8,128)(2,1)S(1)} %fusion.2), channel_id=1, source_target_pairs={{0,0},{1,32},{2,64},{3,96},{4,128},{5,160},{6,192},{7,224},{32,1},... | collective-permute-start | bytes 737288 | tf_op jit(solution)/shard_map/ppermute | solution.py:135
  230.7 16.1 %collective-permute-done.1 = bf16[960,128]{1,0:T(8,128)(2,1)S(1)} collective-permute-done((bf16[960,128]{1,0:T(8,128)(2,1)S(1)}, bf16[960,128]{1,0:T(8,128)(2,1)S(1)}, u32[]{:S(2)}, u32[]{:S(2)}) %collective-permute-start.1) | collective-permute-done | bytes 245792 | tf_op jit(solution)/shard_map/ppermute | solution.py:135
  246.8 0.7 copy.23
  (6 shorter events, 0.1 us)
Async XLA Ops:
  6.5 4.5 %copy-start.4 = (bf16[960,128]{1,0:T(8,128)(2,1)S(1)}, bf16[960,128]{1,0:T(8,128)(2,1)}, u32[]{:S(2)}) copy-start(bf16[960,128]{1,0:T(8,128)(2,1)} %param.11) | copy-start | bytes 737284
  6.5 108.2 %all-gather.2.cloned.1.call-start = ((), (), s32[]{:S(2)}) async-start(), calls=%async_computation.4 | async-start | bytes 8847360 | tf_op jit(solution)/shard_map/all_gather | solution.py:102
  11.0 24.9 %collective-permute-start = (bf16[960,128]{1,0:T(8,128)(2,1)S(1)}, bf16[960,128]{1,0:T(8,128)(2,1)S(1)}, u32[]{:S(2)}, u32[]{:S(2)}) collective-permute-start(bf16[960,128]{1,0:T(8,128)(2,1)S(1)} %copy-done.4), channel_id=1, source_target_pairs={{0,0},{1,32},{2,64},{3,96},{4,128},{5,160},{6,192},{7,224},{32,1},... | collective-permute-start | bytes 737288 | tf_op jit(solution)/shard_map/ppermute | solution.py:107
  42.0 59.6 %all-to-all-start.1 = ((bf16[32,120,400]{1,2,0:T(8,128)(2,1)}), bf16[32,120,400]{1,2,0:T(8,128)(2,1)S(1)}, u32[]{:S(2)}, u32[]{:S(2)}) async-start(bf16[32,120,400]{1,2,0:T(8,128)(2,1)} %copy.20), calls=%async_computation.2 | async-start | bytes 6553600 | tf_op jit(solution)/shard_map/all_to_all | solution.py:115
  101.7 60.1 %all-to-all-start = ((bf16[32,120,560]{1,2,0:T(8,128)(2,1)}), bf16[32,120,560]{1,2,0:T(8,128)(2,1)}, u32[]{:S(2)}, u32[]{:S(2)}) async-start(bf16[32,120,560]{1,2,0:T(8,128)(2,1)} %copy.17), calls=%async_computation | async-start | bytes 9175040 | tf_op jit(solution)/shard_map/all_to_all | solution.py:115
  107.1 73.3 %reduce-scatter.5.cloned.1.call-start = ((), (), s32[]{:S(2)}) async-start(), calls=%async_computation.6 | async-start | bytes 1843200 | tf_op jit(solution)/shard_map/reduce_scatter | solution.py:117
  122.6 98.9 %reduce-scatter.3.cloned.1.call-start = ((), (), s32[]{:S(2)}) async-start(), calls=%async_computation.5 | async-start | bytes 2580480 | tf_op jit(solution)/shard_map/reduce_scatter | solution.py:117
  169.2 9.6 %copy-start = (f32[192]{0:T(256)S(1)}, f32[192]{0:T(256)}, u32[]{:S(2)}) copy-start(f32[192]{0:T(256)} %param.15) | copy-start | bytes 2308
  169.2 9.8 %copy-start.1 = (f32[240]{0:T(256)S(1)}, f32[240]{0:T(256)}, u32[]{:S(2)}) copy-start(f32[240]{0:T(256)} %param.14) | copy-start | bytes 2884
  169.2 10.2 %copy-start.2 = (s32[192]{0:T(256)S(1)}, s32[192]{0:T(256)}, u32[]{:S(2)}) copy-start(s32[192]{0:T(256)} %param.13) | copy-start | bytes 2308
  169.2 10.4 %copy-start.3 = (s32[240]{0:T(256)S(1)}, s32[240]{0:T(256)}, u32[]{:S(2)}) copy-start(s32[240]{0:T(256)} %param.12) | copy-start | bytes 2884
  222.9 23.9 %collective-permute-start.1 = (bf16[960,128]{1,0:T(8,128)(2,1)S(1)}, bf16[960,128]{1,0:T(8,128)(2,1)S(1)}, u32[]{:S(2)}, u32[]{:S(2)}) collective-permute-start(bf16[960,128]{1,0:T(8,128)(2,1)S(1)} %fusion.2), channel_id=1, source_target_pairs={{0,0},{1,32},{2,64},{3,96},{4,128},{5,160},{6,192},{7,224},{32,1},... | collective-permute-start | bytes 737288 | tf_op jit(solution)/shard_map/ppermute | solution.py:135
Sparse Core Ops, SparseCore 0:
  11.2 82.6 all-gather.1
  122.7 39.6 reduce-scatter.4
  178.9 42.6 reduce-scatter.2
